TPU v7x, 32 devices: a whole 2x2x4 slice. The times are simulated.
32 devices in a mesh: ta: 8 (over z, y), col: 4 (over x, core).
Axes of the slice: x: 2, y: 2, z: 4, core: 2. Of those that a mesh axis runs over, the one named last changes fastest.
Arguments:
- strain: bfloat16 [2048, 512], P('col', 'ta'), may hold values from -6 to 6
- filter_taps: float32 [64], replicated, may hold values from -0.75 to 0.75
Outputs:
- cross_spectra: bfloat16 [4, 512, 128, 256], P('col', 'ta')
All inputs are finite; a program needn't handle non-finite values.
Results may differ from a plain program's by a relative error of at most 0.0066.
Values may be sent and summed in bfloat16 or wider, within the bound.
No kernel may reach another device: no remote copies, remote signals or barrier semaphores. Data moves between devices by JAX's collectives and lax.ppermute only.
A program may use at most 64 MiB of HBM per device.

v0:
```python
import functools

import jax
import jax.numpy as jnp
from jax import lax
from jax.experimental import pallas as pl
from jax.experimental.pallas import tpu as pltpu
from jax.sharding import PartitionSpec as P

NFFT = 256
NF = 128
LAGS = 128


def tap_rows(filter_taps, outputs):
    tap_count = filter_taps.shape[0]
    window = 2 * outputs + tap_count
    flipped = filter_taps[::-1]
    period = jnp.concatenate([flipped, jnp.zeros((window + 2 - tap_count,), jnp.float32)])
    repeated = jnp.tile(period, outputs)[: outputs * window]
    return repeated.reshape(outputs, window)


def decimate(history, samples, filter_taps):
    channels, length = samples.shape
    tap_count = filter_taps.shape[0]
    outputs = min(length, NFFT) // 2
    blocks = length // (2 * outputs)
    joined = jnp.concatenate(
        [history, samples, jnp.zeros((channels, 2 * outputs - tap_count), jnp.float32)], axis=1
    )
    joined = joined.reshape(channels, blocks + 1, 2 * outputs)
    windows = jnp.concatenate([joined[:, :-1], joined[:, 1:, :tap_count]], axis=2)
    matrix = tap_rows(filter_taps, outputs)
    result = jnp.einsum("cbw,tw->cbt", windows, matrix, precision=lax.Precision.HIGHEST)
    return result.reshape(channels, blocks * outputs).astype(jnp.bfloat16)


def fourier_table():
    moment = lax.broadcasted_iota(jnp.int32, (NFFT, NF), 0)
    frequency = lax.broadcasted_iota(jnp.int32, (NFFT, NF), 1) + 1
    phase_index = moment * frequency % NFFT
    angles = phase_index.astype(jnp.float32) * (2.0 * jnp.pi / NFFT)
    window_taper = 0.5 - 0.5 * jnp.cos(moment.astype(jnp.float32) * (2.0 * jnp.pi / NFFT))
    return jnp.concatenate(
        [window_taper * jnp.cos(angles), -window_taper * jnp.sin(angles)], axis=1
    )


def whiten(filtered):
    channels, length = filtered.shape
    pieces = filtered.reshape(channels, length // NF, NF)
    segment_rows = jnp.concatenate([pieces[:, :-1], pieces[:, 1:]], axis=2)
    spectrum = jnp.einsum(
        "csn,nf->csf",
        segment_rows.astype(jnp.float32),
        fourier_table(),
        precision=lax.Precision.HIGHEST,
    )
    real_part = spectrum[..., :NF]
    imag_part = spectrum[..., NF:]
    powers = real_part * real_part + imag_part * imag_part
    mean_power = jnp.mean(powers, axis=-1, keepdims=True)
    whitening = 1.0 / jnp.sqrt(powers + mean_power + 1e-06)
    return jnp.concatenate([real_part * whitening, imag_part * whitening], axis=-1).astype(
        jnp.bfloat16
    )


def cross_kernel(segments, rows_per_step, own_ref, ext_ref, out_ref):
    step = pl.program_id(0)
    base = pl.multiple_of(step * rows_per_step, rows_per_step)
    for i in range(rows_per_step):
        acc_re = None
        acc_im = None
        for s in range(segments):
            a = own_ref[pl.ds(base, rows_per_step), pl.ds(s * NFFT, NFFT)]
            a = a.astype(jnp.float32)[i : i + 1]
            window = ext_ref[pl.ds(base, LAGS + rows_per_step), pl.ds(s * NFFT, NFFT)]
            b = window.astype(jnp.float32)[i : i + LAGS]
            terms = product_terms(a, b)
            if acc_re is None:
                acc_re, acc_im = terms
            else:
                acc_re = [x + y for x, y in zip(acc_re, terms[0])]
                acc_im = [x + y for x, y in zip(acc_im, terms[1])]
        store_row(out_ref, i, acc_re, acc_im, segments)


def product_terms(a, b):
    ar = a[:, :NF]
    ai = a[:, NF:]
    br = b[:, :NF]
    bi = b[:, NF:]
    return [ar * br, ai * bi], [ai * br, ar * bi]


def store_row(out_ref, i, acc_re, acc_im, segments):
    re = (acc_re[0] + acc_re[1]) / segments
    im = (acc_im[0] - acc_im[1]) / segments
    out_ref[i, :, :NF] = re.astype(out_ref.dtype)
    out_ref[i, :, NF:] = im.astype(out_ref.dtype)


def cross_kernel_shifted(segments, rows_per_step, own_ref, ext_ref, out_ref, own_f32, shifted):
    step = pl.program_id(0)
    span = shifted.shape[1]

    @pl.when(step == 0)
    def _():
        own_f32[...] = own_ref[...].astype(jnp.float32)
        whole = ext_ref[...].astype(jnp.float32)
        for i in range(rows_per_step):
            shifted[i] = whole[i : i + span]

    base = pl.multiple_of(step * rows_per_step, rows_per_step)
    for i in range(rows_per_step):
        acc_re = None
        acc_im = None
        for s in range(segments):
            a = own_f32[pl.ds(base + i, 1), pl.ds(s * NFFT, NFFT)]
            b = shifted[i, pl.ds(base, LAGS), pl.ds(s * NFFT, NFFT)]
            terms = product_terms(a, b)
            if acc_re is None:
                acc_re, acc_im = terms
            else:
                acc_re = [x + y for x, y in zip(acc_re, terms[0])]
                acc_im = [x + y for x, y in zip(acc_im, terms[1])]
        store_row(out_ref, i, acc_re, acc_im, segments)


def cross_spectra(own, extended):
    rows, segments, columns = own.shape
    reach_rows = extended.shape[0]
    own_flat = own.reshape(rows, segments * columns)
    ext_flat = extended.reshape(reach_rows, segments * columns)
    rows_per_step = 8
    span = reach_rows - rows_per_step
    scratch_bytes = rows_per_step * span * segments * columns * 4
    cost = pl.CostEstimate(
        flops=6 * rows * LAGS * NF * segments,
        transcendentals=0,
        bytes_accessed=rows * LAGS * columns * 2 + 2 * segments * (rows + reach_rows) * columns,
    )
    common = dict(
        out_shape=jax.ShapeDtypeStruct((rows, LAGS, columns), jnp.bfloat16),
        grid=(rows // rows_per_step,),
        in_specs=[
            pl.BlockSpec((rows, segments * columns), lambda i: (0, 0)),
            pl.BlockSpec((reach_rows, segments * columns), lambda i: (0, 0)),
        ],
        out_specs=pl.BlockSpec((rows_per_step, LAGS, columns), lambda i: (i, 0, 0)),
        cost_estimate=cost,
    )
    if scratch_bytes <= 8 * 1024 * 1024:
        return pl.pallas_call(
            functools.partial(cross_kernel_shifted, segments, rows_per_step),
            scratch_shapes=[
                pltpu.VMEM((rows, segments * columns), jnp.float32),
                pltpu.VMEM((rows_per_step, span, segments * columns), jnp.float32),
            ],
            compiler_params=pltpu.CompilerParams(dimension_semantics=("arbitrary",)),
            **common,
        )(own_flat, ext_flat)
    return pl.pallas_call(
        functools.partial(cross_kernel, segments, rows_per_step), **common
    )(own_flat, ext_flat)


def body(strain, filter_taps):
    tap_count = filter_taps.shape[0]
    extent = lax.axis_size("ta")
    columns_n = lax.axis_size("col")
    position = lax.axis_index("ta")
    section_rows, slab = strain.shape
    block_rows = section_rows // extent
    reach = LAGS // block_rows
    window = 2 * reach
    before = (reach - 1) * block_rows
    padded = jnp.concatenate(
        [
            jnp.zeros((before, slab), strain.dtype),
            strain,
            jnp.zeros((reach * block_rows, slab), strain.dtype),
        ],
        axis=0,
    )
    blocks = padded.reshape(extent + window - 1, block_rows, slab)
    outgoing = jnp.stack([blocks[w : w + extent] for w in range(window)], axis=1)
    outgoing = outgoing.reshape(extent * window * block_rows, slab)
    regrouped = lax.all_to_all(outgoing, "ta", split_axis=0, concat_axis=1, tiled=True)
    filtered = decimate(
        jnp.zeros((regrouped.shape[0], tap_count), jnp.float32),
        regrouped.astype(jnp.float32),
        filter_taps,
    )
    whitened = whiten(filtered)
    segments, columns = whitened.shape[1:]
    first_of_section = reach - 1 - jnp.minimum(position, reach - 1)
    payload = lax.dynamic_slice_in_dim(whitened, first_of_section * block_rows, reach * block_rows, 0)

    def linear(ta_index, col_index):
        return ta_index * columns_n + col_index

    route = [
        (linear(m, c + 1), linear(extent - reach + m, c))
        for c in range(columns_n - 1)
        for m in range(reach)
    ]
    next_section = lax.ppermute(payload, ("ta", "col"), route)
    local = whitened[before : before + (reach + 1) * block_rows]
    extended = local
    for j in range(extent - reach, extent):
        kept = (extent - j) * block_rows
        candidate = jnp.concatenate(
            [local[:kept], next_section[: (reach + 1) * block_rows - kept]], axis=0
        )
        extended = jnp.where(position == j, candidate, extended)
    own = local[:block_rows]
    return cross_spectra(own, extended)[None]


def solution(mesh):
    return jax.shard_map(
        body,
        mesh=mesh,
        in_specs=(P("col", "ta"), P()),
        out_specs=P("col", "ta", None, None),
        check_vma=False,
    )
```

profile of v0, /device:TPU:29, one launch (start us, length us, event | category | flops | bytes accessed | tf_op | source)
XLA Modules:
  0.0 34.0 jit_solution(1920885265314045113)
XLA Ops:
  0.0 0.0 copy-start.1
  0.0 1.0 %stack.16 = bf16[8,1,64,64]{2,0,3,1:T(8,128)(2,1)S(1)} reshape(bf16[512,64]{0,1:T(8,128)(2,1)} %param.2) | data formatting | bytes 131072 | tf_op jit(solution)/shard_map/stack | solution.py:189
  1.0 1.1 %pad_slice_fusion.4 = (bf16[512,64]{0,1:T(8,128)(2,1)S(1)}, bf16[512,64]{0,1:T(8,128)(2,1)S(1)}, bf16[512,64]{0,1:T(8,128)(2,1)S(1)}) fusion(bf16[512,64]{0,1:T(8,128)(2,1)} %param.2), kind=kLoop, calls=%fused_computation.39 | loop fusion | bytes 262144 | tf_op jit(solution)/shard_map/slice | solution.py:189
  2.1 0.2 copy.5
  2.3 0.1 stack.15
  2.4 0.2 copy.4
  2.6 0.1 stack.18
  2.8 0.2 copy.7
  3.0 0.1 stack.17
  3.1 0.2 copy.6
  3.3 1.5 %pad_maximum_fusion = bf16[8,4,64,64]{2,1,3,0:T(4,128)(2,1)S(1)} fusion(bf16[8,1,64,64]{2,1,3,0:T(2,128)(2,1)S(1)} %copy.7, bf16[8,1,64,64]{2,1,3,0:T(2,128)(2,1)S(1)} %copy.6, bf16[8,1,64,64]{2,1,3,0:T(2,128)(2,1)S(1)} %copy.5, bf16[8,1,64,64]{2,1,3,0:T(2,128)(2,1)S(1)} %copy.4), kind=kLoop, calls=%fused_computation.6 | loop fusion | flops 1048576 | bytes 524288 | tf_op jit(solution)/shard_map/stack | solution.py:189
  4.8 1.0 %all_to_all.10 = bf16[8,256,64]{1,2,0:T(8,128)(2,1)} reshape(bf16[8,4,64,64]{2,1,3,0:T(4,128)(2,1)S(1)} %pad_maximum_fusion) | data formatting | bytes 524288 | tf_op jit(solution)/shard_map/all_to_all | solution.py:191
  5.9 5.4 %all-to-all-start = ((bf16[8,256,64]{1,2,0:T(8,128)(2,1)}), bf16[8,256,64]{1,2,0:T(8,128)(2,1)S(1)}, u32[]{:S(2)}, u32[]{:S(2)}) async-start(bf16[8,256,64]{1,2,0:T(8,128)(2,1)} %all_to_all.10), calls=%async_computation | async-start | bytes 524288 | tf_op jit(solution)/shard_map/all_to_all | solution.py:191
  11.3 0.0 copy-done.1
  11.3 0.1 rev.3
  11.4 0.1 pad.18.clone
  11.5 0.2 tile.10
  11.8 0.1 reshape.73
  11.9 0.5 %cosine_multiply_fusion = (f32[256,128]{1,0:T(8,128)S(1)}, f32[256,128]{1,0:T(8,128)S(1)}) fusion(s32[128]{0:T(128)S(1)} %iota_add_fusion, f32[256]{0:T(256)S(1)} %get-tuple-element.16, f32[256]{0:T(256)S(1)} %get-tuple-element.17), kind=kLoop, calls=%fused_computation.31 | loop fusion | flops 524288 | bytes 264704 | tf_op jit(solution)/shard_map/mul | solution.py:46
  12.5 5.6 %all-to-all-done = bf16[8,256,64]{1,2,0:T(8,128)(2,1)S(1)} async-done(((bf16[8,256,64]{1,2,0:T(8,128)(2,1)}), bf16[8,256,64]{1,2,0:T(8,128)(2,1)S(1)}, u32[]{:S(2)}, u32[]{:S(2)}) %all-to-all-start) | async-done | bytes 262176 | tf_op jit(solution)/shard_map/all_to_all | solution.py:191
  18.1 0.3 maximum_maximum_fusion
  18.4 0.7 %convolution_convert_fusion = bf16[256,2,128]{0,2,1:T(8,128)(2,1)S(1)} fusion(f32[256,2,64]{0,2,1:T(8,128)S(1)} %slice.68, f32[256,2,256]{0,2,1:T(8,128)S(1)} %slice.67, f32[128,320]{1,0:T(8,128)S(1)} %reshape.73), kind=kOutput, calls=%fused_computation.1 | convolution fusion | flops 251887616 | bytes 950272 | tf_op jit(solution)/shard_map/cbw,tw->cbt/dot_general | solution.py:35
  19.1 0.3 convolution_bitcast_fusion
  19.4 0.1 fusion.25
  19.5 0.1 multiply_convert_fusion
  19.7 1.3 %collective-permute-start = (bf16[128,1,256]{2,0,1:T(8,128)(2,1)S(1)}, bf16[128,1,256]{2,0,1:T(8,128)(2,1)S(1)}, u32[]{:S(2)}, u32[]{:S(2)}) collective-permute-start(bf16[128,1,256]{2,0,1:T(8,128)(2,1)S(1)} %get-tuple-element.8), channel_id=1, source_target_pairs={{1,24},{5,28},{2,25},{6,29},{3,26},{7,30}} | collective-permute-start | bytes 196616 | tf_op jit(solution)/shard_map/ppermute | solution.py:210
  21.0 0.0 copy-start
  21.0 7.4 %collective-permute-done = bf16[128,1,256]{2,0,1:T(8,128)(2,1)S(1)} collective-permute-done((bf16[128,1,256]{2,0,1:T(8,128)(2,1)S(1)}, bf16[128,1,256]{2,0,1:T(8,128)(2,1)S(1)}, u32[]{:S(2)}, u32[]{:S(2)}) %collective-permute-start) | collective-permute-done | bytes 65568 | tf_op jit(solution)/shard_map/ppermute | solution.py:210
  28.4 0.7 %fusion.17.ext_ref = bf16[192,256]{1,0:T(8,128)(2,1)} fusion(bf16[256,1,128]{2,0,1:T(8,128)(2,1)S(1)} %get-tuple-element.5, bf16[256,1,128]{2,0,1:T(8,128)(2,1)S(1)} %get-tuple-element.6, bf16[128,1,256]{2,0,1:T(8,128)(2,1)S(1)} %collective-permute-done, bf16[64,1,256]{2,0,1:T(8,128)(2,1)S(1)} %fusion.20, bf16[64,1,256]{2,0,1:T(8,128)(2,1)S(1)} %slice.78, ...), kind=kLoop, calls=%fused_computation.38 | loop fusion | flops 688128 | bytes 425986 | tf_op jit(solution)/shard_map/reshape | solution.py:136
  29.1 0.0 copy-done
  29.1 4.9 %shard_map.28 = bf16[64,128,256]{2,1,0:T(8,128)(2,1)} custom-call(bf16[64,256]{1,0:T(8,128)(2,1)} %bitcast.29, bf16[192,256]{1,0:T(8,128)(2,1)} %fusion.17.ext_ref), custom_call_target="tpu_custom_call" | custom-call | flops 6291456 | bytes 4325376 | tf_op jit(solution)/shard_map/pallas_call | solution.py:156
  (16 shorter events, 0.2 us)
Async XLA Ops:
  0.0 11.3 %copy-start.1 = (f32[64]{0:T(128)S(1)}, f32[64]{0:T(128)}, u32[]{:S(2)}) copy-start(f32[64]{0:T(128)} %param.3) | copy-start | bytes 772
  5.9 12.2 %all-to-all-start = ((bf16[8,256,64]{1,2,0:T(8,128)(2,1)}), bf16[8,256,64]{1,2,0:T(8,128)(2,1)S(1)}, u32[]{:S(2)}, u32[]{:S(2)}) async-start(bf16[8,256,64]{1,2,0:T(8,128)(2,1)} %all_to_all.10), calls=%async_computation | async-start | bytes 524288 | tf_op jit(solution)/shard_map/all_to_all | solution.py:191
  19.7 8.7 %collective-permute-start = (bf16[128,1,256]{2,0,1:T(8,128)(2,1)S(1)}, bf16[128,1,256]{2,0,1:T(8,128)(2,1)S(1)}, u32[]{:S(2)}, u32[]{:S(2)}) collective-permute-start(bf16[128,1,256]{2,0,1:T(8,128)(2,1)S(1)} %get-tuple-element.8), channel_id=1, source_target_pairs={{1,24},{5,28},{2,25},{6,29},{3,26},{7,30}} | collective-permute-start | bytes 196616 | tf_op jit(solution)/shard_map/ppermute | solution.py:210
  21.0 8.1 %copy-start = (bf16[64,1,256]{2,0,1:T(8,128)(2,1)}, bf16[64,1,256]{2,0,1:T(8,128)(2,1)S(1)}, u32[]{:S(2)}) copy-start(bf16[64,1,256]{2,0,1:T(8,128)(2,1)S(1)} %fusion.20) | copy-start | bytes 98308
where the time goes:
time: 34.3 us; the launch traced here: 34 us
  waiting for transfers between devices  12.9 us (38%)
  starting transfers between devices  6.73 us (20%)
  Pallas kernels  4.91 us (14%)
  local copies, waits for them, and re-layouts  4.9 us (14%)
  other arithmetic  3.3 us (10%)
  matrix products  0.97 us (3%)
    ppermute x1, waiting for transfers between devices, body(): next_section = lax.ppermute(payload, ('ta', 'col'), route)  7.38 us
    all_to_all x1, waiting for transfers between devices, body(): lax.all_to_all(outgoing, 'ta', split_axis=0, concat_axis=1, tiled=True)  5.55 us
    all_to_all x1, starting transfers between devices, body(): lax.all_to_all(outgoing, 'ta', split_axis=0, concat_axis=1, tiled=True)  5.44 us
    pallas_call x1, Pallas kernels, cross_spectra(): pl.pallas_call(functools.partial(cross_kernel_shifted, segments, rows_per...  4.91 us
    another operation x8, local copies, waits for them, and re-layouts, body(): outgoing = jnp.stack([blocks[w:w + extent] for w in range(window)], axis=1)  2.19 us
    another operation x1, other arithmetic, body(): outgoing = jnp.stack([blocks[w:w + extent] for w in range(window)], axis=1)  1.49 us
    ppermute x1, starting transfers between devices, body(): next_section = lax.ppermute(payload, ('ta', 'col'), route)  1.29 us
    slice x1, local copies, waits for them, and re-layouts, body(): outgoing = jnp.stack([blocks[w:w + extent] for w in range(window)], axis=1)  1.06 us
  transfers between devices with their start and end apart: 2, of which 2 were waited for; matrix products, arithmetic and copies ran while one was open for 3% of the time, Pallas kernels for 0%

commit v1 on v0

--- a/solution.py
+++ b/solution.py
@@ -21,19 +21,24 @@
     return repeated.reshape(outputs, window)
 
 
-def decimate(history, samples, filter_taps):
-    channels, length = samples.shape
+def decimate_t(samples, filter_taps):
+    length, channels = samples.shape
     tap_count = filter_taps.shape[0]
     outputs = min(length, NFFT) // 2
     blocks = length // (2 * outputs)
     joined = jnp.concatenate(
-        [history, samples, jnp.zeros((channels, 2 * outputs - tap_count), jnp.float32)], axis=1
-    )
-    joined = joined.reshape(channels, blocks + 1, 2 * outputs)
-    windows = jnp.concatenate([joined[:, :-1], joined[:, 1:, :tap_count]], axis=2)
+        [
+            jnp.zeros((tap_count, channels), jnp.float32),
+            samples,
+            jnp.zeros((2 * outputs - tap_count, channels), jnp.float32),
+        ],
+        axis=0,
+    )
+    joined = joined.reshape(blocks + 1, 2 * outputs, channels)
+    windows = jnp.concatenate([joined[:-1], joined[1:, :tap_count]], axis=1)
     matrix = tap_rows(filter_taps, outputs)
-    result = jnp.einsum("cbw,tw->cbt", windows, matrix, precision=lax.Precision.HIGHEST)
-    return result.reshape(channels, blocks * outputs).astype(jnp.bfloat16)
+    result = jnp.einsum("tw,bwc->btc", matrix, windows, precision=lax.Precision.HIGHEST)
+    return result.reshape(blocks * outputs, channels).astype(jnp.bfloat16)
 
 
 def fourier_table():
@@ -47,24 +52,49 @@
     )
 
 
-def whiten(filtered):
-    channels, length = filtered.shape
-    pieces = filtered.reshape(channels, length // NF, NF)
-    segment_rows = jnp.concatenate([pieces[:, :-1], pieces[:, 1:]], axis=2)
+def whiten_t(filtered):
+    length, channels = filtered.shape
+    pieces = filtered.reshape(length // NF, NF, channels)
+    segment_rows = jnp.concatenate([pieces[:-1], pieces[1:]], axis=1)
     spectrum = jnp.einsum(
-        "csn,nf->csf",
+        "nf,snc->sfc",
+        fourier_table(),
         segment_rows.astype(jnp.float32),
-        fourier_table(),
         precision=lax.Precision.HIGHEST,
     )
-    real_part = spectrum[..., :NF]
-    imag_part = spectrum[..., NF:]
+    real_part = spectrum[:, :NF]
+    imag_part = spectrum[:, NF:]
     powers = real_part * real_part + imag_part * imag_part
-    mean_power = jnp.mean(powers, axis=-1, keepdims=True)
+    mean_power = jnp.mean(powers, axis=1, keepdims=True)
     whitening = 1.0 / jnp.sqrt(powers + mean_power + 1e-06)
-    return jnp.concatenate([real_part * whitening, imag_part * whitening], axis=-1).astype(
+    return jnp.concatenate([real_part * whitening, imag_part * whitening], axis=1).astype(
         jnp.bfloat16
     )
+
+
+def xor_order(chunks, position, extent):
+    bit = 1
+    while bit < extent:
+        shape = chunks.shape
+        swapped = chunks.reshape((extent // (2 * bit), 2, bit) + shape[1:])[:, ::-1].reshape(shape)
+        chunks = jnp.where((position & bit) != 0, swapped, chunks)
+        bit *= 2
+    return chunks
+
+
+def exchange_time(windows, position, extent):
+    if extent & (extent - 1) or extent > 16:
+        return lax.all_to_all(windows, "ta", split_axis=0, concat_axis=0, tiled=True)
+    chunks = xor_order(windows, position, extent)
+    bit = 1
+    while bit < extent:
+        shape = chunks.shape
+        view = chunks.reshape((extent // (2 * bit), 2, bit) + shape[1:])
+        route = [(i, i ^ bit) for i in range(extent)]
+        arrived = lax.ppermute(view[:, 1], "ta", route)
+        chunks = jnp.stack([view[:, 0], arrived], axis=1).reshape(shape)
+        bit *= 2
+    return xor_order(chunks, position, extent)
 
 
 def cross_kernel(segments, rows_per_step, own_ref, ext_ref, out_ref):
@@ -168,7 +198,6 @@
 
 
 def body(strain, filter_taps):
-    tap_count = filter_taps.shape[0]
     extent = lax.axis_size("ta")
     columns_n = lax.axis_size("col")
     position = lax.axis_index("ta")
@@ -177,24 +206,22 @@
     reach = LAGS // block_rows
     window = 2 * reach
     before = (reach - 1) * block_rows
+    turned = strain.T
     padded = jnp.concatenate(
         [
-            jnp.zeros((before, slab), strain.dtype),
-            strain,
-            jnp.zeros((reach * block_rows, slab), strain.dtype),
+            jnp.zeros((slab, before), strain.dtype),
+            turned,
+            jnp.zeros((slab, reach * block_rows), strain.dtype),
         ],
-        axis=0,
-    )
-    blocks = padded.reshape(extent + window - 1, block_rows, slab)
-    outgoing = jnp.stack([blocks[w : w + extent] for w in range(window)], axis=1)
-    outgoing = outgoing.reshape(extent * window * block_rows, slab)
-    regrouped = lax.all_to_all(outgoing, "ta", split_axis=0, concat_axis=1, tiled=True)
-    filtered = decimate(
-        jnp.zeros((regrouped.shape[0], tap_count), jnp.float32),
-        regrouped.astype(jnp.float32),
-        filter_taps,
-    )
-    whitened = whiten(filtered)
+        axis=1,
+    )
+    windows = jnp.stack(
+        [padded[:, j * block_rows : (j + window) * block_rows] for j in range(extent)]
+    )
+    gathered = exchange_time(windows, position, extent)
+    samples = gathered.reshape(extent * slab, window * block_rows)
+    filtered = decimate_t(samples.astype(jnp.float32), filter_taps)
+    whitened = whiten_t(filtered).transpose(2, 0, 1)
     segments, columns = whitened.shape[1:]
     first_of_section = reach - 1 - jnp.minimum(position, reach - 1)
     payload = lax.dynamic_slice_in_dim(whitened, first_of_section * block_rows, reach * block_rows, 0)

time: 34.3 us -> 40.6 us (1.18)
  the two profiles are of different devices: /device:TPU:29 before, /device:TPU:1 now
where the time goes in v1:
time: 40.6 us; the launch traced here: 40 us
  starting transfers between devices  14.4 us (35%)
  waiting for transfers between devices  9.28 us (23%)
  local copies, waits for them, and re-layouts  7.84 us (19%)
  Pallas kernels  4.91 us (12%)
  other arithmetic  2.27 us (6%)
  matrix products  0.97 us (2%)
    ppermute x1, starting transfers between devices, body(): next_section = lax.ppermute(payload, ('ta', 'col'), route)  8.75 us
    ppermute x3, waiting for transfers between devices, exchange_time(): arrived = lax.ppermute(view[:, 1], 'ta', route)  8.58 us
    unnamed x11, local copies, waits for them, and re-layouts  5.75 us
    ppermute x3, starting transfers between devices, exchange_time(): arrived = lax.ppermute(view[:, 1], 'ta', route)  5.67 us
    pallas_call x1, Pallas kernels, cross_spectra(): pl.pallas_call(functools.partial(cross_kernel_shifted, segments, rows_per...  4.91 us
  transfers between devices with their start and end apart: 4, of which 4 were waited for; matrix products, arithmetic and copies ran while one was open for 4% of the time, Pallas kernels for 0%

profile of v1, /device:TPU:1, one launch (start us, length us, event | category | flops | bytes accessed | tf_op | source)
XLA Modules:
  0.0 40.0 jit_solution(4848603105823852143)
XLA Ops:
  0.0 0.0 copy-start
  0.0 0.8 %fusion.31 = bf16[8,64,256]{2,1,0:T(8,128)(2,1)S(1)} fusion(bf16[64,512]{1,0:T(8,128)(2,1)} %bitcast.115), kind=kLoop, calls=%fused_computation.67 | loop fusion | bytes 98304
  0.9 0.8 %fusion.36 = bf16[8,64,256]{2,1,0:T(8,128)(2,1)S(1)} fusion(bf16[8,64,256]{2,1,0:T(8,128)(2,1)S(1)} %fusion.31, bf16[64,512]{1,0:T(8,128)(2,1)} %bitcast.116), kind=kLoop, calls=%fused_computation.77 | loop fusion | bytes 65536
  1.6 0.9 %fusion.35 = bf16[8,64,256]{2,1,0:T(8,128)(2,1)S(1)} fusion(bf16[8,64,256]{2,1,0:T(8,128)(2,1)S(1)} %fusion.36, bf16[64,512]{1,0:T(8,128)(2,1)} %bitcast.117), kind=kLoop, calls=%fused_computation.75 | loop fusion | bytes 65536
  2.5 0.8 %fusion.34 = bf16[8,64,256]{2,1,0:T(8,128)(2,1)S(1)} fusion(bf16[8,64,256]{2,1,0:T(8,128)(2,1)S(1)} %fusion.35, bf16[64,512]{1,0:T(8,128)(2,1)} %bitcast.118), kind=kLoop, calls=%fused_computation.73 | loop fusion | bytes 65536
  3.3 0.9 %fusion.33 = bf16[8,64,256]{2,1,0:T(8,128)(2,1)S(1)} fusion(bf16[8,64,256]{2,1,0:T(8,128)(2,1)S(1)} %fusion.34, bf16[64,512]{1,0:T(8,128)(2,1)} %bitcast.119), kind=kLoop, calls=%fused_computation.71 | loop fusion | bytes 65536
  4.1 0.8 %fusion.32 = bf16[8,64,256]{2,1,0:T(8,128)(2,1)S(1)} fusion(bf16[8,64,256]{2,1,0:T(8,128)(2,1)S(1)} %fusion.33, bf16[64,512]{1,0:T(8,128)(2,1)} %bitcast.120), kind=kLoop, calls=%fused_computation.69 | loop fusion | bytes 65536
  4.9 0.8 %fusion.27 = bf16[8,64,256]{2,1,0:T(8,128)(2,1)S(1)} fusion(bf16[8,64,256]{2,1,0:T(8,128)(2,1)S(1)} %fusion.32, bf16[64,512]{1,0:T(8,128)(2,1)} %bitcast.121), kind=kLoop, calls=%fused_computation.63 | loop fusion | bytes 98304
  5.7 0.7 %fusion.29 = bf16[8,64,256]{2,1,0:T(8,128)(2,1)S(1)} fusion(bf16[8,64,256]{2,1,0:T(8,128)(2,1)S(1)} %fusion.27, bf16[64,512]{1,0:T(8,128)(2,1)} %bitcast.122), kind=kLoop, calls=%fused_computation.65 | loop fusion | bytes 98304 | tf_op jit(solution)/shard_map/stack | solution.py:218
  6.6 0.1 fusion.10
  6.8 2.1 %collective-permute-start = (bf16[4,1,64,256]{3,2,0,1:T(8,128)(2,1)S(1)}, bf16[4,1,64,256]{3,2,0,1:T(8,128)(2,1)S(1)}, u32[]{:S(2)}, u32[]{:S(2)}) collective-permute-start(bf16[4,1,64,256]{3,2,0,1:T(8,128)(2,1)S(1)} %get-tuple-element.12), channel_id=1, source_target_pairs={{0,4},{4,0},{8,12},{12,8},{16,20},{20,16},{24,28},{28,24},{1,5},{5... | collective-permute-start | bytes 393224 | tf_op jit(solution)/shard_map/ppermute | solution.py:94
  8.9 3.2 %collective-permute-done = bf16[4,1,64,256]{3,2,0,1:T(8,128)(2,1)S(1)} collective-permute-done((bf16[4,1,64,256]{3,2,0,1:T(8,128)(2,1)S(1)}, bf16[4,1,64,256]{3,2,0,1:T(8,128)(2,1)S(1)}, u32[]{:S(2)}, u32[]{:S(2)}) %collective-permute-start) | collective-permute-done | bytes 131104 | tf_op jit(solution)/shard_map/ppermute | solution.py:94
  12.2 1.3 %collective-permute-start.1 = (bf16[2,2,64,256]{3,2,1,0:T(8,128)(2,1)S(1)}, bf16[2,2,64,256]{3,2,1,0:T(8,128)(2,1)S(1)}, u32[]{:S(2)}, u32[]{:S(2)}) collective-permute-start(bf16[2,2,64,256]{3,2,1,0:T(8,128)(2,1)S(1)} %bitcast.131), channel_id=1, source_target_pairs={{0,8},{4,12},{8,0},{12,4},{16,24},{20,28},{24,16},{28,20},{1,9},{5... | collective-permute-start | bytes 393224 | tf_op jit(solution)/shard_map/ppermute | solution.py:94
  13.5 0.0 copy-done
  13.5 0.1 rev.27
  13.6 0.1 pad.19.clone
  13.7 0.2 tile.10
  13.9 0.1 reshape.203
  14.1 2.0 %collective-permute-done.1 = bf16[2,2,64,256]{3,2,1,0:T(8,128)(2,1)S(1)} collective-permute-done((bf16[2,2,64,256]{3,2,1,0:T(8,128)(2,1)S(1)}, bf16[2,2,64,256]{3,2,1,0:T(8,128)(2,1)S(1)}, u32[]{:S(2)}, u32[]{:S(2)}) %collective-permute-start.1) | collective-permute-done | bytes 131104 | tf_op jit(solution)/shard_map/ppermute | solution.py:94
  16.1 2.3 %collective-permute-start.2 = (bf16[1,4,64,256]{3,2,1,0:T(8,128)(2,1)S(1)}, bf16[1,4,64,256]{3,2,1,0:T(8,128)(2,1)S(1)}, u32[]{:S(2)}, u32[]{:S(2)}) collective-permute-start(bf16[1,4,64,256]{3,2,1,0:T(8,128)(2,1)S(1)} %get-tuple-element.8), channel_id=1, source_target_pairs={{0,16},{4,20},{8,24},{12,28},{16,0},{20,4},{24,8},{28,12},{1,17},{... | collective-permute-start | bytes 393224 | tf_op jit(solution)/shard_map/ppermute | solution.py:94
  18.4 0.5 %cosine_multiply_fusion = (f32[256,128]{1,0:T(8,128)S(1)}, f32[256,128]{1,0:T(8,128)S(1)}) fusion(s32[128]{0:T(128)S(1)} %iota_add_fusion, f32[256]{0:T(256)S(1)} %get-tuple-element.19, f32[256]{0:T(256)S(1)} %get-tuple-element.20), kind=kLoop, calls=%fused_computation.50 | loop fusion | flops 524288 | bytes 264704 | tf_op jit(solution)/shard_map/mul | solution.py:51
  19.0 3.4 %collective-permute-done.2 = bf16[1,4,64,256]{3,2,1,0:T(8,128)(2,1)S(1)} collective-permute-done((bf16[1,4,64,256]{3,2,1,0:T(8,128)(2,1)S(1)}, bf16[1,4,64,256]{3,2,1,0:T(8,128)(2,1)S(1)}, u32[]{:S(2)}, u32[]{:S(2)}) %collective-permute-start.2) | collective-permute-done | bytes 131104 | tf_op jit(solution)/shard_map/ppermute | solution.py:94
  22.5 0.1 fusion.9
  22.7 0.3 maximum_maximum_fusion
  23.0 0.7 %fusion = bf16[2,128,256]{2,1,0:T(8,128)(2,1)S(1)} fusion(f32[2,64,256]{2,1,0:T(8,128)S(1)} %slice.126, f32[2,256,256]{2,1,0:T(8,128)S(1)} %bitcast.113, f32[128,320]{1,0:T(8,128)S(1)} %reshape.203), kind=kOutput, calls=%fused_computation.2 | convolution fusion | flops 251887616 | bytes 950272 | tf_op jit(solution)/shard_map/tw,bwc->btc/dot_general | solution.py:40
  23.7 0.3 convolution_bitcast_fusion
  24.0 0.1 fusion.41
  24.1 0.1 multiply_convert_fusion.1
  24.3 8.8 %collective-permute-start.3 = (bf16[128,1,256]{2,0,1:T(8,128)(2,1)S(1)}, bf16[128,1,256]{2,0,1:T(8,128)(2,1)S(1)}, u32[]{:S(2)}, u32[]{:S(2)}) collective-permute-start(bf16[128,1,256]{2,0,1:T(8,128)(2,1)S(1)} %fusion.25), channel_id=1, source_target_pairs={{1,24},{5,28},{2,25},{6,29},{3,26},{7,30}} | collective-permute-start | bytes 196616 | tf_op jit(solution)/shard_map/ppermute | solution.py:237
  33.1 0.6 %fusion.44 = (bf16[64,1,256]{2,0,1:T(8,128)(2,1)S(1)}, bf16[64,256]{1,0:T(8,128)(2,1)}) fusion(bf16[256,1,256]{2,0,1:T(8,128)(2,1)S(1)} %fusion.12), kind=kLoop, calls=%fused_computation.89 | loop fusion | bytes 98304 | tf_op jit(solution)/shard_map/slice | solution.py:246
  33.7 0.7 %collective-permute-done.3 = bf16[128,1,256]{2,0,1:T(8,128)(2,1)S(1)} collective-permute-done((bf16[128,1,256]{2,0,1:T(8,128)(2,1)S(1)}, bf16[128,1,256]{2,0,1:T(8,128)(2,1)S(1)}, u32[]{:S(2)}, u32[]{:S(2)}) %collective-permute-start.3) | collective-permute-done | bytes 65568 | tf_op jit(solution)/shard_map/ppermute | solution.py:237
  34.4 0.7 %fusion.23.ext_ref = bf16[192,256]{1,0:T(8,128)(2,1)} fusion(bf16[256,1,256]{2,0,1:T(8,128)(2,1)S(1)} %fusion.12, bf16[128,1,256]{2,0,1:T(8,128)(2,1)S(1)} %collective-permute-done.3, bf16[64,1,256]{2,0,1:T(8,128)(2,1)S(1)} %get-tuple-element.13, bf16[64,1,256]{2,0,1:T(8,128)(2,1)S(1)} %slice.134, bf16[128,1,256]{2,0,1:T(8,128)(2,1)S(1)} %slice.133, ...), kind=kLoop, calls=%fused_computation.56 | loop fusion | flops 491520 | bytes 393218 | tf_op jit(solution)/shard_map/reshape | solution.py:166
  35.0 4.9 %shard_map.28 = bf16[64,128,256]{2,1,0:T(8,128)(2,1)} custom-call(bf16[64,256]{1,0:T(8,128)(2,1)} %get-tuple-element.14.own_ref, bf16[192,256]{1,0:T(8,128)(2,1)} %fusion.23.ext_ref), custom_call_target="tpu_custom_call" | custom-call | flops 6291456 | bytes 4325376 | tf_op jit(solution)/shard_map/pallas_call | solution.py:186
  (33 shorter events, 0.6 us)
Async XLA Ops:
  0.0 13.5 %copy-start = (f32[64]{0:T(128)S(1)}, f32[64]{0:T(128)}, u32[]{:S(2)}) copy-start(f32[64]{0:T(128)} %param.3) | copy-start | bytes 772
  6.8 5.4 %collective-permute-start = (bf16[4,1,64,256]{3,2,0,1:T(8,128)(2,1)S(1)}, bf16[4,1,64,256]{3,2,0,1:T(8,128)(2,1)S(1)}, u32[]{:S(2)}, u32[]{:S(2)}) collective-permute-start(bf16[4,1,64,256]{3,2,0,1:T(8,128)(2,1)S(1)} %get-tuple-element.12), channel_id=1, source_target_pairs={{0,4},{4,0},{8,12},{12,8},{16,20},{20,16},{24,28},{28,24},{1,5},{5... | collective-permute-start | bytes 393224 | tf_op jit(solution)/shard_map/ppermute | solution.py:94
  12.2 3.9 %collective-permute-start.1 = (bf16[2,2,64,256]{3,2,1,0:T(8,128)(2,1)S(1)}, bf16[2,2,64,256]{3,2,1,0:T(8,128)(2,1)S(1)}, u32[]{:S(2)}, u32[]{:S(2)}) collective-permute-start(bf16[2,2,64,256]{3,2,1,0:T(8,128)(2,1)S(1)} %bitcast.131), channel_id=1, source_target_pairs={{0,8},{4,12},{8,0},{12,4},{16,24},{20,28},{24,16},{28,20},{1,9},{5... | collective-permute-start | bytes 393224 | tf_op jit(solution)/shard_map/ppermute | solution.py:94
  16.1 6.2 %collective-permute-start.2 = (bf16[1,4,64,256]{3,2,1,0:T(8,128)(2,1)S(1)}, bf16[1,4,64,256]{3,2,1,0:T(8,128)(2,1)S(1)}, u32[]{:S(2)}, u32[]{:S(2)}) collective-permute-start(bf16[1,4,64,256]{3,2,1,0:T(8,128)(2,1)S(1)} %get-tuple-element.8), channel_id=1, source_target_pairs={{0,16},{4,20},{8,24},{12,28},{16,0},{20,4},{24,8},{28,12},{1,17},{... | collective-permute-start | bytes 393224 | tf_op jit(solution)/shard_map/ppermute | solution.py:94
  24.3 10.1 %collective-permute-start.3 = (bf16[128,1,256]{2,0,1:T(8,128)(2,1)S(1)}, bf16[128,1,256]{2,0,1:T(8,128)(2,1)S(1)}, u32[]{:S(2)}, u32[]{:S(2)}) collective-permute-start(bf16[128,1,256]{2,0,1:T(8,128)(2,1)S(1)} %fusion.25), channel_id=1, source_target_pairs={{1,24},{5,28},{2,25},{6,29},{3,26},{7,30}} | collective-permute-start | bytes 196616 | tf_op jit(solution)/shard_map/ppermute | solution.py:237

commit v2 on v1

--- a/solution.py
+++ b/solution.py
@@ -72,29 +72,26 @@
     )
 
 
-def xor_order(chunks, position, extent):
-    bit = 1
-    while bit < extent:
-        shape = chunks.shape
-        swapped = chunks.reshape((extent // (2 * bit), 2, bit) + shape[1:])[:, ::-1].reshape(shape)
-        chunks = jnp.where((position & bit) != 0, swapped, chunks)
-        bit *= 2
-    return chunks
-
-
-def exchange_time(windows, position, extent):
-    if extent & (extent - 1) or extent > 16:
-        return lax.all_to_all(windows, "ta", split_axis=0, concat_axis=0, tiled=True)
-    chunks = xor_order(windows, position, extent)
-    bit = 1
-    while bit < extent:
-        shape = chunks.shape
-        view = chunks.reshape((extent // (2 * bit), 2, bit) + shape[1:])
-        route = [(i, i ^ bit) for i in range(extent)]
-        arrived = lax.ppermute(view[:, 1], "ta", route)
-        chunks = jnp.stack([view[:, 0], arrived], axis=1).reshape(shape)
-        bit *= 2
-    return xor_order(chunks, position, extent)
+def windows_kernel(before, after, width, x_ref, out_ref):
+    x = x_ref[...].astype(jnp.float32)
+    slab = x.shape[0]
+    step = (x.shape[1] + before + after - width) // (out_ref.shape[0] - 1)
+    padded = jnp.concatenate(
+        [jnp.zeros((slab, before), jnp.float32), x, jnp.zeros((slab, after), jnp.float32)], axis=1
+    )
+    for j in range(out_ref.shape[0]):
+        out_ref[j] = padded[:, j * step : j * step + width].astype(out_ref.dtype)
+
+
+def channel_windows(turned, extent, before, after, width):
+    slab, rows = turned.shape
+    return pl.pallas_call(
+        functools.partial(windows_kernel, before, after, width),
+        out_shape=jax.ShapeDtypeStruct((extent, slab, width), turned.dtype),
+        cost_estimate=pl.CostEstimate(
+            flops=0, transcendentals=0, bytes_accessed=2 * (slab * rows + extent * slab * width)
+        ),
+    )(turned)
 
 
 def cross_kernel(segments, rows_per_step, own_ref, ext_ref, out_ref):
@@ -206,19 +203,10 @@
     reach = LAGS // block_rows
     window = 2 * reach
     before = (reach - 1) * block_rows
-    turned = strain.T
-    padded = jnp.concatenate(
-        [
-            jnp.zeros((slab, before), strain.dtype),
-            turned,
-            jnp.zeros((slab, reach * block_rows), strain.dtype),
-        ],
-        axis=1,
-    )
-    windows = jnp.stack(
-        [padded[:, j * block_rows : (j + window) * block_rows] for j in range(extent)]
-    )
-    gathered = exchange_time(windows, position, extent)
+    windows = channel_windows(
+        strain.T, extent, before, reach * block_rows, window * block_rows
+    )
+    gathered = lax.all_to_all(windows, "ta", split_axis=0, concat_axis=0, tiled=True)
     samples = gathered.reshape(extent * slab, window * block_rows)
     filtered = decimate_t(samples.astype(jnp.float32), filter_taps)
     whitened = whiten_t(filtered).transpose(2, 0, 1)

time: 40.6 us -> 30.2 us (0.74)
  the two profiles are of different devices: /device:TPU:1 before, /device:TPU:29 now
where the time goes in v2:
time: 30.2 us; the launch traced here: 29.9 us
  waiting for transfers between devices  11.7 us (39%)
  starting transfers between devices  6.73 us (22%)
  Pallas kernels  6.65 us (22%)
  local copies, waits for them, and re-layouts  1.85 us (6%)
  other arithmetic  1.84 us (6%)
  matrix products  0.97 us (3%)
    ppermute x1, waiting for transfers between devices, body(): next_section = lax.ppermute(payload, ('ta', 'col'), route)  6.8 us
    all_to_all x1, starting transfers between devices, body(): lax.all_to_all(windows, 'ta', split_axis=0, concat_axis=0, tiled=True)  5.44 us
    pallas_call x1, Pallas kernels, cross_spectra(): pl.pallas_call(functools.partial(cross_kernel_shifted, segments, rows_per...  4.91 us
    all_to_all x1, waiting for transfers between devices, body(): lax.all_to_all(windows, 'ta', split_axis=0, concat_axis=0, tiled=True)  4.9 us
    pallas_call x1, Pallas kernels, channel_windows(): pl.pallas_call(functools.partial(windows_kernel, before, after, width), o...  1.74 us
    ppermute x1, starting transfers between devices, body(): next_section = lax.ppermute(payload, ('ta', 'col'), route)  1.29 us
    rev x1, local copies, waits for them, and re-layouts, tap_rows(): flipped = filter_taps[::-1]  0.75 us
    reshape x1, other arithmetic, cross_spectra(): ext_flat = extended.reshape(reach_rows, segments * columns)  0.67 us
  transfers between devices with their start and end apart: 2, of which 2 were waited for; matrix products, arithmetic and copies ran while one was open for 8% of the time, Pallas kernels for 0%

profile of v2, /device:TPU:29, one launch (start us, length us, event | category | flops | bytes accessed | tf_op | source)
XLA Modules:
  0.0 29.9 jit_solution(16600712413041469273)
XLA Ops:
  0.0 1.7 %shard_map.28 = bf16[8,64,256]{2,1,0:T(8,128)(2,1)} custom-call(bf16[64,512]{1,0:T(8,128)(2,1)} %bitcast.29), custom_call_target="tpu_custom_call" | custom-call | bytes 327680 | tf_op jit(solution)/shard_map/pallas_call | solution.py:88
  1.7 5.4 %all-to-all-start = ((bf16[8,64,256]{2,1,0:T(8,128)(2,1)}), bf16[8,64,256]{2,1,0:T(8,128)(2,1)S(1)}, u32[]{:S(2)}, u32[]{:S(2)}) async-start(bf16[8,64,256]{2,1,0:T(8,128)(2,1)} %shard_map.28), calls=%async_computation | async-start | bytes 524288 | tf_op jit(solution)/shard_map/all_to_all | solution.py:209
  7.2 0.7 %rev.3 = f32[64]{0:T(128)S(1)} reverse(f32[64]{0:T(128)} %param.3), dimensions={0} | reverse | bytes 512 | tf_op jit(solution)/shard_map/rev | solution.py:18
  7.9 0.1 pad.16.clone
  8.0 0.2 tile.10
  8.3 0.1 reshape.68
  8.4 0.5 %cosine_multiply_fusion = (f32[256,128]{1,0:T(8,128)S(1)}, f32[256,128]{1,0:T(8,128)S(1)}) fusion(s32[128]{0:T(128)S(1)} %iota_add_fusion, f32[256]{0:T(256)S(1)} %get-tuple-element.13, f32[256]{0:T(256)S(1)} %get-tuple-element.14), kind=kLoop, calls=%fused_computation.31 | loop fusion | flops 524288 | bytes 264704 | tf_op jit(solution)/shard_map/mul | solution.py:51
  9.0 4.9 %all-to-all-done = bf16[8,64,256]{2,1,0:T(8,128)(2,1)S(1)} async-done(((bf16[8,64,256]{2,1,0:T(8,128)(2,1)}), bf16[8,64,256]{2,1,0:T(8,128)(2,1)S(1)}, u32[]{:S(2)}, u32[]{:S(2)}) %all-to-all-start) | async-done | bytes 262176 | tf_op jit(solution)/shard_map/all_to_all | solution.py:209
  13.9 0.1 bitcast_convert_fusion
  14.0 0.3 maximum_maximum_fusion
  14.3 0.7 %fusion = bf16[2,128,256]{2,1,0:T(8,128)(2,1)S(1)} fusion(f32[2,64,256]{2,1,0:T(8,128)S(1)} %slice.56, f32[2,256,256]{2,1,0:T(8,128)S(1)} %bitcast.27, f32[128,320]{1,0:T(8,128)S(1)} %reshape.68), kind=kOutput, calls=%fused_computation.2 | convolution fusion | flops 251887616 | bytes 950272 | tf_op jit(solution)/shard_map/tw,bwc->btc/dot_general | solution.py:40
  15.0 0.3 %convolution_bitcast_fusion = f32[1,256,256]{1,2,0:T(8,128)S(1)} fusion(f32[256,128]{1,0:T(8,128)S(1)} %get-tuple-element.12, f32[256,128]{1,0:T(8,128)S(1)} %get-tuple-element.11, bf16[1,128,256]{2,1,0:T(8,128)(2,1)S(1)} %get-tuple-element.10, bf16[1,128,256]{2,1,0:T(8,128)(2,1)S(1)} %get-tuple-element.9), kind=kOutput, calls=%fused_computation | convolution fusion | flops 201654272 | bytes 655360 | tf_op jit(solution)/shard_map/nf,snc->sfc/dot_general | solution.py:59
  15.3 0.1 fusion.25
  15.4 0.1 multiply_convert_fusion.1
  15.6 1.3 %collective-permute-start = (bf16[128,1,256]{2,0,1:T(8,128)(2,1)S(1)}, bf16[128,1,256]{2,0,1:T(8,128)(2,1)S(1)}, u32[]{:S(2)}, u32[]{:S(2)}) collective-permute-start(bf16[128,1,256]{2,0,1:T(8,128)(2,1)S(1)} %fusion.20), channel_id=1, source_target_pairs={{1,24},{5,28},{2,25},{6,29},{3,26},{7,30}} | collective-permute-start | bytes 196616 | tf_op jit(solution)/shard_map/ppermute | solution.py:225
  16.9 0.6 %fusion.26 = (bf16[64,1,256]{2,0,1:T(8,128)(2,1)S(1)}, bf16[64,256]{1,0:T(8,128)(2,1)}) fusion(bf16[256,1,256]{2,0,1:T(8,128)(2,1)S(1)} %fusion.8), kind=kLoop, calls=%fused_computation.49 | loop fusion | bytes 98304 | tf_op jit(solution)/shard_map/slice | solution.py:234
  17.5 6.8 %collective-permute-done = bf16[128,1,256]{2,0,1:T(8,128)(2,1)S(1)} collective-permute-done((bf16[128,1,256]{2,0,1:T(8,128)(2,1)S(1)}, bf16[128,1,256]{2,0,1:T(8,128)(2,1)S(1)}, u32[]{:S(2)}, u32[]{:S(2)}) %collective-permute-start) | collective-permute-done | bytes 65568 | tf_op jit(solution)/shard_map/ppermute | solution.py:225
  24.3 0.7 %fusion.18.ext_ref = bf16[192,256]{1,0:T(8,128)(2,1)} fusion(bf16[256,1,256]{2,0,1:T(8,128)(2,1)S(1)} %fusion.8, bf16[128,1,256]{2,0,1:T(8,128)(2,1)S(1)} %collective-permute-done, bf16[64,1,256]{2,0,1:T(8,128)(2,1)S(1)} %get-tuple-element.7, bf16[64,1,256]{2,0,1:T(8,128)(2,1)S(1)} %slice.64, bf16[128,1,256]{2,0,1:T(8,128)(2,1)S(1)} %slice.63, pred[]{:T(512)S(6)} %eq.9, ...), kind=kLoop, calls=%fused_computation.37 | loop fusion | flops 491520 | bytes 393218 | tf_op jit(solution)/shard_map/reshape | solution.py:163
  25.0 4.9 %shard_map.29 = bf16[64,128,256]{2,1,0:T(8,128)(2,1)} custom-call(bf16[64,256]{1,0:T(8,128)(2,1)} %get-tuple-element.8.own_ref, bf16[192,256]{1,0:T(8,128)(2,1)} %fusion.18.ext_ref), custom_call_target="tpu_custom_call" | custom-call | flops 6291456 | bytes 4325376 | tf_op jit(solution)/shard_map/pallas_call | solution.py:183
  (16 shorter events, 0.2 us)
Async XLA Ops:
  1.7 12.2 %all-to-all-start = ((bf16[8,64,256]{2,1,0:T(8,128)(2,1)}), bf16[8,64,256]{2,1,0:T(8,128)(2,1)S(1)}, u32[]{:S(2)}, u32[]{:S(2)}) async-start(bf16[8,64,256]{2,1,0:T(8,128)(2,1)} %shard_map.28), calls=%async_computation | async-start | bytes 524288 | tf_op jit(solution)/shard_map/all_to_all | solution.py:209
  15.6 8.7 %collective-permute-start = (bf16[128,1,256]{2,0,1:T(8,128)(2,1)S(1)}, bf16[128,1,256]{2,0,1:T(8,128)(2,1)S(1)}, u32[]{:S(2)}, u32[]{:S(2)}) collective-permute-start(bf16[128,1,256]{2,0,1:T(8,128)(2,1)S(1)} %fusion.20), channel_id=1, source_target_pairs={{1,24},{5,28},{2,25},{6,29},{3,26},{7,30}} | collective-permute-start | bytes 196616 | tf_op jit(solution)/shard_map/ppermute | solution.py:225

commit v3 on v2

--- a/solution.py
+++ b/solution.py
@@ -156,6 +156,81 @@
         store_row(out_ref, i, acc_re, acc_im, segments)
 
 
+def cross_kernel_direct(segments, rows, reach, extent, before, chunk,
+                        pos_ref, win_ref, next_ref, out_hbm, own_f32, shifted, buffers, sems):
+    span = shifted.shape[1]
+    position = pos_ref[0]
+    own_f32[...] = win_ref[before : before + rows].astype(jnp.float32)
+    local = win_ref[before : before + (reach + 1) * rows].astype(jnp.float32)
+    following = next_ref[...].astype(jnp.float32)
+    extended = local
+    for j in range(extent - reach, extent):
+        kept = (extent - j) * rows
+        candidate = jnp.concatenate([local[:kept], following[: (reach + 1) * rows - kept]], axis=0)
+        extended = jnp.where(position == j, candidate, extended)
+    for i in range(chunk):
+        shifted[i] = extended[i : i + span]
+    copies = []
+    for m in range(rows // chunk):
+        slot = m % 2
+        if m >= 2:
+            copies[m - 2].wait()
+        base = m * chunk
+        for i in range(chunk):
+            acc_re = None
+            acc_im = None
+            for s in range(segments):
+                a = own_f32[base + i : base + i + 1, s * NFFT : (s + 1) * NFFT]
+                b = shifted[i, base : base + LAGS, s * NFFT : (s + 1) * NFFT]
+                terms = product_terms(a, b)
+                if acc_re is None:
+                    acc_re, acc_im = terms
+                else:
+                    acc_re = [x + y for x, y in zip(acc_re, terms[0])]
+                    acc_im = [x + y for x, y in zip(acc_im, terms[1])]
+            store_row(buffers.at[slot], i, acc_re, acc_im, segments)
+        copy = pltpu.make_async_copy(
+            buffers.at[slot], out_hbm.at[pl.ds(base, chunk)], sems.at[slot]
+        )
+        copy.start()
+        copies.append(copy)
+    for copy in copies[-2:]:
+        copy.wait()
+
+
+def cross_spectra_direct(whitened, following, position, rows, reach, extent, before):
+    window_rows, segments, columns = whitened.shape
+    chunk = 8
+    reach_rows = (reach + 1) * rows
+    span = reach_rows - chunk
+    width = segments * columns
+    return pl.pallas_call(
+        functools.partial(cross_kernel_direct, segments, rows, reach, extent, before, chunk),
+        out_shape=jax.ShapeDtypeStruct((rows, LAGS, columns), jnp.bfloat16),
+        in_specs=[
+            pl.BlockSpec(memory_space=pltpu.SMEM),
+            pl.BlockSpec(memory_space=pltpu.VMEM),
+            pl.BlockSpec(memory_space=pltpu.VMEM),
+        ],
+        out_specs=pl.BlockSpec(memory_space=pl.ANY),
+        scratch_shapes=[
+            pltpu.VMEM((rows, width), jnp.float32),
+            pltpu.VMEM((chunk, span, width), jnp.float32),
+            pltpu.VMEM((2, chunk, LAGS, columns), jnp.bfloat16),
+            pltpu.SemaphoreType.DMA((2,)),
+        ],
+        cost_estimate=pl.CostEstimate(
+            flops=6 * rows * LAGS * NF * segments,
+            transcendentals=0,
+            bytes_accessed=rows * LAGS * columns * 2 + 2 * (window_rows + following.shape[0]) * width,
+        ),
+    )(
+        position.reshape(1).astype(jnp.int32),
+        whitened.reshape(window_rows, width),
+        following.reshape(following.shape[0], width),
+    )
+
+
 def cross_spectra(own, extended):
     rows, segments, columns = own.shape
     reach_rows = extended.shape[0]
@@ -223,6 +298,10 @@
         for m in range(reach)
     ]
     next_section = lax.ppermute(payload, ("ta", "col"), route)
+    if segments * 8 * (reach + 1) * block_rows * columns * 4 <= 8 * 1024 * 1024:
+        return cross_spectra_direct(
+            whitened, next_section, position, block_rows, reach, extent, before
+        )[None]
     local = whitened[before : before + (reach + 1) * block_rows]
     extended = local
     for j in range(extent - reach, extent):

time: 30.2 us -> 30.2 us (level)
    unnamed x0 -> x2, local copies, waits for them, and re-layouts: none -> 0.62 us
    slice x3 -> x0, local copies, waits for them, and re-layouts: 0.61 us -> none  [the longest x1 0.61 us: body(): own = local[:block_rows]]
where the time goes in v3:
time: 30.2 us; the launch traced here: 29.9 us
  waiting for transfers between devices  11.7 us (39%)
  starting transfers between devices  6.73 us (22%)
  Pallas kernels  6.71 us (22%)
  local copies, waits for them, and re-layouts  1.86 us (6%)
  other arithmetic  1.81 us (6%)
  matrix products  0.97 us (3%)
    ppermute x1, waiting for transfers between devices, body(): next_section = lax.ppermute(payload, ('ta', 'col'), route)  6.75 us
    all_to_all x1, starting transfers between devices, body(): lax.all_to_all(windows, 'ta', split_axis=0, concat_axis=0, tiled=True)  5.44 us
    pallas_call x1, Pallas kernels, cross_spectra_direct(): pl.pallas_call(functools.partial(cross_kernel_direct, segments, rows, rea...  4.97 us
    all_to_all x1, waiting for transfers between devices, body(): lax.all_to_all(windows, 'ta', split_axis=0, concat_axis=0, tiled=True)  4.9 us
    pallas_call x1, Pallas kernels, channel_windows(): pl.pallas_call(functools.partial(windows_kernel, before, after, width), o...  1.74 us
    ppermute x1, starting transfers between devices, body(): next_section = lax.ppermute(payload, ('ta', 'col'), route)  1.29 us
    rev x1, local copies, waits for them, and re-layouts, tap_rows(): flipped = filter_taps[::-1]  0.75 us
    reshape x1, other arithmetic, cross_spectra_direct(): whitened.reshape(window_rows, width)  0.66 us
  transfers between devices with their start and end apart: 2, of which 2 were waited for; matrix products, arithmetic and copies ran while one was open for 8% of the time, Pallas kernels for 0%

profile of v3, /device:TPU:29, one launch (start us, length us, event | category | flops | bytes accessed | tf_op | source)
XLA Modules:
  0.0 29.9 jit_solution(4034861191043428024)
XLA Ops:
  0.0 1.7 %shard_map.28 = bf16[8,64,256]{2,1,0:T(8,128)(2,1)} custom-call(bf16[64,512]{1,0:T(8,128)(2,1)} %bitcast.30), custom_call_target="tpu_custom_call" | custom-call | bytes 327680 | tf_op jit(solution)/shard_map/pallas_call | solution.py:88
  1.7 5.4 %all-to-all-start = ((bf16[8,64,256]{2,1,0:T(8,128)(2,1)}), bf16[8,64,256]{2,1,0:T(8,128)(2,1)S(1)}, u32[]{:S(2)}, u32[]{:S(2)}) async-start(bf16[8,64,256]{2,1,0:T(8,128)(2,1)} %shard_map.28), calls=%async_computation | async-start | bytes 524288 | tf_op jit(solution)/shard_map/all_to_all | solution.py:284
  7.2 0.7 %rev.3 = f32[64]{0:T(128)S(1)} reverse(f32[64]{0:T(128)} %param.3), dimensions={0} | reverse | bytes 512 | tf_op jit(solution)/shard_map/rev | solution.py:18
  7.9 0.1 pad.12.clone
  8.0 0.2 tile.10
  8.3 0.1 reshape.72
  8.4 0.5 %cosine_multiply_fusion = (f32[256,128]{1,0:T(8,128)S(1)}, f32[256,128]{1,0:T(8,128)S(1)}) fusion(s32[128]{0:T(128)S(1)} %iota_add_fusion, f32[256]{0:T(256)S(1)} %get-tuple-element.11, f32[256]{0:T(256)S(1)} %get-tuple-element.12), kind=kLoop, calls=%fused_computation.31 | loop fusion | flops 524288 | bytes 264704 | tf_op jit(solution)/shard_map/mul | solution.py:51
  9.0 4.9 %all-to-all-done = bf16[8,64,256]{2,1,0:T(8,128)(2,1)S(1)} async-done(((bf16[8,64,256]{2,1,0:T(8,128)(2,1)}), bf16[8,64,256]{2,1,0:T(8,128)(2,1)S(1)}, u32[]{:S(2)}, u32[]{:S(2)}) %all-to-all-start) | async-done | bytes 262176 | tf_op jit(solution)/shard_map/all_to_all | solution.py:284
  13.9 0.1 bitcast_convert_fusion
  14.0 0.3 maximum_maximum_fusion
  14.3 0.7 %fusion = bf16[2,128,256]{2,1,0:T(8,128)(2,1)S(1)} fusion(f32[2,64,256]{2,1,0:T(8,128)S(1)} %slice.37, f32[2,256,256]{2,1,0:T(8,128)S(1)} %bitcast.27, f32[128,320]{1,0:T(8,128)S(1)} %reshape.72), kind=kOutput, calls=%fused_computation.2 | convolution fusion | flops 251887616 | bytes 950272 | tf_op jit(solution)/shard_map/tw,bwc->btc/dot_general | solution.py:40
  15.0 0.3 %convolution_bitcast_fusion = f32[1,256,256]{1,2,0:T(8,128)S(1)} fusion(f32[256,128]{1,0:T(8,128)S(1)} %get-tuple-element.10, f32[256,128]{1,0:T(8,128)S(1)} %get-tuple-element.9, bf16[1,128,256]{2,1,0:T(8,128)(2,1)S(1)} %get-tuple-element.8, bf16[1,128,256]{2,1,0:T(8,128)(2,1)S(1)} %get-tuple-element.7), kind=kOutput, calls=%fused_computation | convolution fusion | flops 201654272 | bytes 655360 | tf_op jit(solution)/shard_map/nf,snc->sfc/dot_general | solution.py:59
  15.3 0.1 fusion.23
  15.4 0.1 multiply_convert_fusion.1
  15.6 1.3 %collective-permute-start = (bf16[128,1,256]{2,0,1:T(8,128)(2,1)S(1)}, bf16[128,1,256]{2,0,1:T(8,128)(2,1)S(1)}, u32[]{:S(2)}, u32[]{:S(2)}) collective-permute-start(bf16[128,1,256]{2,0,1:T(8,128)(2,1)S(1)} %fusion.18), channel_id=1, source_target_pairs={{1,24},{5,28},{2,25},{6,29},{3,26},{7,30}} | collective-permute-start | bytes 196616 | tf_op jit(solution)/shard_map/ppermute | solution.py:300
  16.9 0.7 %fusion.8.win_ref = bf16[256,256]{1,0:T(8,128)(2,1)} fusion(bf16[1,128,256]{1,2,0:T(8,128)(2,1)S(1)} %get-tuple-element.6, bf16[1,128,256]{1,2,0:T(8,128)(2,1)S(1)} %get-tuple-element.5), kind=kLoop, calls=%fused_computation.19 | loop fusion | flops 262144 | bytes 262144 | tf_op jit(solution)/shard_map/reshape | solution.py:229
  17.5 6.7 %collective-permute-done = bf16[128,1,256]{2,0,1:T(8,128)(2,1)S(1)} collective-permute-done((bf16[128,1,256]{2,0,1:T(8,128)(2,1)S(1)}, bf16[128,1,256]{2,0,1:T(8,128)(2,1)S(1)}, u32[]{:S(2)}, u32[]{:S(2)}) %collective-permute-start) | collective-permute-done | bytes 65568 | tf_op jit(solution)/shard_map/ppermute | solution.py:300
  24.3 0.0 copy-start
  24.3 0.6 %copy-done = bf16[128,1,256]{2,0,1:T(8,128)(2,1)} copy-done((bf16[128,1,256]{2,0,1:T(8,128)(2,1)}, bf16[128,1,256]{2,0,1:T(8,128)(2,1)S(1)}, u32[]{:S(2)}) %copy-start) | copy-done | bytes 65560
  24.9 5.0 %shard_map.29 = bf16[64,128,256]{2,1,0:T(8,128)(2,1)} custom-call(s32[1]{0:T(128)} %bitcast.pos_ref, bf16[256,256]{1,0:T(8,128)(2,1)} %fusion.8.win_ref, bf16[128,256]{1,0:T(8,128)(2,1)} %bitcast.29), custom_call_target="tpu_custom_call" | custom-call | flops 6291456 | bytes 4390912 | tf_op jit(solution)/shard_map/pallas_call | solution.py:207
  (13 shorter events, 0.2 us)
Async XLA Ops:
  1.7 12.2 %all-to-all-start = ((bf16[8,64,256]{2,1,0:T(8,128)(2,1)}), bf16[8,64,256]{2,1,0:T(8,128)(2,1)S(1)}, u32[]{:S(2)}, u32[]{:S(2)}) async-start(bf16[8,64,256]{2,1,0:T(8,128)(2,1)} %shard_map.28), calls=%async_computation | async-start | bytes 524288 | tf_op jit(solution)/shard_map/all_to_all | solution.py:284
  15.6 8.7 %collective-permute-start = (bf16[128,1,256]{2,0,1:T(8,128)(2,1)S(1)}, bf16[128,1,256]{2,0,1:T(8,128)(2,1)S(1)}, u32[]{:S(2)}, u32[]{:S(2)}) collective-permute-start(bf16[128,1,256]{2,0,1:T(8,128)(2,1)S(1)} %fusion.18), channel_id=1, source_target_pairs={{1,24},{5,28},{2,25},{6,29},{3,26},{7,30}} | collective-permute-start | bytes 196616 | tf_op jit(solution)/shard_map/ppermute | solution.py:300
  24.3 0.6 %copy-start = (bf16[128,1,256]{2,0,1:T(8,128)(2,1)}, bf16[128,1,256]{2,0,1:T(8,128)(2,1)S(1)}, u32[]{:S(2)}) copy-start(bf16[128,1,256]{2,0,1:T(8,128)(2,1)S(1)} %collective-permute-done) | copy-start | bytes 196612

commit v4 on v3

--- a/solution.py
+++ b/solution.py
@@ -123,8 +123,11 @@
 
 
 def store_row(out_ref, i, acc_re, acc_im, segments):
-    re = (acc_re[0] + acc_re[1]) / segments
-    im = (acc_im[0] - acc_im[1]) / segments
+    re = acc_re[0] + acc_re[1]
+    im = acc_im[0] - acc_im[1]
+    if segments > 1:
+        re = re / segments
+        im = im / segments
     out_ref[i, :, :NF] = re.astype(out_ref.dtype)
     out_ref[i, :, NF:] = im.astype(out_ref.dtype)
 
@@ -157,16 +160,30 @@
 
 
 def cross_kernel_direct(segments, rows, reach, extent, before, chunk,
-                        pos_ref, win_ref, next_ref, out_hbm, own_f32, shifted, buffers, sems):
+                        pos_ref, win_ref, next_hbm, out_hbm, own_f32, shifted, following,
+                        buffers, sems, next_sem):
+    fetch = pltpu.make_async_copy(next_hbm, following, next_sem)
+    fetch.start()
     span = shifted.shape[1]
     position = pos_ref[0]
-    own_f32[...] = win_ref[before : before + rows].astype(jnp.float32)
-    local = win_ref[before : before + (reach + 1) * rows].astype(jnp.float32)
-    following = next_ref[...].astype(jnp.float32)
+    width = (reach + 1) * rows
+    local = jnp.concatenate(
+        [
+            win_ref[s * NFFT : (s + 1) * NFFT, before : before + width].astype(jnp.float32).T
+            for s in range(segments)
+        ],
+        axis=1,
+    )
+    own_f32[...] = local[:rows]
+    fetch.wait()
+    arrived = jnp.concatenate(
+        [following[s * NFFT : (s + 1) * NFFT, :].astype(jnp.float32).T for s in range(segments)],
+        axis=1,
+    )
     extended = local
     for j in range(extent - reach, extent):
         kept = (extent - j) * rows
-        candidate = jnp.concatenate([local[:kept], following[: (reach + 1) * rows - kept]], axis=0)
+        candidate = jnp.concatenate([local[:kept], arrived[: width - kept]], axis=0)
         extended = jnp.where(position == j, candidate, extended)
     for i in range(chunk):
         shifted[i] = extended[i : i + span]
@@ -198,37 +215,35 @@
         copy.wait()
 
 
-def cross_spectra_direct(whitened, following, position, rows, reach, extent, before):
-    window_rows, segments, columns = whitened.shape
+def cross_spectra_direct(whitened_t, following_t, position, rows, reach, extent, before):
+    width, window_rows = whitened_t.shape
+    segments = width // NFFT
     chunk = 8
     reach_rows = (reach + 1) * rows
     span = reach_rows - chunk
-    width = segments * columns
     return pl.pallas_call(
         functools.partial(cross_kernel_direct, segments, rows, reach, extent, before, chunk),
-        out_shape=jax.ShapeDtypeStruct((rows, LAGS, columns), jnp.bfloat16),
+        out_shape=jax.ShapeDtypeStruct((rows, LAGS, NFFT), jnp.bfloat16),
         in_specs=[
             pl.BlockSpec(memory_space=pltpu.SMEM),
             pl.BlockSpec(memory_space=pltpu.VMEM),
-            pl.BlockSpec(memory_space=pltpu.VMEM),
+            pl.BlockSpec(memory_space=pl.ANY),
         ],
         out_specs=pl.BlockSpec(memory_space=pl.ANY),
         scratch_shapes=[
             pltpu.VMEM((rows, width), jnp.float32),
             pltpu.VMEM((chunk, span, width), jnp.float32),
-            pltpu.VMEM((2, chunk, LAGS, columns), jnp.bfloat16),
+            pltpu.VMEM(following_t.shape, following_t.dtype),
+            pltpu.VMEM((2, chunk, LAGS, NFFT), jnp.bfloat16),
             pltpu.SemaphoreType.DMA((2,)),
+            pltpu.SemaphoreType.DMA(()),
         ],
         cost_estimate=pl.CostEstimate(
             flops=6 * rows * LAGS * NF * segments,
             transcendentals=0,
-            bytes_accessed=rows * LAGS * columns * 2 + 2 * (window_rows + following.shape[0]) * width,
+            bytes_accessed=rows * LAGS * NFFT * 2 + 2 * (window_rows + following_t.shape[1]) * width,
         ),
-    )(
-        position.reshape(1).astype(jnp.int32),
-        whitened.reshape(window_rows, width),
-        following.reshape(following.shape[0], width),
-    )
+    )(position.reshape(1).astype(jnp.int32), whitened_t, following_t)
 
 
 def cross_spectra(own, extended):
@@ -284,10 +299,9 @@
     gathered = lax.all_to_all(windows, "ta", split_axis=0, concat_axis=0, tiled=True)
     samples = gathered.reshape(extent * slab, window * block_rows)
     filtered = decimate_t(samples.astype(jnp.float32), filter_taps)
-    whitened = whiten_t(filtered).transpose(2, 0, 1)
-    segments, columns = whitened.shape[1:]
+    whitened_t = whiten_t(filtered)
+    segments, columns, window_rows = whitened_t.shape
     first_of_section = reach - 1 - jnp.minimum(position, reach - 1)
-    payload = lax.dynamic_slice_in_dim(whitened, first_of_section * block_rows, reach * block_rows, 0)
 
     def linear(ta_index, col_index):
         return ta_index * columns_n + col_index
@@ -297,11 +311,16 @@
         for c in range(columns_n - 1)
         for m in range(reach)
     ]
+    if segments * 8 * (reach + 1) * block_rows * columns * 4 <= 8 * 1024 * 1024:
+        flat = whitened_t.reshape(segments * columns, window_rows)
+        payload = lax.dynamic_slice_in_dim(flat, first_of_section * block_rows, reach * block_rows, 1)
+        next_section = lax.ppermute(payload, ("ta", "col"), route)
+        return cross_spectra_direct(
+            flat, next_section, position, block_rows, reach, extent, before
+        )[None]
+    whitened = whitened_t.transpose(2, 0, 1)
+    payload = lax.dynamic_slice_in_dim(whitened, first_of_section * block_rows, reach * block_rows, 0)
     next_section = lax.ppermute(payload, ("ta", "col"), route)
-    if segments * 8 * (reach + 1) * block_rows * columns * 4 <= 8 * 1024 * 1024:
-        return cross_spectra_direct(
-            whitened, next_section, position, block_rows, reach, extent, before
-        )[None]
     local = whitened[before : before + (reach + 1) * block_rows]
     extended = local
     for j in range(extent - reach, extent):

time: 30.2 us -> 31.1 us (1.030)
  Pallas kernels: 6.71 us -> 7.53 us
    pallas_call x1, Pallas kernels: 4.97 us -> 5.79 us  [cross_spectra_direct(): pl.pallas_call(functools.partial(cross_kernel_direct, segments, rows, rea...]
    reshape x1 -> x0, other arithmetic: 0.66 us -> none  [cross_spectra_direct(): whitened.reshape(window_rows, width)]
    concatenate x0 -> x1, other arithmetic: none -> 0.65 us  [whiten_t(): jnp.concatenate([real_part * whitening, imag_part * whitening], axis=1)]
where the time goes in v4:
time: 31.1 us; the launch traced here: 30.8 us
  waiting for transfers between devices  11.7 us (38%)
  Pallas kernels  7.53 us (24%)
  starting transfers between devices  6.73 us (22%)
  local copies, waits for them, and re-layouts  1.86 us (6%)
  other arithmetic  1.85 us (6%)
  matrix products  1.04 us (3%)
    ppermute x1, waiting for transfers between devices, body(): next_section = lax.ppermute(payload, ('ta', 'col'), route)  6.75 us
    pallas_call x1, Pallas kernels, cross_spectra_direct(): pl.pallas_call(functools.partial(cross_kernel_direct, segments, rows, rea...  5.79 us
    all_to_all x1, starting transfers between devices, body(): lax.all_to_all(windows, 'ta', split_axis=0, concat_axis=0, tiled=True)  5.44 us
    all_to_all x1, waiting for transfers between devices, body(): lax.all_to_all(windows, 'ta', split_axis=0, concat_axis=0, tiled=True)  4.9 us
    pallas_call x1, Pallas kernels, channel_windows(): pl.pallas_call(functools.partial(windows_kernel, before, after, width), o...  1.74 us
    ppermute x1, starting transfers between devices, body(): next_section = lax.ppermute(payload, ('ta', 'col'), route)  1.29 us
    rev x1, local copies, waits for them, and re-layouts, tap_rows(): flipped = filter_taps[::-1]  0.75 us
    concatenate x1, other arithmetic, whiten_t(): jnp.concatenate([real_part * whitening, imag_part * whitening], axis=1)  0.65 us
  transfers between devices with their start and end apart: 2, of which 2 were waited for; matrix products, arithmetic and copies ran while one was open for 8% of the time, Pallas kernels for 0%

profile of v4, /device:TPU:29, one launch (start us, length us, event | category | flops | bytes accessed | tf_op | source)
XLA Modules:
  0.0 30.8 jit_solution(4388009034556170551)
XLA Ops:
  0.0 1.7 %shard_map.28 = bf16[8,64,256]{2,1,0:T(8,128)(2,1)} custom-call(bf16[64,512]{1,0:T(8,128)(2,1)} %bitcast.28), custom_call_target="tpu_custom_call" | custom-call | bytes 327680 | tf_op jit(solution)/shard_map/pallas_call | solution.py:88
  1.7 5.4 %all-to-all-start = ((bf16[8,64,256]{2,1,0:T(8,128)(2,1)}), bf16[8,64,256]{2,1,0:T(8,128)(2,1)S(1)}, u32[]{:S(2)}, u32[]{:S(2)}) async-start(bf16[8,64,256]{2,1,0:T(8,128)(2,1)} %shard_map.28), calls=%async_computation | async-start | bytes 524288 | tf_op jit(solution)/shard_map/all_to_all | solution.py:299
  7.2 0.7 %rev.3 = f32[64]{0:T(128)S(1)} reverse(f32[64]{0:T(128)} %param.3), dimensions={0} | reverse | bytes 512 | tf_op jit(solution)/shard_map/rev | solution.py:18
  7.9 0.1 pad.14.clone
  8.0 0.2 tile.10
  8.3 0.1 reshape.74
  8.4 0.5 %cosine_multiply_fusion = (f32[256,128]{1,0:T(8,128)S(1)}, f32[256,128]{1,0:T(8,128)S(1)}) fusion(s32[128]{0:T(128)S(1)} %iota_add_fusion, f32[256]{0:T(256)S(1)} %get-tuple-element.11, f32[256]{0:T(256)S(1)} %get-tuple-element.12), kind=kLoop, calls=%fused_computation.30 | loop fusion | flops 524288 | bytes 264704 | tf_op jit(solution)/shard_map/mul | solution.py:51
  9.0 4.9 %all-to-all-done = bf16[8,64,256]{2,1,0:T(8,128)(2,1)S(1)} async-done(((bf16[8,64,256]{2,1,0:T(8,128)(2,1)}), bf16[8,64,256]{2,1,0:T(8,128)(2,1)S(1)}, u32[]{:S(2)}, u32[]{:S(2)}) %all-to-all-start) | async-done | bytes 262176 | tf_op jit(solution)/shard_map/all_to_all | solution.py:299
  13.9 0.1 bitcast_convert_fusion
  14.0 0.3 maximum_maximum_fusion
  14.3 0.7 %fusion = bf16[2,128,256]{2,1,0:T(8,128)(2,1)S(1)} fusion(f32[2,64,256]{2,1,0:T(8,128)S(1)} %slice.37, f32[2,256,256]{2,1,0:T(8,128)S(1)} %bitcast.24, f32[128,320]{1,0:T(8,128)S(1)} %reshape.74), kind=kOutput, calls=%fused_computation.2 | convolution fusion | flops 251887616 | bytes 950272 | tf_op jit(solution)/shard_map/tw,bwc->btc/dot_general | solution.py:40
  15.0 0.4 %convolution_bitcast_fusion = f32[1,256,256]{2,1,0:T(8,128)S(1)} fusion(f32[256,128]{1,0:T(8,128)S(1)} %get-tuple-element.10, f32[256,128]{1,0:T(8,128)S(1)} %get-tuple-element.9, bf16[1,128,256]{2,1,0:T(8,128)(2,1)S(1)} %get-tuple-element.8, bf16[1,128,256]{2,1,0:T(8,128)(2,1)S(1)} %get-tuple-element.7), kind=kOutput, calls=%fused_computation | convolution fusion | flops 201654272 | bytes 655360 | tf_op jit(solution)/shard_map/nf,snc->sfc/dot_general | solution.py:59
  15.4 0.1 multiply_convert_fusion.1
  15.5 0.2 fusion.17
  15.7 1.3 %collective-permute-start = (bf16[256,128]{1,0:T(8,128)(2,1)S(1)}, bf16[256,128]{1,0:T(8,128)(2,1)S(1)}, u32[]{:S(2)}, u32[]{:S(2)}) collective-permute-start(bf16[256,128]{1,0:T(8,128)(2,1)S(1)} %fusion.17), channel_id=1, source_target_pairs={{1,24},{5,28},{2,25},{6,29},{3,26},{7,30}} | collective-permute-start | bytes 196616 | tf_op jit(solution)/shard_map/ppermute | solution.py:317
  17.0 0.7 %pad_maximum_fusion.win_ref = bf16[256,256]{1,0:T(8,128)(2,1)} fusion(bf16[128,256]{1,0:T(8,128)(2,1)S(1)} %bitcast.27, bf16[128,256]{1,0:T(8,128)(2,1)S(1)} %bitcast.26), kind=kLoop, calls=%fused_computation.22 | loop fusion | flops 262144 | bytes 262144 | tf_op jit(solution)/shard_map/concatenate | solution.py:70
  17.6 6.8 %collective-permute-done.next_hbm = bf16[256,128]{1,0:T(8,128)(2,1)S(1)} collective-permute-done((bf16[256,128]{1,0:T(8,128)(2,1)S(1)}, bf16[256,128]{1,0:T(8,128)(2,1)S(1)}, u32[]{:S(2)}, u32[]{:S(2)}) %collective-permute-start) | collective-permute-done | bytes 65568 | tf_op jit(solution)/shard_map/ppermute | solution.py:317
  24.4 0.0 copy-start
  24.4 0.6 %copy-done = bf16[256,128]{1,0:T(8,128)(2,1)} copy-done((bf16[256,128]{1,0:T(8,128)(2,1)}, bf16[256,128]{1,0:T(8,128)(2,1)S(1)}, u32[]{:S(2)}) %copy-start) | copy-done | bytes 65560
  25.0 5.8 %shard_map.29 = bf16[64,128,256]{2,1,0:T(8,128)(2,1)} custom-call(s32[1]{0:T(128)} %bitcast.pos_ref, bf16[256,256]{1,0:T(8,128)(2,1)} %pad_maximum_fusion.win_ref, bf16[256,128]{1,0:T(8,128)(2,1)} %copy-done), custom_call_target="tpu_custom_call" | custom-call | flops 6291456 | bytes 4390912 | tf_op jit(solution)/shard_map/pallas_call | solution.py:224
  (13 shorter events, 0.2 us)
Async XLA Ops:
  1.7 12.2 %all-to-all-start = ((bf16[8,64,256]{2,1,0:T(8,128)(2,1)}), bf16[8,64,256]{2,1,0:T(8,128)(2,1)S(1)}, u32[]{:S(2)}, u32[]{:S(2)}) async-start(bf16[8,64,256]{2,1,0:T(8,128)(2,1)} %shard_map.28), calls=%async_computation | async-start | bytes 524288 | tf_op jit(solution)/shard_map/all_to_all | solution.py:299
  15.7 8.7 %collective-permute-start = (bf16[256,128]{1,0:T(8,128)(2,1)S(1)}, bf16[256,128]{1,0:T(8,128)(2,1)S(1)}, u32[]{:S(2)}, u32[]{:S(2)}) collective-permute-start(bf16[256,128]{1,0:T(8,128)(2,1)S(1)} %fusion.17), channel_id=1, source_target_pairs={{1,24},{5,28},{2,25},{6,29},{3,26},{7,30}} | collective-permute-start | bytes 196616 | tf_op jit(solution)/shard_map/ppermute | solution.py:317
  24.4 0.6 %copy-start = (bf16[256,128]{1,0:T(8,128)(2,1)}, bf16[256,128]{1,0:T(8,128)(2,1)S(1)}, u32[]{:S(2)}) copy-start(bf16[256,128]{1,0:T(8,128)(2,1)S(1)} %collective-permute-done.next_hbm) | copy-start | bytes 196612

commit v5 on v4

--- a/solution.py
+++ b/solution.py
@@ -187,11 +187,14 @@
         extended = jnp.where(position == j, candidate, extended)
     for i in range(chunk):
         shifted[i] = extended[i : i + span]
+    slots, parts = buffers.shape[0], sems.shape[1]
+    part = chunk // parts
     copies = []
     for m in range(rows // chunk):
-        slot = m % 2
-        if m >= 2:
-            copies[m - 2].wait()
+        slot = m % slots
+        if m >= slots:
+            for copy in copies[m - slots]:
+                copy.wait()
         base = m * chunk
         for i in range(chunk):
             acc_re = None
@@ -206,13 +209,19 @@
                     acc_re = [x + y for x, y in zip(acc_re, terms[0])]
                     acc_im = [x + y for x, y in zip(acc_im, terms[1])]
             store_row(buffers.at[slot], i, acc_re, acc_im, segments)
-        copy = pltpu.make_async_copy(
-            buffers.at[slot], out_hbm.at[pl.ds(base, chunk)], sems.at[slot]
-        )
-        copy.start()
-        copies.append(copy)
-    for copy in copies[-2:]:
-        copy.wait()
+        group = []
+        for p in range(parts):
+            copy = pltpu.make_async_copy(
+                buffers.at[slot, pl.ds(p * part, part)],
+                out_hbm.at[pl.ds(base + p * part, part)],
+                sems.at[slot, p],
+            )
+            copy.start()
+            group.append(copy)
+        copies.append(group)
+    for group in copies[-slots:]:
+        for copy in group:
+            copy.wait()
 
 
 def cross_spectra_direct(whitened_t, following_t, position, rows, reach, extent, before):
@@ -234,8 +243,8 @@
             pltpu.VMEM((rows, width), jnp.float32),
             pltpu.VMEM((chunk, span, width), jnp.float32),
             pltpu.VMEM(following_t.shape, following_t.dtype),
-            pltpu.VMEM((2, chunk, LAGS, NFFT), jnp.bfloat16),
-            pltpu.SemaphoreType.DMA((2,)),
+            pltpu.VMEM((4, chunk, LAGS, NFFT), jnp.bfloat16),
+            pltpu.SemaphoreType.DMA((4, 4)),
             pltpu.SemaphoreType.DMA(()),
         ],
         cost_estimate=pl.CostEstimate(

time: 31.1 us -> 29.7 us (0.955)
  Pallas kernels: 7.53 us -> 6.12 us
    pallas_call x1, Pallas kernels: 5.79 us -> 4.37 us  [cross_spectra_direct(): pl.pallas_call(functools.partial(cross_kernel_direct, segments, rows, rea...]
where the time goes in v5:
time: 29.7 us; the launch traced here: 29.4 us
  waiting for transfers between devices  11.7 us (39%)
  starting transfers between devices  6.73 us (23%)
  Pallas kernels  6.12 us (21%)
  local copies, waits for them, and re-layouts  1.86 us (6%)
  other arithmetic  1.85 us (6%)
  matrix products  1.04 us (4%)
    ppermute x1, waiting for transfers between devices, body(): next_section = lax.ppermute(payload, ('ta', 'col'), route)  6.75 us
    all_to_all x1, starting transfers between devices, body(): lax.all_to_all(windows, 'ta', split_axis=0, concat_axis=0, tiled=True)  5.44 us
    all_to_all x1, waiting for transfers between devices, body(): lax.all_to_all(windows, 'ta', split_axis=0, concat_axis=0, tiled=True)  4.9 us
    pallas_call x1, Pallas kernels, cross_spectra_direct(): pl.pallas_call(functools.partial(cross_kernel_direct, segments, rows, rea...  4.37 us
    pallas_call x1, Pallas kernels, channel_windows(): pl.pallas_call(functools.partial(windows_kernel, before, after, width), o...  1.74 us
    ppermute x1, starting transfers between devices, body(): next_section = lax.ppermute(payload, ('ta', 'col'), route)  1.29 us
    rev x1, local copies, waits for them, and re-layouts, tap_rows(): flipped = filter_taps[::-1]  0.75 us
    concatenate x1, other arithmetic, whiten_t(): jnp.concatenate([real_part * whitening, imag_part * whitening], axis=1)  0.65 us
  transfers between devices with their start and end apart: 2, of which 2 were waited for; matrix products, arithmetic and copies ran while one was open for 8% of the time, Pallas kernels for 0%

profile of v5, /device:TPU:29, one launch (start us, length us, event | category | flops | bytes accessed | tf_op | source)
XLA Modules:
  0.0 29.4 jit_solution(1242850943612747469)
XLA Ops:
  0.0 1.7 %shard_map.28 = bf16[8,64,256]{2,1,0:T(8,128)(2,1)} custom-call(bf16[64,512]{1,0:T(8,128)(2,1)} %bitcast.28), custom_call_target="tpu_custom_call" | custom-call | bytes 327680 | tf_op jit(solution)/shard_map/pallas_call | solution.py:88
  1.7 5.4 %all-to-all-start = ((bf16[8,64,256]{2,1,0:T(8,128)(2,1)}), bf16[8,64,256]{2,1,0:T(8,128)(2,1)S(1)}, u32[]{:S(2)}, u32[]{:S(2)}) async-start(bf16[8,64,256]{2,1,0:T(8,128)(2,1)} %shard_map.28), calls=%async_computation | async-start | bytes 524288 | tf_op jit(solution)/shard_map/all_to_all | solution.py:308
  7.2 0.7 %rev.3 = f32[64]{0:T(128)S(1)} reverse(f32[64]{0:T(128)} %param.3), dimensions={0} | reverse | bytes 512 | tf_op jit(solution)/shard_map/rev | solution.py:18
  7.9 0.1 pad.14.clone
  8.0 0.2 tile.10
  8.3 0.1 reshape.74
  8.4 0.5 %cosine_multiply_fusion = (f32[256,128]{1,0:T(8,128)S(1)}, f32[256,128]{1,0:T(8,128)S(1)}) fusion(s32[128]{0:T(128)S(1)} %iota_add_fusion, f32[256]{0:T(256)S(1)} %get-tuple-element.11, f32[256]{0:T(256)S(1)} %get-tuple-element.12), kind=kLoop, calls=%fused_computation.30 | loop fusion | flops 524288 | bytes 264704 | tf_op jit(solution)/shard_map/mul | solution.py:51
  9.0 4.9 %all-to-all-done = bf16[8,64,256]{2,1,0:T(8,128)(2,1)S(1)} async-done(((bf16[8,64,256]{2,1,0:T(8,128)(2,1)}), bf16[8,64,256]{2,1,0:T(8,128)(2,1)S(1)}, u32[]{:S(2)}, u32[]{:S(2)}) %all-to-all-start) | async-done | bytes 262176 | tf_op jit(solution)/shard_map/all_to_all | solution.py:308
  13.9 0.1 bitcast_convert_fusion
  14.0 0.3 maximum_maximum_fusion
  14.3 0.7 %fusion = bf16[2,128,256]{2,1,0:T(8,128)(2,1)S(1)} fusion(f32[2,64,256]{2,1,0:T(8,128)S(1)} %slice.37, f32[2,256,256]{2,1,0:T(8,128)S(1)} %bitcast.24, f32[128,320]{1,0:T(8,128)S(1)} %reshape.74), kind=kOutput, calls=%fused_computation.2 | convolution fusion | flops 251887616 | bytes 950272 | tf_op jit(solution)/shard_map/tw,bwc->btc/dot_general | solution.py:40
  15.0 0.4 %convolution_bitcast_fusion = f32[1,256,256]{2,1,0:T(8,128)S(1)} fusion(f32[256,128]{1,0:T(8,128)S(1)} %get-tuple-element.10, f32[256,128]{1,0:T(8,128)S(1)} %get-tuple-element.9, bf16[1,128,256]{2,1,0:T(8,128)(2,1)S(1)} %get-tuple-element.8, bf16[1,128,256]{2,1,0:T(8,128)(2,1)S(1)} %get-tuple-element.7), kind=kOutput, calls=%fused_computation | convolution fusion | flops 201654272 | bytes 655360 | tf_op jit(solution)/shard_map/nf,snc->sfc/dot_general | solution.py:59
  15.4 0.1 multiply_convert_fusion.1
  15.5 0.2 fusion.17
  15.7 1.3 %collective-permute-start = (bf16[256,128]{1,0:T(8,128)(2,1)S(1)}, bf16[256,128]{1,0:T(8,128)(2,1)S(1)}, u32[]{:S(2)}, u32[]{:S(2)}) collective-permute-start(bf16[256,128]{1,0:T(8,128)(2,1)S(1)} %fusion.17), channel_id=1, source_target_pairs={{1,24},{5,28},{2,25},{6,29},{3,26},{7,30}} | collective-permute-start | bytes 196616 | tf_op jit(solution)/shard_map/ppermute | solution.py:326
  17.0 0.7 %pad_maximum_fusion.win_ref = bf16[256,256]{1,0:T(8,128)(2,1)} fusion(bf16[128,256]{1,0:T(8,128)(2,1)S(1)} %bitcast.27, bf16[128,256]{1,0:T(8,128)(2,1)S(1)} %bitcast.26), kind=kLoop, calls=%fused_computation.22 | loop fusion | flops 262144 | bytes 262144 | tf_op jit(solution)/shard_map/concatenate | solution.py:70
  17.6 6.8 %collective-permute-done.next_hbm = bf16[256,128]{1,0:T(8,128)(2,1)S(1)} collective-permute-done((bf16[256,128]{1,0:T(8,128)(2,1)S(1)}, bf16[256,128]{1,0:T(8,128)(2,1)S(1)}, u32[]{:S(2)}, u32[]{:S(2)}) %collective-permute-start) | collective-permute-done | bytes 65568 | tf_op jit(solution)/shard_map/ppermute | solution.py:326
  24.4 0.0 copy-start
  24.4 0.6 %copy-done = bf16[256,128]{1,0:T(8,128)(2,1)} copy-done((bf16[256,128]{1,0:T(8,128)(2,1)}, bf16[256,128]{1,0:T(8,128)(2,1)S(1)}, u32[]{:S(2)}) %copy-start) | copy-done | bytes 65560
  25.0 4.4 %shard_map.29 = bf16[64,128,256]{2,1,0:T(8,128)(2,1)} custom-call(s32[1]{0:T(128)} %bitcast.pos_ref, bf16[256,256]{1,0:T(8,128)(2,1)} %pad_maximum_fusion.win_ref, bf16[256,128]{1,0:T(8,128)(2,1)} %copy-done), custom_call_target="tpu_custom_call" | custom-call | flops 6291456 | bytes 4390912 | tf_op jit(solution)/shard_map/pallas_call | solution.py:233
  (13 shorter events, 0.2 us)
Async XLA Ops:
  1.7 12.2 %all-to-all-start = ((bf16[8,64,256]{2,1,0:T(8,128)(2,1)}), bf16[8,64,256]{2,1,0:T(8,128)(2,1)S(1)}, u32[]{:S(2)}, u32[]{:S(2)}) async-start(bf16[8,64,256]{2,1,0:T(8,128)(2,1)} %shard_map.28), calls=%async_computation | async-start | bytes 524288 | tf_op jit(solution)/shard_map/all_to_all | solution.py:308
  15.7 8.7 %collective-permute-start = (bf16[256,128]{1,0:T(8,128)(2,1)S(1)}, bf16[256,128]{1,0:T(8,128)(2,1)S(1)}, u32[]{:S(2)}, u32[]{:S(2)}) collective-permute-start(bf16[256,128]{1,0:T(8,128)(2,1)S(1)} %fusion.17), channel_id=1, source_target_pairs={{1,24},{5,28},{2,25},{6,29},{3,26},{7,30}} | collective-permute-start | bytes 196616 | tf_op jit(solution)/shard_map/ppermute | solution.py:326
  24.4 0.6 %copy-start = (bf16[256,128]{1,0:T(8,128)(2,1)}, bf16[256,128]{1,0:T(8,128)(2,1)S(1)}, u32[]{:S(2)}) copy-start(bf16[256,128]{1,0:T(8,128)(2,1)S(1)} %collective-permute-done.next_hbm) | copy-start | bytes 196612

commit v6 on v5

--- a/solution.py
+++ b/solution.py
@@ -76,9 +76,12 @@
     x = x_ref[...].astype(jnp.float32)
     slab = x.shape[0]
     step = (x.shape[1] + before + after - width) // (out_ref.shape[0] - 1)
-    padded = jnp.concatenate(
-        [jnp.zeros((slab, before), jnp.float32), x, jnp.zeros((slab, after), jnp.float32)], axis=1
-    )
+    parts = [x]
+    if before:
+        parts.insert(0, jnp.zeros((slab, before), jnp.float32))
+    if after:
+        parts.append(jnp.zeros((slab, after), jnp.float32))
+    padded = jnp.concatenate(parts, axis=1) if len(parts) > 1 else x
     for j in range(out_ref.shape[0]):
         out_ref[j] = padded[:, j * step : j * step + width].astype(out_ref.dtype)
 
@@ -92,6 +95,96 @@
             flops=0, transcendentals=0, bytes_accessed=2 * (slab * rows + extent * slab * width)
         ),
     )(turned)
+
+
+def xor_order(chunks, position, extent):
+    bit = 1
+    while bit < extent:
+        shape = chunks.shape
+        swapped = chunks.reshape((extent // (2 * bit), 2, bit) + shape[1:])[:, ::-1].reshape(shape)
+        chunks = jnp.where((position & bit) != 0, swapped, chunks)
+        bit *= 2
+    return chunks
+
+
+def exchange_time(windows, position, extent):
+    if extent & (extent - 1) or extent > 16:
+        return lax.all_to_all(windows, "ta", split_axis=0, concat_axis=0, tiled=True)
+    chunks = xor_order(windows, position, extent)
+    bit = 1
+    while bit < extent:
+        shape = chunks.shape
+        view = chunks.reshape((extent // (2 * bit), 2, bit) + shape[1:])
+        route = [(i, i ^ bit) for i in range(extent)]
+        arrived = lax.ppermute(view[:, 1], "ta", route)
+        chunks = jnp.stack([view[:, 0], arrived], axis=1).reshape(shape)
+        bit *= 2
+    return xor_order(chunks, position, extent)
+
+
+def cross_kernel(segments, rows_per_step, own_ref, ext_ref, out_ref):
+    step = pl.program_id(0)
+    base = pl.multiple_of(step * rows_per_step, rows_per_step)
+    for i in range(rows_per_step):
+        acc_re = None
+        acc_im = None
+        for s in range(segments):
+            a = own_ref[pl.ds(base, rows_per_step), pl.ds(s * NFFT, NFFT)]
+            a = a.astype(jnp.float32)[i : i + 1]
+            window = ext_ref[pl.ds(base, LAGS + rows_per_step), pl.ds(s * NFFT, NFFT)]
+            b = window.astype(jnp.float32)[i : i + LAGS]
+            terms = product_terms(a, b)
+            if acc_re is None:
+                acc_re, acc_im = terms
+            else:
+                acc_re = [x + y for x, y in zip(acc_re, terms[0])]
+                acc_im = [x + y for x, y in zip(acc_im, terms[1])]
+        store_row(out_ref, i, acc_re, acc_im, segments)
+
+
+def product_terms(a, b):
+    ar = a[:, :NF]
+    ai = a[:, NF:]
+    br = b[:, :NF]
+    bi = b[:, NF:]
+    return [ar * br, ai * bi], [ai * br, ar * bi]
+
+
+def store_row(out_ref, i, acc_re, acc_im, segments):
+    re = acc_re[0] + acc_re[1]
+    im = acc_im[0] - acc_im[1]
+    if segments > 1:
+        re = re / segments
+        im = im / segments
+    out_ref[i, :, :NF] = re.astype(out_ref.dtype)
+    out_ref[i, :, NF:] = im.astype(out_ref.dtype)
+
+
+def cross_kernel_shifted(segments, rows_per_step, own_ref, ext_ref, out_ref, own_f32, shifted):
+    step = pl.program_id(0)
+    span = shifted.shape[1]
+
+    @pl.when(step == 0)
+    def _():
+        own_f32[...] = own_ref[...].astype(jnp.float32)
+        whole = ext_ref[...].astype(jnp.float32)
+        for i in range(rows_per_step):
+            shifted[i] = whole[i : i + span]
+
+    base = pl.multiple_of(step * rows_per_step, rows_per_step)
+    for i in range(rows_per_step):
+        acc_re = None
+        acc_im = None
+        for s in range(segments):
+            a = own_f32[pl.ds(base + i, 1), pl.ds(s * NFFT, NFFT)]
+            b = shifted[i, pl.ds(base, LAGS), pl.ds(s * NFFT, NFFT)]
+            terms = product_terms(a, b)
+            if acc_re is None:
+                acc_re, acc_im = terms
+            else:
+                acc_re = [x + y for x, y in zip(acc_re, terms[0])]
+                acc_im = [x + y for x, y in zip(acc_im, terms[1])]
+        store_row(out_ref, i, acc_re, acc_im, segments)
 
 
 def cross_kernel(segments, rows_per_step, own_ref, ext_ref, out_ref):
@@ -255,6 +348,84 @@
     )(position.reshape(1).astype(jnp.int32), whitened_t, following_t)
 
 
+def cross_kernel_pieces(segments, rows, chunk, *refs):
+    pieces = refs[:-5]
+    out_hbm, own_f32, shifted, buffers, sems = refs[-5:]
+    span = shifted.shape[1]
+    extended = jnp.concatenate(
+        [
+            jnp.concatenate(
+                [piece[s * NFFT : (s + 1) * NFFT, :].astype(jnp.float32).T for s in range(segments)],
+                axis=1,
+            )
+            for piece in pieces
+        ],
+        axis=0,
+    )
+    own_f32[...] = extended[:rows]
+    for i in range(chunk):
+        shifted[i] = extended[i : i + span]
+    slots, parts = buffers.shape[0], sems.shape[1]
+    part = chunk // parts
+    copies = []
+    for m in range(rows // chunk):
+        slot = m % slots
+        if m >= slots:
+            for copy in copies[m - slots]:
+                copy.wait()
+        base = m * chunk
+        for i in range(chunk):
+            acc_re = None
+            acc_im = None
+            for s in range(segments):
+                a = own_f32[base + i : base + i + 1, s * NFFT : (s + 1) * NFFT]
+                b = shifted[i, base : base + LAGS, s * NFFT : (s + 1) * NFFT]
+                terms = product_terms(a, b)
+                if acc_re is None:
+                    acc_re, acc_im = terms
+                else:
+                    acc_re = [x + y for x, y in zip(acc_re, terms[0])]
+                    acc_im = [x + y for x, y in zip(acc_im, terms[1])]
+            store_row(buffers.at[slot], i, acc_re, acc_im, segments)
+        group = []
+        for p in range(parts):
+            copy = pltpu.make_async_copy(
+                buffers.at[slot, pl.ds(p * part, part)],
+                out_hbm.at[pl.ds(base + p * part, part)],
+                sems.at[slot, p],
+            )
+            copy.start()
+            group.append(copy)
+        copies.append(group)
+    for group in copies[-slots:]:
+        for copy in group:
+            copy.wait()
+
+
+def cross_spectra_pieces(pieces):
+    width, rows = pieces[0].shape
+    segments = width // NFFT
+    chunk = 8
+    span = len(pieces) * rows - chunk
+    return pl.pallas_call(
+        functools.partial(cross_kernel_pieces, segments, rows, chunk),
+        out_shape=jax.ShapeDtypeStruct((rows, LAGS, NFFT), jnp.bfloat16),
+        in_specs=[pl.BlockSpec(memory_space=pltpu.VMEM)] * len(pieces),
+        out_specs=pl.BlockSpec(memory_space=pl.ANY),
+        scratch_shapes=[
+            pltpu.VMEM((rows, width), jnp.float32),
+            pltpu.VMEM((chunk, span, width), jnp.float32),
+            pltpu.VMEM((4, chunk, LAGS, NFFT), jnp.bfloat16),
+            pltpu.SemaphoreType.DMA((4, 4)),
+        ],
+        cost_estimate=pl.CostEstimate(
+            flops=6 * rows * LAGS * NF * segments,
+            transcendentals=0,
+            bytes_accessed=rows * LAGS * NFFT * 2 + 2 * len(pieces) * rows * width,
+        ),
+    )(*pieces)
+
+
 def cross_spectra(own, extended):
     rows, segments, columns = own.shape
     reach_rows = extended.shape[0]
@@ -300,46 +471,26 @@
     section_rows, slab = strain.shape
     block_rows = section_rows // extent
     reach = LAGS // block_rows
-    window = 2 * reach
-    before = (reach - 1) * block_rows
-    windows = channel_windows(
-        strain.T, extent, before, reach * block_rows, window * block_rows
-    )
-    gathered = lax.all_to_all(windows, "ta", split_axis=0, concat_axis=0, tiled=True)
-    samples = gathered.reshape(extent * slab, window * block_rows)
+    chunks = channel_windows(strain.T, extent, 0, 0, block_rows)
+    gathered = exchange_time(chunks, position, extent)
+    samples = gathered.reshape(extent * slab, block_rows)
     filtered = decimate_t(samples.astype(jnp.float32), filter_taps)
     whitened_t = whiten_t(filtered)
-    segments, columns, window_rows = whitened_t.shape
-    first_of_section = reach - 1 - jnp.minimum(position, reach - 1)
-
-    def linear(ta_index, col_index):
-        return ta_index * columns_n + col_index
-
-    route = [
-        (linear(m, c + 1), linear(extent - reach + m, c))
-        for c in range(columns_n - 1)
-        for m in range(reach)
-    ]
+    segments, columns, _ = whitened_t.shape
+    flat = whitened_t.reshape(segments * columns, block_rows)
+    total = columns_n * extent
+
+    def linear(block):
+        return (block % extent) * columns_n + block // extent
+
+    pieces = [flat]
+    for offset in range(1, reach + 1):
+        route = [(linear(b + offset), linear(b)) for b in range(total) if b + offset < total]
+        pieces.append(lax.ppermute(flat, ("ta", "col"), route))
     if segments * 8 * (reach + 1) * block_rows * columns * 4 <= 8 * 1024 * 1024:
-        flat = whitened_t.reshape(segments * columns, window_rows)
-        payload = lax.dynamic_slice_in_dim(flat, first_of_section * block_rows, reach * block_rows, 1)
-        next_section = lax.ppermute(payload, ("ta", "col"), route)
-        return cross_spectra_direct(
-            flat, next_section, position, block_rows, reach, extent, before
-        )[None]
-    whitened = whitened_t.transpose(2, 0, 1)
-    payload = lax.dynamic_slice_in_dim(whitened, first_of_section * block_rows, reach * block_rows, 0)
-    next_section = lax.ppermute(payload, ("ta", "col"), route)
-    local = whitened[before : before + (reach + 1) * block_rows]
-    extended = local
-    for j in range(extent - reach, extent):
-        kept = (extent - j) * block_rows
-        candidate = jnp.concatenate(
-            [local[:kept], next_section[: (reach + 1) * block_rows - kept]], axis=0
-        )
-        extended = jnp.where(position == j, candidate, extended)
-    own = local[:block_rows]
-    return cross_spectra(own, extended)[None]
+        return cross_spectra_pieces(pieces)[None]
+    extended = jnp.concatenate(pieces, axis=1).reshape(segments, columns, -1).transpose(2, 0, 1)
+    return cross_spectra(extended[:block_rows], extended)[None]
 
 
 def solution(mesh):

time: 29.7 us -> 37.8 us (1.27)
  the two profiles are of different devices: /device:TPU:29 before, /device:TPU:1 now
where the time goes in v6:
time: 37.8 us; the launch traced here: 37.5 us
  starting transfers between devices  17.2 us (46%)
  waiting for transfers between devices  7.02 us (19%)
  Pallas kernels  5.22 us (14%)
  local copies, waits for them, and re-layouts  4.59 us (12%)
  other arithmetic  2.36 us (6%)
  matrix products  0.79 us (2%)
    ppermute x2, starting transfers between devices, body(): pieces.append(lax.ppermute(flat, ('ta', 'col'), route))  11.8 us
    ppermute x3, starting transfers between devices, exchange_time(): arrived = lax.ppermute(view[:, 1], 'ta', route)  5.49 us
    ppermute x3, waiting for transfers between devices, exchange_time(): arrived = lax.ppermute(view[:, 1], 'ta', route)  4.03 us
    pallas_call x1, Pallas kernels, cross_spectra_pieces(): pl.pallas_call(functools.partial(cross_kernel_pieces, segments, rows, chu...  3.62 us
    ppermute x2, waiting for transfers between devices, body(): pieces.append(lax.ppermute(flat, ('ta', 'col'), route))  3 us
    rev x6, local copies, waits for them, and re-layouts, xor_order(): chunks.reshape((extent // (2 * bit), 2, bit) + shape[1:])[:, ::-1]  1.74 us
    pallas_call x1, Pallas kernels, channel_windows(): pl.pallas_call(functools.partial(windows_kernel, before, after, width), o...  1.59 us
    select_n x5, other arithmetic, xor_order(): chunks = jnp.where(position & bit != 0, swapped, chunks)  1.38 us
  transfers between devices with their start and end apart: 5, of which 3 were waited for; matrix products, arithmetic and copies ran while one was open for 5% of the time, Pallas kernels for 0%

profile of v6, /device:TPU:1, one launch (start us, length us, event | category | flops | bytes accessed | tf_op | source)
XLA Modules:
  0.0 37.5 jit_solution(16462638267330644366)
XLA Ops:
  0.0 1.6 %shard_map.28 = bf16[8,64,64]{2,1,0:T(8,128)(2,1)} custom-call(bf16[64,512]{1,0:T(8,128)(2,1)} %bitcast.83), custom_call_target="tpu_custom_call" | custom-call | bytes 131072 | tf_op jit(solution)/shard_map/pallas_call | solution.py:91
  1.6 0.9 %rev.21 = bf16[4,2,1,64,64]{4,3,1,0,2:T(8,128)(2,1)S(1)} reverse(bf16[4,2,1,64,64]{4,3,1,0,2:T(8,128)(2,1)} %bitcast.71), dimensions={1} | reverse | bytes 131072 | tf_op jit(solution)/shard_map/rev | solution.py:104
  2.5 0.9 %bitcast_select_fusion.2 = bf16[8,64,64]{2,1,0:T(8,128)(2,1)S(1)} fusion(bf16[8,64,64]{2,1,0:T(8,128)(2,1)} %shard_map.28, bf16[4,2,1,64,64]{4,3,1,0,2:T(8,128)(2,1)S(1)} %rev.21, pred[]{:T(512)S(6)} %ne.24), kind=kLoop, calls=%fused_computation.26 | loop fusion | flops 32768 | bytes 196609 | tf_op jit(solution)/shard_map/jit(_where)/select_n | solution.py:105
  3.6 1.2 %collective-permute-start = (bf16[4,1,64,64]{3,2,0,1:T(8,128)(2,1)S(1)}, bf16[4,1,64,64]{3,2,0,1:T(8,128)(2,1)S(1)}, u32[]{:S(2)}, u32[]{:S(2)}) collective-permute-start(bf16[4,1,64,64]{3,2,0,1:T(8,128)(2,1)S(1)} %get-tuple-element.13), channel_id=1, source_target_pairs={{0,4},{4,0},{8,12},{12,8},{16,20},{20,16},{24,28},{28,24},{1,5},{5... | collective-permute-start | bytes 98312 | tf_op jit(solution)/shard_map/ppermute | solution.py:119
  4.9 2.4 %collective-permute-done = bf16[4,1,64,64]{3,2,0,1:T(8,128)(2,1)S(1)} collective-permute-done((bf16[4,1,64,64]{3,2,0,1:T(8,128)(2,1)S(1)}, bf16[4,1,64,64]{3,2,0,1:T(8,128)(2,1)S(1)}, u32[]{:S(2)}, u32[]{:S(2)}) %collective-permute-start) | collective-permute-done | bytes 32800 | tf_op jit(solution)/shard_map/ppermute | solution.py:119
  7.3 1.7 %collective-permute-start.1 = (bf16[2,2,64,64]{3,2,0,1:T(8,128)(2,1)S(1)}, bf16[2,2,64,64]{3,2,0,1:T(8,128)(2,1)S(1)}, u32[]{:S(2)}, u32[]{:S(2)}) collective-permute-start(bf16[2,2,64,64]{3,2,0,1:T(8,128)(2,1)S(1)} %get-tuple-element.11), channel_id=1, source_target_pairs={{0,8},{4,12},{8,0},{12,4},{16,24},{20,28},{24,16},{28,20},{1,9},{5... | collective-permute-start | bytes 98312 | tf_op jit(solution)/shard_map/ppermute | solution.py:119
  9.0 1.7 %collective-permute-done.1 = bf16[2,2,64,64]{3,2,0,1:T(8,128)(2,1)S(1)} collective-permute-done((bf16[2,2,64,64]{3,2,0,1:T(8,128)(2,1)S(1)}, bf16[2,2,64,64]{3,2,0,1:T(8,128)(2,1)S(1)}, u32[]{:S(2)}, u32[]{:S(2)}) %collective-permute-start.1) | collective-permute-done | bytes 32800 | tf_op jit(solution)/shard_map/ppermute | solution.py:119
  10.7 0.1 copy.7
  10.8 0.1 fusion.26
  10.9 2.5 %collective-permute-start.2 = (bf16[1,4,64,64]{2,1,3,0:T(4,128)(2,1)S(1)}, bf16[1,4,64,64]{2,1,3,0:T(4,128)(2,1)S(1)}, u32[]{:S(2)}, u32[]{:S(2)}) collective-permute-start(bf16[1,4,64,64]{2,1,3,0:T(4,128)(2,1)S(1)} %get-tuple-element.9), channel_id=1, source_target_pairs={{0,16},{4,20},{8,24},{12,28},{16,0},{20,4},{24,8},{28,12},{1,17},{... | collective-permute-start | bytes 98312 | tf_op jit(solution)/shard_map/ppermute | solution.py:119
  13.4 0.5 %cosine_multiply_fusion = (f32[256,128]{1,0:T(8,128)S(1)}, f32[256,128]{1,0:T(8,128)S(1)}) fusion(s32[128]{0:T(128)S(1)} %iota_add_fusion, f32[256]{0:T(256)S(1)} %get-tuple-element.18, f32[256]{0:T(256)S(1)} %get-tuple-element.19), kind=kLoop, calls=%fused_computation.28 | loop fusion | flops 524288 | bytes 264704 | tf_op jit(solution)/shard_map/mul | solution.py:51
  13.9 0.7 %rev.27 = f32[64]{0:T(128)S(1)} reverse(f32[64]{0:T(128)} %param.3), dimensions={0} | reverse | bytes 512 | tf_op jit(solution)/shard_map/rev | solution.py:18
  14.7 0.1 pad.12.clone
  14.8 0.2 tile.10
  15.1 0.1 reshape.154
  15.2 0.0 collective-permute-done.2
  15.2 0.1 pad_maximum_fusion.1
  15.3 0.1 reshape.152
  15.4 0.7 %rev.24 = bf16[4,2,1,64,64]{3,1,0,4,2:T(2,128)(2,1)S(1)} reverse(bf16[4,2,1,64,64]{3,1,0,4,2:T(2,128)(2,1)S(1)} %bitcast.72), dimensions={1} | reverse | bytes 131072 | tf_op jit(solution)/shard_map/rev | solution.py:104
  16.1 0.1 reshape.151
  16.3 0.2 broadcast_select_fusion
  16.5 0.1 rev.25
  16.6 0.1 reshape.150
  16.7 0.2 select_select_fusion
  17.0 0.1 reshape.149
  17.1 0.1 pad_slice_fusion
  17.3 0.1 maximum_maximum_fusion
  17.4 0.1 reshape.153
  17.5 0.4 %fusion = bf16[2,128,64]{1,2,0:T(8,128)(2,1)S(1)} fusion(f32[2,64,64]{1,2,0:T(8,128)S(1)} %copy.19, f32[2,256,64]{1,2,0:T(8,128)S(1)} %bitcast.77, f32[128,320]{1,0:T(8,128)S(1)} %reshape.154), kind=kOutput, calls=%fused_computation.2 | convolution fusion | flops 62971904 | bytes 360448 | tf_op jit(solution)/shard_map/tw,bwc->btc/dot_general | solution.py:40
  18.0 0.4 %convolution_bitcast_fusion = f32[1,256,64]{2,1,0:T(8,128)S(1)} fusion(f32[256,128]{1,0:T(8,128)S(1)} %get-tuple-element.17, f32[256,128]{1,0:T(8,128)S(1)} %get-tuple-element.16, bf16[1,128,64]{1,2,0:T(8,128)(2,1)S(1)} %get-tuple-element.15, bf16[1,128,64]{1,2,0:T(8,128)(2,1)S(1)} %get-tuple-element.14), kind=kOutput, calls=%fused_computation | convolution fusion | flops 50462720 | bytes 360448 | tf_op jit(solution)/shard_map/nf,snc->sfc/dot_general | solution.py:59
  18.5 0.0 copy-start
  18.5 9.8 %collective-permute-start.4 = (bf16[256,64]{1,0:T(8,128)(2,1)S(1)}, bf16[256,64]{1,0:T(8,128)(2,1)S(1)}, u32[]{:S(2)}, u32[]{:S(2)}) collective-permute-start(bf16[256,64]{1,0:T(8,128)(2,1)S(1)} %pad_maximum_fusion.3.refs_0_), channel_id=1, source_target_pairs={{8,0},{12,4},{16,8},{20,12},{24,16},{28,20},{1,24},{5,28},{9,1},{1... | collective-permute-start | bytes 98312 | tf_op jit(solution)/shard_map/ppermute | solution.py:489
  28.2 2.0 %collective-permute-start.3 = (bf16[256,64]{1,0:T(8,128)(2,1)S(1)}, bf16[256,64]{1,0:T(8,128)(2,1)S(1)}, u32[]{:S(2)}, u32[]{:S(2)}) collective-permute-start(bf16[256,64]{1,0:T(8,128)(2,1)S(1)} %pad_maximum_fusion.3.refs_0_), channel_id=1, source_target_pairs={{4,0},{8,4},{12,8},{16,12},{20,16},{24,20},{28,24},{1,28},{5,1},{9... | collective-permute-start | bytes 98312 | tf_op jit(solution)/shard_map/ppermute | solution.py:489
  30.2 0.0 collective-permute-done.4.refs_2_
  30.2 0.0 copy-start.1
  30.3 3.0 %collective-permute-done.3.refs_1_ = bf16[256,64]{1,0:T(8,128)(2,1)S(1)} collective-permute-done((bf16[256,64]{1,0:T(8,128)(2,1)S(1)}, bf16[256,64]{1,0:T(8,128)(2,1)S(1)}, u32[]{:S(2)}, u32[]{:S(2)}) %collective-permute-start.3) | collective-permute-done | bytes 32800 | tf_op jit(solution)/shard_map/ppermute | solution.py:489
  33.3 0.0 copy-done
  33.3 0.0 copy-done.1
  33.3 0.0 copy-start.2
  33.3 0.6 %copy-done.2 = bf16[256,64]{1,0:T(8,128)(2,1)} copy-done((bf16[256,64]{1,0:T(8,128)(2,1)}, bf16[256,64]{1,0:T(8,128)(2,1)S(1)}, u32[]{:S(2)}) %copy-start.2) | copy-done | bytes 32792
  33.9 3.6 %shard_map.29 = bf16[64,128,256]{2,1,0:T(8,128)(2,1)} custom-call(bf16[256,64]{1,0:T(8,128)(2,1)} %copy-done, bf16[256,64]{1,0:T(8,128)(2,1)} %copy-done.2, bf16[256,64]{1,0:T(8,128)(2,1)} %copy-done.1), custom_call_target="tpu_custom_call" | custom-call | flops 6291456 | bytes 4292608 | tf_op jit(solution)/shard_map/pallas_call | solution.py:410
  (25 shorter events, 0.4 us)
Async XLA Ops:
  3.6 3.7 %collective-permute-start = (bf16[4,1,64,64]{3,2,0,1:T(8,128)(2,1)S(1)}, bf16[4,1,64,64]{3,2,0,1:T(8,128)(2,1)S(1)}, u32[]{:S(2)}, u32[]{:S(2)}) collective-permute-start(bf16[4,1,64,64]{3,2,0,1:T(8,128)(2,1)S(1)} %get-tuple-element.13), channel_id=1, source_target_pairs={{0,4},{4,0},{8,12},{12,8},{16,20},{20,16},{24,28},{28,24},{1,5},{5... | collective-permute-start | bytes 98312 | tf_op jit(solution)/shard_map/ppermute | solution.py:119
  7.3 3.4 %collective-permute-start.1 = (bf16[2,2,64,64]{3,2,0,1:T(8,128)(2,1)S(1)}, bf16[2,2,64,64]{3,2,0,1:T(8,128)(2,1)S(1)}, u32[]{:S(2)}, u32[]{:S(2)}) collective-permute-start(bf16[2,2,64,64]{3,2,0,1:T(8,128)(2,1)S(1)} %get-tuple-element.11), channel_id=1, source_target_pairs={{0,8},{4,12},{8,0},{12,4},{16,24},{20,28},{24,16},{28,20},{1,9},{5... | collective-permute-start | bytes 98312 | tf_op jit(solution)/shard_map/ppermute | solution.py:119
  10.9 4.3 %collective-permute-start.2 = (bf16[1,4,64,64]{2,1,3,0:T(4,128)(2,1)S(1)}, bf16[1,4,64,64]{2,1,3,0:T(4,128)(2,1)S(1)}, u32[]{:S(2)}, u32[]{:S(2)}) collective-permute-start(bf16[1,4,64,64]{2,1,3,0:T(4,128)(2,1)S(1)} %get-tuple-element.9), channel_id=1, source_target_pairs={{0,16},{4,20},{8,24},{12,28},{16,0},{20,4},{24,8},{28,12},{1,17},{... | collective-permute-start | bytes 98312 | tf_op jit(solution)/shard_map/ppermute | solution.py:119
  18.5 14.8 %copy-start = (bf16[256,64]{1,0:T(8,128)(2,1)}, bf16[256,64]{1,0:T(8,128)(2,1)S(1)}, u32[]{:S(2)}) copy-start(bf16[256,64]{1,0:T(8,128)(2,1)S(1)} %pad_maximum_fusion.3.refs_0_) | copy-start | bytes 98308
  18.5 11.8 %collective-permute-start.4 = (bf16[256,64]{1,0:T(8,128)(2,1)S(1)}, bf16[256,64]{1,0:T(8,128)(2,1)S(1)}, u32[]{:S(2)}, u32[]{:S(2)}) collective-permute-start(bf16[256,64]{1,0:T(8,128)(2,1)S(1)} %pad_maximum_fusion.3.refs_0_), channel_id=1, source_target_pairs={{8,0},{12,4},{16,8},{20,12},{24,16},{28,20},{1,24},{5,28},{9,1},{1... | collective-permute-start | bytes 98312 | tf_op jit(solution)/shard_map/ppermute | solution.py:489
  28.2 5.0 %collective-permute-start.3 = (bf16[256,64]{1,0:T(8,128)(2,1)S(1)}, bf16[256,64]{1,0:T(8,128)(2,1)S(1)}, u32[]{:S(2)}, u32[]{:S(2)}) collective-permute-start(bf16[256,64]{1,0:T(8,128)(2,1)S(1)} %pad_maximum_fusion.3.refs_0_), channel_id=1, source_target_pairs={{4,0},{8,4},{12,8},{16,12},{20,16},{24,20},{28,24},{1,28},{5,1},{9... | collective-permute-start | bytes 98312 | tf_op jit(solution)/shard_map/ppermute | solution.py:489
  30.2 3.0 %copy-start.1 = (bf16[256,64]{1,0:T(8,128)(2,1)}, bf16[256,64]{1,0:T(8,128)(2,1)S(1)}, u32[]{:S(2)}) copy-start(bf16[256,64]{1,0:T(8,128)(2,1)S(1)} %collective-permute-done.4.refs_2_) | copy-start | bytes 98308
  33.3 0.6 %copy-start.2 = (bf16[256,64]{1,0:T(8,128)(2,1)}, bf16[256,64]{1,0:T(8,128)(2,1)S(1)}, u32[]{:S(2)}) copy-start(bf16[256,64]{1,0:T(8,128)(2,1)S(1)} %collective-permute-done.3.refs_1_) | copy-start | bytes 98308

commit v7 on v5

--- a/solution.py
+++ b/solution.py
@@ -72,26 +72,26 @@
     )
 
 
-def windows_kernel(before, after, width, x_ref, out_ref):
-    x = x_ref[...].astype(jnp.float32)
-    slab = x.shape[0]
-    step = (x.shape[1] + before + after - width) // (out_ref.shape[0] - 1)
+def windows_kernel(width, x_ref, tail_ref, out_ref):
     padded = jnp.concatenate(
-        [jnp.zeros((slab, before), jnp.float32), x, jnp.zeros((slab, after), jnp.float32)], axis=1
-    )
+        [x_ref[...].astype(jnp.float32), tail_ref[...].astype(jnp.float32)], axis=1
+    )
+    step = (padded.shape[1] - width) // (out_ref.shape[0] - 1)
     for j in range(out_ref.shape[0]):
         out_ref[j] = padded[:, j * step : j * step + width].astype(out_ref.dtype)
 
 
-def channel_windows(turned, extent, before, after, width):
+def channel_windows(turned, tail, extent, width):
     slab, rows = turned.shape
     return pl.pallas_call(
-        functools.partial(windows_kernel, before, after, width),
+        functools.partial(windows_kernel, width),
         out_shape=jax.ShapeDtypeStruct((extent, slab, width), turned.dtype),
         cost_estimate=pl.CostEstimate(
-            flops=0, transcendentals=0, bytes_accessed=2 * (slab * rows + extent * slab * width)
+            flops=0,
+            transcendentals=0,
+            bytes_accessed=2 * (slab * (rows + tail.shape[1]) + extent * slab * width),
         ),
-    )(turned)
+    )(turned, tail)
 
 
 def cross_kernel(segments, rows_per_step, own_ref, ext_ref, out_ref):
@@ -159,32 +159,21 @@
         store_row(out_ref, i, acc_re, acc_im, segments)
 
 
-def cross_kernel_direct(segments, rows, reach, extent, before, chunk,
-                        pos_ref, win_ref, next_hbm, out_hbm, own_f32, shifted, following,
-                        buffers, sems, next_sem):
-    fetch = pltpu.make_async_copy(next_hbm, following, next_sem)
-    fetch.start()
+def cross_kernel_pieces(segments, rows, chunk, *refs):
+    pieces = refs[:-5]
+    out_hbm, own_f32, shifted, buffers, sems = refs[-5:]
     span = shifted.shape[1]
-    position = pos_ref[0]
-    width = (reach + 1) * rows
-    local = jnp.concatenate(
+    extended = jnp.concatenate(
         [
-            win_ref[s * NFFT : (s + 1) * NFFT, before : before + width].astype(jnp.float32).T
-            for s in range(segments)
+            jnp.concatenate(
+                [piece[s * NFFT : (s + 1) * NFFT, :].astype(jnp.float32).T for s in range(segments)],
+                axis=1,
+            )
+            for piece in pieces
         ],
-        axis=1,
-    )
-    own_f32[...] = local[:rows]
-    fetch.wait()
-    arrived = jnp.concatenate(
-        [following[s * NFFT : (s + 1) * NFFT, :].astype(jnp.float32).T for s in range(segments)],
-        axis=1,
-    )
-    extended = local
-    for j in range(extent - reach, extent):
-        kept = (extent - j) * rows
-        candidate = jnp.concatenate([local[:kept], arrived[: width - kept]], axis=0)
-        extended = jnp.where(position == j, candidate, extended)
+        axis=0,
+    )
+    own_f32[...] = extended[:rows]
     for i in range(chunk):
         shifted[i] = extended[i : i + span]
     slots, parts = buffers.shape[0], sems.shape[1]
@@ -224,35 +213,29 @@
             copy.wait()
 
 
-def cross_spectra_direct(whitened_t, following_t, position, rows, reach, extent, before):
-    width, window_rows = whitened_t.shape
+def cross_spectra_pieces(pieces):
+    width = pieces[0].shape[0]
+    rows = sum(piece.shape[1] for piece in pieces) - LAGS
     segments = width // NFFT
     chunk = 8
-    reach_rows = (reach + 1) * rows
-    span = reach_rows - chunk
+    span = rows + LAGS - chunk
     return pl.pallas_call(
-        functools.partial(cross_kernel_direct, segments, rows, reach, extent, before, chunk),
+        functools.partial(cross_kernel_pieces, segments, rows, chunk),
         out_shape=jax.ShapeDtypeStruct((rows, LAGS, NFFT), jnp.bfloat16),
-        in_specs=[
-            pl.BlockSpec(memory_space=pltpu.SMEM),
-            pl.BlockSpec(memory_space=pltpu.VMEM),
-            pl.BlockSpec(memory_space=pl.ANY),
-        ],
+        in_specs=[pl.BlockSpec(memory_space=pltpu.VMEM)] * len(pieces),
         out_specs=pl.BlockSpec(memory_space=pl.ANY),
         scratch_shapes=[
             pltpu.VMEM((rows, width), jnp.float32),
             pltpu.VMEM((chunk, span, width), jnp.float32),
-            pltpu.VMEM(following_t.shape, following_t.dtype),
             pltpu.VMEM((4, chunk, LAGS, NFFT), jnp.bfloat16),
             pltpu.SemaphoreType.DMA((4, 4)),
-            pltpu.SemaphoreType.DMA(()),
         ],
         cost_estimate=pl.CostEstimate(
             flops=6 * rows * LAGS * NF * segments,
             transcendentals=0,
-            bytes_accessed=rows * LAGS * NFFT * 2 + 2 * (window_rows + following_t.shape[1]) * width,
+            bytes_accessed=rows * LAGS * NFFT * 2 + 2 * (rows + LAGS) * width,
         ),
-    )(position.reshape(1).astype(jnp.int32), whitened_t, following_t)
+    )(*pieces)
 
 
 def cross_spectra(own, extended):
@@ -296,50 +279,24 @@
 def body(strain, filter_taps):
     extent = lax.axis_size("ta")
     columns_n = lax.axis_size("col")
-    position = lax.axis_index("ta")
     section_rows, slab = strain.shape
     block_rows = section_rows // extent
     reach = LAGS // block_rows
-    window = 2 * reach
-    before = (reach - 1) * block_rows
-    windows = channel_windows(
-        strain.T, extent, before, reach * block_rows, window * block_rows
-    )
+    turned = strain.T
+    route = [(c + 1, c) for c in range(columns_n - 1)]
+    tail = lax.ppermute(turned[:, : reach * block_rows], "col", route)
+    width = (reach + 1) * block_rows
+    windows = channel_windows(turned, tail, extent, width)
     gathered = lax.all_to_all(windows, "ta", split_axis=0, concat_axis=0, tiled=True)
-    samples = gathered.reshape(extent * slab, window * block_rows)
+    samples = gathered.reshape(extent * slab, width)
     filtered = decimate_t(samples.astype(jnp.float32), filter_taps)
     whitened_t = whiten_t(filtered)
-    segments, columns, window_rows = whitened_t.shape
-    first_of_section = reach - 1 - jnp.minimum(position, reach - 1)
-
-    def linear(ta_index, col_index):
-        return ta_index * columns_n + col_index
-
-    route = [
-        (linear(m, c + 1), linear(extent - reach + m, c))
-        for c in range(columns_n - 1)
-        for m in range(reach)
-    ]
-    if segments * 8 * (reach + 1) * block_rows * columns * 4 <= 8 * 1024 * 1024:
-        flat = whitened_t.reshape(segments * columns, window_rows)
-        payload = lax.dynamic_slice_in_dim(flat, first_of_section * block_rows, reach * block_rows, 1)
-        next_section = lax.ppermute(payload, ("ta", "col"), route)
-        return cross_spectra_direct(
-            flat, next_section, position, block_rows, reach, extent, before
-        )[None]
-    whitened = whitened_t.transpose(2, 0, 1)
-    payload = lax.dynamic_slice_in_dim(whitened, first_of_section * block_rows, reach * block_rows, 0)
-    next_section = lax.ppermute(payload, ("ta", "col"), route)
-    local = whitened[before : before + (reach + 1) * block_rows]
-    extended = local
-    for j in range(extent - reach, extent):
-        kept = (extent - j) * block_rows
-        candidate = jnp.concatenate(
-            [local[:kept], next_section[: (reach + 1) * block_rows - kept]], axis=0
-        )
-        extended = jnp.where(position == j, candidate, extended)
-    own = local[:block_rows]
-    return cross_spectra(own, extended)[None]
+    segments, columns, _ = whitened_t.shape
+    if segments * 8 * width * columns * 4 <= 8 * 1024 * 1024:
+        flat = whitened_t.reshape(segments * columns, width)
+        return cross_spectra_pieces([flat])[None]
+    extended = whitened_t.transpose(2, 0, 1)
+    return cross_spectra(extended[:block_rows], extended)[None]
 
 
 def solution(mesh):

time: 29.7 us -> 30 us (1.010)
  the two profiles are of different devices: /device:TPU:29 before, /device:TPU:1 now
where the time goes in v7:
time: 30 us; the launch traced here: 29.6 us
  waiting for transfers between devices  10.7 us (36%)
  starting transfers between devices  7.51 us (25%)
  Pallas kernels  5.29 us (18%)
  local copies, waits for them, and re-layouts  3.32 us (11%)
  other arithmetic  1.6 us (5%)
  matrix products  1.04 us (3%)
    all_to_all x1, waiting for transfers between devices, body(): lax.all_to_all(windows, 'ta', split_axis=0, concat_axis=0, tiled=True)  6.77 us
    all_to_all x1, starting transfers between devices, body(): lax.all_to_all(windows, 'ta', split_axis=0, concat_axis=0, tiled=True)  5.55 us
    ppermute x1, waiting for transfers between devices, body(): tail = lax.ppermute(turned[:, :reach * block_rows], 'col', route)  3.95 us
    pallas_call x1, Pallas kernels, cross_spectra_pieces(): pl.pallas_call(functools.partial(cross_kernel_pieces, segments, rows, chu...  3.64 us
    ppermute x1, starting transfers between devices, body(): tail = lax.ppermute(turned[:, :reach * block_rows], 'col', route)  1.95 us
    pallas_call x1, Pallas kernels, channel_windows(): pl.pallas_call(functools.partial(windows_kernel, width), out_shape=jax.Sh...  1.65 us
    rev x1, local copies, waits for them, and re-layouts, tap_rows(): flipped = filter_taps[::-1]  0.75 us
    slice x1, local copies, waits for them, and re-layouts, body(): tail = lax.ppermute(turned[:, :reach * block_rows], 'col', route)  0.72 us
  transfers between devices with their start and end apart: 2, of which 2 were waited for; matrix products, arithmetic and copies ran while one was open for 6% of the time, Pallas kernels for 0%

profile of v7, /device:TPU:1, one launch (start us, length us, event | category | flops | bytes accessed | tf_op | source)
XLA Modules:
  0.0 29.6 jit_solution(7142364485015385016)
XLA Ops:
  0.0 0.7 %slice.41 = bf16[64,128]{1,0:T(8,128)(2,1)S(1)} slice(bf16[64,512]{1,0:T(8,128)(2,1)} %bitcast.29), slice={[0:64], [0:128]} | slice | bytes 32768 | tf_op jit(solution)/shard_map/slice | solution.py:287
  0.7 2.0 %collective-permute-start = (bf16[64,128]{1,0:T(8,128)(2,1)S(1)}, bf16[64,128]{1,0:T(8,128)(2,1)S(1)}, u32[]{:S(2)}, u32[]{:S(2)}) collective-permute-start(bf16[64,128]{1,0:T(8,128)(2,1)S(1)} %slice.41), channel_id=1, source_target_pairs={{1,0},{2,1},{3,2},{5,4},{6,5},{7,6},{9,8},{10,9},{11,10},{13,12},{... | collective-permute-start | bytes 49160 | tf_op jit(solution)/shard_map/ppermute | solution.py:287
  2.7 4.0 %collective-permute-done.tail_ref = bf16[64,128]{1,0:T(8,128)(2,1)S(1)} collective-permute-done((bf16[64,128]{1,0:T(8,128)(2,1)S(1)}, bf16[64,128]{1,0:T(8,128)(2,1)S(1)}, u32[]{:S(2)}, u32[]{:S(2)}) %collective-permute-start) | collective-permute-done | bytes 16416 | tf_op jit(solution)/shard_map/ppermute | solution.py:287
  6.6 0.0 copy-start
  6.6 0.6 %copy-done = bf16[64,128]{1,0:T(8,128)(2,1)} copy-done((bf16[64,128]{1,0:T(8,128)(2,1)}, bf16[64,128]{1,0:T(8,128)(2,1)S(1)}, u32[]{:S(2)}) %copy-start) | copy-done | bytes 16408
  7.2 1.6 %shard_map.28 = bf16[8,64,192]{2,1,0:T(8,128)(2,1)} custom-call(bf16[64,512]{1,0:T(8,128)(2,1)} %bitcast.30, bf16[64,128]{1,0:T(8,128)(2,1)} %copy-done), custom_call_target="tpu_custom_call" | custom-call | bytes 278528 | tf_op jit(solution)/shard_map/pallas_call | solution.py:86
  8.9 5.6 %all-to-all-start = ((bf16[8,64,192]{2,1,0:T(8,128)(2,1)}), bf16[8,64,192]{2,1,0:T(8,128)(2,1)S(1)}, u32[]{:S(2)}, u32[]{:S(2)}) async-start(bf16[8,64,192]{2,1,0:T(8,128)(2,1)} %shard_map.28), calls=%async_computation | async-start | bytes 524288 | tf_op jit(solution)/shard_map/all_to_all | solution.py:290
  14.4 0.7 %rev.3 = f32[64]{0:T(128)S(1)} reverse(f32[64]{0:T(128)} %param.3), dimensions={0} | reverse | bytes 512 | tf_op jit(solution)/shard_map/rev | solution.py:18
  15.2 0.1 pad.12.clone
  15.3 0.2 tile.10
  15.5 0.1 reshape.48
  15.7 0.5 %cosine_multiply_fusion = (f32[256,128]{1,0:T(8,128)S(1)}, f32[256,128]{1,0:T(8,128)S(1)}) fusion(s32[128]{0:T(128)S(1)} %iota_add_fusion, f32[256]{0:T(256)S(1)} %get-tuple-element.11, f32[256]{0:T(256)S(1)} %get-tuple-element.12), kind=kLoop, calls=%fused_computation.26 | loop fusion | flops 524288 | bytes 264704 | tf_op jit(solution)/shard_map/mul | solution.py:51
  16.2 6.8 %all-to-all-done = bf16[8,64,192]{2,1,0:T(8,128)(2,1)S(1)} async-done(((bf16[8,64,192]{2,1,0:T(8,128)(2,1)}), bf16[8,64,192]{2,1,0:T(8,128)(2,1)S(1)}, u32[]{:S(2)}, u32[]{:S(2)}) %all-to-all-start) | async-done | bytes 196640 | tf_op jit(solution)/shard_map/all_to_all | solution.py:290
  23.0 0.1 bitcast_convert_fusion
  23.1 0.2 copy.4
  23.3 0.2 pad_slice_fusion
  23.5 0.2 maximum_maximum_fusion
  23.7 0.3 %reshape.47 = f32[3,256,192]{1,0,2:T(4,128)S(1)} reshape(f32[768,192]{0,1:T(8,128)S(1)} %maximum_maximum_fusion) | data formatting | bytes 1179648 | tf_op jit(solution)/shard_map/reshape | solution.py:37
  24.0 0.1 slice.42
  24.1 0.7 %fusion = bf16[2,128,192]{1,2,0:T(8,128)(2,1)S(1)} fusion(f32[2,64,192]{1,2,0:T(8,128)S(1)} %copy.13, f32[2,256,192]{1,2,0:T(8,128)S(1)} %bitcast.27, f32[128,320]{1,0:T(8,128)S(1)} %reshape.48), kind=kOutput, calls=%fused_computation.2 | convolution fusion | flops 188915712 | bytes 753664 | tf_op jit(solution)/shard_map/tw,bwc->btc/dot_general | solution.py:40
  24.8 0.4 %convolution_bitcast_fusion = f32[1,256,192]{2,1,0:T(8,128)S(1)} fusion(f32[256,128]{1,0:T(8,128)S(1)} %get-tuple-element.10, f32[256,128]{1,0:T(8,128)S(1)} %get-tuple-element.9, bf16[1,128,192]{1,2,0:T(8,128)(2,1)S(1)} %get-tuple-element.8, bf16[1,128,192]{1,2,0:T(8,128)(2,1)S(1)} %get-tuple-element.7), kind=kOutput, calls=%fused_computation | convolution fusion | flops 151257088 | bytes 557056 | tf_op jit(solution)/shard_map/nf,snc->sfc/dot_general | solution.py:59
  25.2 0.1 fusion.16
  25.3 0.7 %pad_maximum_fusion.refs_0_ = bf16[256,192]{1,0:T(8,128)(2,1)} fusion(bf16[128,192]{1,0:T(8,128)(2,1)S(1)} %get-tuple-element.6, bf16[128,192]{1,0:T(8,128)(2,1)S(1)} %get-tuple-element.5), kind=kLoop, calls=%fused_computation.20 | loop fusion | flops 196608 | bytes 196608 | tf_op jit(solution)/shard_map/concatenate | solution.py:70
  26.0 3.6 %shard_map.29 = bf16[64,128,256]{2,1,0:T(8,128)(2,1)} custom-call(bf16[256,192]{1,0:T(8,128)(2,1)} %pad_maximum_fusion.refs_0_), custom_call_target="tpu_custom_call" | custom-call | flops 6291456 | bytes 4292608 | tf_op jit(solution)/shard_map/pallas_call | solution.py:222
  (13 shorter events, 0.2 us)
Async XLA Ops:
  0.7 5.9 %collective-permute-start = (bf16[64,128]{1,0:T(8,128)(2,1)S(1)}, bf16[64,128]{1,0:T(8,128)(2,1)S(1)}, u32[]{:S(2)}, u32[]{:S(2)}) collective-permute-start(bf16[64,128]{1,0:T(8,128)(2,1)S(1)} %slice.41), channel_id=1, source_target_pairs={{1,0},{2,1},{3,2},{5,4},{6,5},{7,6},{9,8},{10,9},{11,10},{13,12},{... | collective-permute-start | bytes 49160 | tf_op jit(solution)/shard_map/ppermute | solution.py:287
  6.6 0.6 %copy-start = (bf16[64,128]{1,0:T(8,128)(2,1)}, bf16[64,128]{1,0:T(8,128)(2,1)S(1)}, u32[]{:S(2)}) copy-start(bf16[64,128]{1,0:T(8,128)(2,1)S(1)} %collective-permute-done.tail_ref) | copy-start | bytes 49156
  8.9 14.1 %all-to-all-start = ((bf16[8,64,192]{2,1,0:T(8,128)(2,1)}), bf16[8,64,192]{2,1,0:T(8,128)(2,1)S(1)}, u32[]{:S(2)}, u32[]{:S(2)}) async-start(bf16[8,64,192]{2,1,0:T(8,128)(2,1)} %shard_map.28), calls=%async_computation | async-start | bytes 524288 | tf_op jit(solution)/shard_map/all_to_all | solution.py:290

commit v8 on v7

--- a/solution.py
+++ b/solution.py
@@ -72,26 +72,58 @@
     )
 
 
-def windows_kernel(width, x_ref, tail_ref, out_ref):
-    padded = jnp.concatenate(
-        [x_ref[...].astype(jnp.float32), tail_ref[...].astype(jnp.float32)], axis=1
-    )
+def windows_kernel(width, tail_rows, x_ref, out_ref):
+    x = x_ref[...].astype(jnp.float32)
+    padded = jnp.concatenate([x, jnp.zeros((x.shape[0], tail_rows), jnp.float32)], axis=1)
     step = (padded.shape[1] - width) // (out_ref.shape[0] - 1)
     for j in range(out_ref.shape[0]):
         out_ref[j] = padded[:, j * step : j * step + width].astype(out_ref.dtype)
 
 
-def channel_windows(turned, tail, extent, width):
+def tail_windows_kernel(width, count, x_ref, tail_ref, windows_hbm, out_hbm, fresh, sem):
+    del windows_hbm
+    x = x_ref[...].astype(jnp.float32)
+    tail = tail_ref[...].astype(jnp.float32)
+    extent = out_hbm.shape[0]
+    rows = x.shape[1]
+    step = (rows + tail.shape[1] - width) // (extent - 1)
+    first = extent - count
+    padded = jnp.concatenate([x[:, first * step :], tail], axis=1)
+    for j in range(count):
+        fresh[j] = padded[:, j * step : j * step + width].astype(fresh.dtype)
+    copy = pltpu.make_async_copy(fresh, out_hbm.at[pl.ds(first, count)], sem)
+    copy.start()
+    copy.wait()
+
+
+def channel_windows(turned, tail, extent, width, tail_rows):
     slab, rows = turned.shape
-    return pl.pallas_call(
-        functools.partial(windows_kernel, width),
+    windows = pl.pallas_call(
+        functools.partial(windows_kernel, width, tail_rows),
         out_shape=jax.ShapeDtypeStruct((extent, slab, width), turned.dtype),
         cost_estimate=pl.CostEstimate(
-            flops=0,
-            transcendentals=0,
-            bytes_accessed=2 * (slab * (rows + tail.shape[1]) + extent * slab * width),
+            flops=0, transcendentals=0, bytes_accessed=2 * (slab * rows + extent * slab * width)
         ),
-    )(turned, tail)
+    )(turned)
+    count = -(-tail_rows // ((rows + tail_rows - width) // (extent - 1)))
+    return pl.pallas_call(
+        functools.partial(tail_windows_kernel, width, count),
+        out_shape=jax.ShapeDtypeStruct((extent, slab, width), turned.dtype),
+        in_specs=[
+            pl.BlockSpec(memory_space=pltpu.VMEM),
+            pl.BlockSpec(memory_space=pltpu.VMEM),
+            pl.BlockSpec(memory_space=pl.ANY),
+        ],
+        out_specs=pl.BlockSpec(memory_space=pl.ANY),
+        scratch_shapes=[
+            pltpu.VMEM((count, slab, width), turned.dtype),
+            pltpu.SemaphoreType.DMA(()),
+        ],
+        input_output_aliases={2: 0},
+        cost_estimate=pl.CostEstimate(
+            flops=0, transcendentals=0, bytes_accessed=2 * (slab * rows + 2 * count * slab * width)
+        ),
+    )(turned, tail, windows)
 
 
 def cross_kernel(segments, rows_per_step, own_ref, ext_ref, out_ref):
@@ -284,9 +316,10 @@
     reach = LAGS // block_rows
     turned = strain.T
     route = [(c + 1, c) for c in range(columns_n - 1)]
-    tail = lax.ppermute(turned[:, : reach * block_rows], "col", route)
+    following = lax.ppermute(turned, "col", route)
+    tail = following[:, : reach * block_rows]
     width = (reach + 1) * block_rows
-    windows = channel_windows(turned, tail, extent, width)
+    windows = channel_windows(turned, tail, extent, width, reach * block_rows)
     gathered = lax.all_to_all(windows, "ta", split_axis=0, concat_axis=0, tiled=True)
     samples = gathered.reshape(extent * slab, width)
     filtered = decimate_t(samples.astype(jnp.float32), filter_taps)

time: 30 us -> 29.5 us (0.983)
  Pallas kernels: 5.29 us -> 6.85 us
  waiting for transfers between devices: 10.7 us -> 9.36 us
  local copies, waits for them, and re-layouts: 3.32 us -> 2.6 us
    pallas_call x1 -> x2, Pallas kernels: 1.65 us -> 3.2 us  [the longest x1 1.65 us: channel_windows(): pl.pallas_call(functools.partial(windows_kernel, width, tail_rows), out_s...]
    ppermute x1, waiting for transfers between devices: 3.95 us -> 3.04 us  [body(): following = lax.ppermute(turned, 'col', route)]
    unnamed x3 -> x1, local copies, waits for them, and re-layouts: 0.61 us -> 0.01 us
    all_to_all x1, waiting for transfers between devices: 6.77 us -> 6.31 us  [body(): lax.all_to_all(windows, 'ta', split_axis=0, concat_axis=0, tiled=True)]
  transfers between devices with their start and end apart: 2 -> 2, of which waited for: 2 -> 2; matrix products, arithmetic and copies ran while one was open for 6% -> 6% of each run, Pallas kernels for 0% -> 6%
where the time goes in v8:
time: 29.5 us; the launch traced here: 29.1 us
  waiting for transfers between devices  9.36 us (32%)
  starting transfers between devices  7.52 us (25%)
  Pallas kernels  6.85 us (23%)
  local copies, waits for them, and re-layouts  2.6 us (9%)
  other arithmetic  1.61 us (5%)
  matrix products  1.04 us (4%)
    all_to_all x1, waiting for transfers between devices, body(): lax.all_to_all(windows, 'ta', split_axis=0, concat_axis=0, tiled=True)  6.31 us
    all_to_all x1, starting transfers between devices, body(): lax.all_to_all(windows, 'ta', split_axis=0, concat_axis=0, tiled=True)  5.57 us
    pallas_call x1, Pallas kernels, cross_spectra_pieces(): pl.pallas_call(functools.partial(cross_kernel_pieces, segments, rows, chu...  3.64 us
    ppermute x1, waiting for transfers between devices, body(): following = lax.ppermute(turned, 'col', route)  3.04 us
    ppermute x1, starting transfers between devices, body(): following = lax.ppermute(turned, 'col', route)  1.96 us
    pallas_call x1, Pallas kernels, channel_windows(): pl.pallas_call(functools.partial(windows_kernel, width, tail_rows), out_s...  1.65 us
    pallas_call x1, Pallas kernels, channel_windows(): pl.pallas_call(functools.partial(tail_windows_kernel, width, count), out_...  1.56 us
    rev x1, local copies, waits for them, and re-layouts, tap_rows(): flipped = filter_taps[::-1]  0.75 us
  transfers between devices with their start and end apart: 2, of which 2 were waited for; matrix products, arithmetic and copies ran while one was open for 6% of the time, Pallas kernels for 6%

profile of v8, /device:TPU:1, one launch (start us, length us, event | category | flops | bytes accessed | tf_op | source)
XLA Modules:
  0.0 29.1 jit_solution(3170248238994288896)
XLA Ops:
  0.0 2.0 %collective-permute-start = (bf16[64,512]{1,0:T(8,128)(2,1)}, bf16[64,512]{1,0:T(8,128)(2,1)S(1)}, u32[]{:S(2)}, u32[]{:S(2)}) collective-permute-start(bf16[64,512]{1,0:T(8,128)(2,1)} %bitcast.29), channel_id=1, source_target_pairs={{1,0},{2,1},{3,2},{5,4},{6,5},{7,6},{9,8},{10,9},{11,10},{13,12},{... | collective-permute-start | bytes 196616 | tf_op jit(solution)/shard_map/ppermute | solution.py:319
  2.0 1.6 %shard_map.28.windows_hbm = bf16[8,64,192]{2,1,0:T(8,128)(2,1)} custom-call(bf16[64,512]{1,0:T(8,128)(2,1)} %bitcast.30), custom_call_target="tpu_custom_call" | custom-call | bytes 262144 | tf_op jit(solution)/shard_map/pallas_call | solution.py:101
  3.6 3.0 %collective-permute-done = bf16[64,512]{1,0:T(8,128)(2,1)S(1)} collective-permute-done((bf16[64,512]{1,0:T(8,128)(2,1)}, bf16[64,512]{1,0:T(8,128)(2,1)S(1)}, u32[]{:S(2)}, u32[]{:S(2)}) %collective-permute-start) | collective-permute-done | bytes 65568 | tf_op jit(solution)/shard_map/ppermute | solution.py:319
  6.7 0.6 %slice.41.tail_ref = bf16[64,128]{1,0:T(8,128)(2,1)} slice(bf16[64,512]{1,0:T(8,128)(2,1)S(1)} %collective-permute-done), slice={[0:64], [0:128]} | slice | bytes 32768 | tf_op jit(solution)/shard_map/slice | solution.py:320
  7.3 1.6 %shard_map.29 = bf16[8,64,192]{2,1,0:T(8,128)(2,1)} custom-call(bf16[64,512]{1,0:T(8,128)(2,1)} %bitcast.31, bf16[64,128]{1,0:T(8,128)(2,1)} %slice.41.tail_ref, bf16[8,64,192]{2,1,0:T(8,128)(2,1)} %shard_map.28.windows_hbm), custom_call_target="tpu_custom_call", output_to_operand_aliasing={{}: (2, {})} | custom-call | bytes 163840 | tf_op jit(solution)/shard_map/pallas_call | solution.py:109
  8.8 5.6 %all-to-all-start = ((bf16[8,64,192]{2,1,0:T(8,128)(2,1)}), bf16[8,64,192]{2,1,0:T(8,128)(2,1)S(1)}, u32[]{:S(2)}, u32[]{:S(2)}) async-start(bf16[8,64,192]{2,1,0:T(8,128)(2,1)} %shard_map.29), calls=%async_computation | async-start | bytes 524288 | tf_op jit(solution)/shard_map/all_to_all | solution.py:323
  14.4 0.7 %rev.3 = f32[64]{0:T(128)S(1)} reverse(f32[64]{0:T(128)} %param.3), dimensions={0} | reverse | bytes 512 | tf_op jit(solution)/shard_map/rev | solution.py:18
  15.1 0.1 pad.12.clone
  15.3 0.2 tile.10
  15.5 0.1 reshape.48
  15.6 0.5 %cosine_multiply_fusion = (f32[256,128]{1,0:T(8,128)S(1)}, f32[256,128]{1,0:T(8,128)S(1)}) fusion(s32[128]{0:T(128)S(1)} %iota_add_fusion, f32[256]{0:T(256)S(1)} %get-tuple-element.11, f32[256]{0:T(256)S(1)} %get-tuple-element.12), kind=kLoop, calls=%fused_computation.26 | loop fusion | flops 524288 | bytes 264704 | tf_op jit(solution)/shard_map/mul | solution.py:51
  16.2 6.3 %all-to-all-done = bf16[8,64,192]{2,1,0:T(8,128)(2,1)S(1)} async-done(((bf16[8,64,192]{2,1,0:T(8,128)(2,1)}), bf16[8,64,192]{2,1,0:T(8,128)(2,1)S(1)}, u32[]{:S(2)}, u32[]{:S(2)}) %all-to-all-start) | async-done | bytes 196640 | tf_op jit(solution)/shard_map/all_to_all | solution.py:323
  22.5 0.1 bitcast_convert_fusion
  22.6 0.2 copy.5
  22.8 0.2 pad_slice_fusion
  23.0 0.2 maximum_maximum_fusion
  23.2 0.3 %reshape.47 = f32[3,256,192]{1,0,2:T(4,128)S(1)} reshape(f32[768,192]{0,1:T(8,128)S(1)} %maximum_maximum_fusion) | data formatting | bytes 1179648 | tf_op jit(solution)/shard_map/reshape | solution.py:37
  23.5 0.1 slice.42
  23.6 0.7 %fusion = bf16[2,128,192]{1,2,0:T(8,128)(2,1)S(1)} fusion(f32[2,64,192]{1,2,0:T(8,128)S(1)} %copy.14, f32[2,256,192]{1,2,0:T(8,128)S(1)} %bitcast.27, f32[128,320]{1,0:T(8,128)S(1)} %reshape.48), kind=kOutput, calls=%fused_computation.2 | convolution fusion | flops 188915712 | bytes 753664 | tf_op jit(solution)/shard_map/tw,bwc->btc/dot_general | solution.py:40
  24.3 0.4 %convolution_bitcast_fusion = f32[1,256,192]{2,1,0:T(8,128)S(1)} fusion(f32[256,128]{1,0:T(8,128)S(1)} %get-tuple-element.10, f32[256,128]{1,0:T(8,128)S(1)} %get-tuple-element.9, bf16[1,128,192]{1,2,0:T(8,128)(2,1)S(1)} %get-tuple-element.8, bf16[1,128,192]{1,2,0:T(8,128)(2,1)S(1)} %get-tuple-element.7), kind=kOutput, calls=%fused_computation | convolution fusion | flops 151257088 | bytes 557056 | tf_op jit(solution)/shard_map/nf,snc->sfc/dot_general | solution.py:59
  24.7 0.1 fusion.16
  24.8 0.7 %pad_maximum_fusion.refs_0_ = bf16[256,192]{1,0:T(8,128)(2,1)} fusion(bf16[128,192]{1,0:T(8,128)(2,1)S(1)} %get-tuple-element.6, bf16[128,192]{1,0:T(8,128)(2,1)S(1)} %get-tuple-element.5), kind=kLoop, calls=%fused_computation.20 | loop fusion | flops 196608 | bytes 196608 | tf_op jit(solution)/shard_map/concatenate | solution.py:70
  25.5 3.6 %shard_map.30 = bf16[64,128,256]{2,1,0:T(8,128)(2,1)} custom-call(bf16[256,192]{1,0:T(8,128)(2,1)} %pad_maximum_fusion.refs_0_), custom_call_target="tpu_custom_call" | custom-call | flops 6291456 | bytes 4292608 | tf_op jit(solution)/shard_map/pallas_call | solution.py:254
  (13 shorter events, 0.2 us)
Async XLA Ops:
  0.0 6.7 %collective-permute-start = (bf16[64,512]{1,0:T(8,128)(2,1)}, bf16[64,512]{1,0:T(8,128)(2,1)S(1)}, u32[]{:S(2)}, u32[]{:S(2)}) collective-permute-start(bf16[64,512]{1,0:T(8,128)(2,1)} %bitcast.29), channel_id=1, source_target_pairs={{1,0},{2,1},{3,2},{5,4},{6,5},{7,6},{9,8},{10,9},{11,10},{13,12},{... | collective-permute-start | bytes 196616 | tf_op jit(solution)/shard_map/ppermute | solution.py:319
  8.8 13.7 %all-to-all-start = ((bf16[8,64,192]{2,1,0:T(8,128)(2,1)}), bf16[8,64,192]{2,1,0:T(8,128)(2,1)S(1)}, u32[]{:S(2)}, u32[]{:S(2)}) async-start(bf16[8,64,192]{2,1,0:T(8,128)(2,1)} %shard_map.29), calls=%async_computation | async-start | bytes 524288 | tf_op jit(solution)/shard_map/all_to_all | solution.py:323

commit v9 on v8

--- a/solution.py
+++ b/solution.py
@@ -270,6 +270,101 @@
     )(*pieces)
 
 
+def fused_kernel(rows, chunk, samples_ref, matrix_ref, table_ref, out_hbm, own_f32, shifted,
+                 buffers, sems):
+    tap_count = matrix_ref.shape[1] - matrix_ref.shape[0] * 2
+    outputs = matrix_ref.shape[0]
+    length, channels = samples_ref.shape
+    blocks = length // (2 * outputs)
+    x = samples_ref[...].astype(jnp.float32)
+    joined = jnp.concatenate(
+        [
+            jnp.zeros((tap_count, channels), jnp.float32),
+            x,
+            jnp.zeros((2 * outputs - tap_count, channels), jnp.float32),
+        ],
+        axis=0,
+    )
+    matrix = matrix_ref[...]
+    filtered = jnp.concatenate(
+        [
+            jnp.dot(
+                matrix,
+                joined[b * 2 * outputs : b * 2 * outputs + 2 * outputs + tap_count],
+                precision=lax.Precision.HIGHEST,
+                preferred_element_type=jnp.float32,
+            )
+            for b in range(blocks)
+        ],
+        axis=0,
+    )
+    filtered = filtered.astype(jnp.bfloat16).astype(jnp.float32)
+    spectrum = jnp.dot(
+        table_ref[...], filtered, precision=lax.Precision.HIGHEST, preferred_element_type=jnp.float32
+    )
+    real_part = spectrum[:NF]
+    imag_part = spectrum[NF:]
+    powers = real_part * real_part + imag_part * imag_part
+    mean_power = jnp.mean(powers, axis=0, keepdims=True)
+    whitening = 1.0 / jnp.sqrt(powers + mean_power + 1e-06)
+    whitened = jnp.concatenate([real_part * whitening, imag_part * whitening], axis=0)
+    extended = whitened.astype(jnp.bfloat16).astype(jnp.float32).T
+    span = shifted.shape[1]
+    own_f32[...] = extended[:rows]
+    for i in range(chunk):
+        shifted[i] = extended[i : i + span]
+    slots, parts = buffers.shape[0], sems.shape[1]
+    part = chunk // parts
+    copies = []
+    for m in range(rows // chunk):
+        slot = m % slots
+        if m >= slots:
+            for copy in copies[m - slots]:
+                copy.wait()
+        base = m * chunk
+        for i in range(chunk):
+            a = own_f32[base + i : base + i + 1, :]
+            b = shifted[i, base : base + LAGS, :]
+            acc_re, acc_im = product_terms(a, b)
+            store_row(buffers.at[slot], i, acc_re, acc_im, 1)
+        group = []
+        for p in range(parts):
+            copy = pltpu.make_async_copy(
+                buffers.at[slot, pl.ds(p * part, part)],
+                out_hbm.at[pl.ds(base + p * part, part)],
+                sems.at[slot, p],
+            )
+            copy.start()
+            group.append(copy)
+        copies.append(group)
+    for group in copies[-slots:]:
+        for copy in group:
+            copy.wait()
+
+
+def fused_spectra(samples, matrix, table_t, rows):
+    length, channels = samples.shape
+    chunk = 8
+    span = channels - chunk
+    return pl.pallas_call(
+        functools.partial(fused_kernel, rows, chunk),
+        out_shape=jax.ShapeDtypeStruct((rows, LAGS, NFFT), jnp.bfloat16),
+        in_specs=[pl.BlockSpec(memory_space=pltpu.VMEM)] * 3,
+        out_specs=pl.BlockSpec(memory_space=pl.ANY),
+        scratch_shapes=[
+            pltpu.VMEM((rows, NFFT), jnp.float32),
+            pltpu.VMEM((chunk, span, NFFT), jnp.float32),
+            pltpu.VMEM((4, chunk, LAGS, NFFT), jnp.bfloat16),
+            pltpu.SemaphoreType.DMA((4, 4)),
+        ],
+        cost_estimate=pl.CostEstimate(
+            flops=6 * rows * LAGS * NF + 12 * channels * (matrix.size * length // 256 + NFFT * NFFT),
+            transcendentals=2 * NF * channels,
+            bytes_accessed=rows * LAGS * NFFT * 2 + 2 * samples.size + 4 * (matrix.size + table_t.size),
+        ),
+    )(samples, matrix, table_t)
+
+
 def cross_spectra(own, extended):
     rows, segments, columns = own.shape
     reach_rows = extended.shape[0]
@@ -322,6 +417,9 @@
     windows = channel_windows(turned, tail, extent, width, reach * block_rows)
     gathered = lax.all_to_all(windows, "ta", split_axis=0, concat_axis=0, tiled=True)
     samples = gathered.reshape(extent * slab, width)
+    if extent * slab == 2 * NFFT:
+        matrix = tap_rows(filter_taps, NFFT // 2)
+        return fused_spectra(samples, matrix, fourier_table().T, block_rows)[None]
     filtered = decimate_t(samples.astype(jnp.float32), filter_taps)
     whitened_t = whiten_t(filtered)
     segments, columns, _ = whitened_t.shape

time: 29.5 us -> 30.6 us (1.037)
  the two profiles are of different devices: /device:TPU:1 before, /device:TPU:0 now
where the time goes in v9:
time: 30.6 us; the launch traced here: 30.2 us
  waiting for transfers between devices  8.84 us (29%)
  starting transfers between devices  8.57 us (28%)
  Pallas kernels  8.35 us (27%)
  local copies, waits for them, and re-layouts  3.06 us (10%)
  other arithmetic  1.36 us (4%)
    all_to_all x1, waiting for transfers between devices, body(): lax.all_to_all(windows, 'ta', split_axis=0, concat_axis=0, tiled=True)  8.84 us
    all_to_all x1, starting transfers between devices, body(): lax.all_to_all(windows, 'ta', split_axis=0, concat_axis=0, tiled=True)  7.29 us
    pallas_call x1, Pallas kernels, fused_spectra(): pl.pallas_call(functools.partial(fused_kernel, rows, chunk), out_shape=ja...  5.15 us
    pallas_call x1, Pallas kernels, channel_windows(): pl.pallas_call(functools.partial(windows_kernel, width, tail_rows), out_s...  1.65 us
    pallas_call x1, Pallas kernels, channel_windows(): pl.pallas_call(functools.partial(tail_windows_kernel, width, count), out_...  1.56 us
    ppermute x1, starting transfers between devices, body(): following = lax.ppermute(turned, 'col', route)  1.28 us
    reshape x1, local copies, waits for them, and re-layouts, tap_rows(): return repeated.reshape(outputs, window)  0.76 us
    rev x1, local copies, waits for them, and re-layouts, tap_rows(): flipped = filter_taps[::-1]  0.75 us
  transfers between devices with their start and end apart: 2, of which 1 were waited for; matrix products, arithmetic and copies ran while one was open for 10% of the time, Pallas kernels for 5%

profile of v9, /device:TPU:0, one launch (start us, length us, event | category | flops | bytes accessed | tf_op | source)
XLA Modules:
  0.0 30.2 jit_solution(3232809049904891870)
XLA Ops:
  0.0 1.3 %collective-permute-start = (bf16[64,512]{1,0:T(8,128)(2,1)}, bf16[64,512]{1,0:T(8,128)(2,1)S(1)}, u32[]{:S(2)}, u32[]{:S(2)}) collective-permute-start(bf16[64,512]{1,0:T(8,128)(2,1)} %bitcast.6), channel_id=1, source_target_pairs={{1,0},{2,1},{3,2},{5,4},{6,5},{7,6},{9,8},{10,9},{11,10},{13,12},{... | collective-permute-start | bytes 196616 | tf_op jit(solution)/shard_map/ppermute | solution.py:414
  1.3 1.6 %shard_map.28.windows_hbm = bf16[8,64,192]{2,1,0:T(8,128)(2,1)} custom-call(bf16[64,512]{1,0:T(8,128)(2,1)} %bitcast.7), custom_call_target="tpu_custom_call" | custom-call | bytes 262144 | tf_op jit(solution)/shard_map/pallas_call | solution.py:101
  3.0 0.7 %rev.3 = f32[64]{0:T(128)S(1)} reverse(f32[64]{0:T(128)} %param.3), dimensions={0} | reverse | bytes 512 | tf_op jit(solution)/shard_map/rev | solution.py:18
  3.8 0.2 tile.10
  4.0 0.8 %reshape.8.matrix_ref = f32[128,320]{1,0:T(8,128)} reshape(f32[40960]{0:T(1024)S(1)} %slice.9) | data formatting | bytes 327680 | tf_op jit(solution)/shard_map/reshape | solution.py:21
  4.8 0.0 collective-permute-done
  4.8 0.6 %slice.8.tail_ref = bf16[64,128]{1,0:T(8,128)(2,1)} slice(bf16[64,512]{1,0:T(8,128)(2,1)S(1)} %collective-permute-done), slice={[0:64], [0:128]} | slice | bytes 32768 | tf_op jit(solution)/shard_map/slice | solution.py:415
  5.4 1.6 %shard_map.29 = bf16[8,64,192]{2,1,0:T(8,128)(2,1)} custom-call(bf16[64,512]{1,0:T(8,128)(2,1)} %bitcast.8, bf16[64,128]{1,0:T(8,128)(2,1)} %slice.8.tail_ref, bf16[8,64,192]{2,1,0:T(8,128)(2,1)} %shard_map.28.windows_hbm), custom_call_target="tpu_custom_call", output_to_operand_aliasing={{}: (2, {})} | custom-call | bytes 163840 | tf_op jit(solution)/shard_map/pallas_call | solution.py:109
  6.9 7.3 %all-to-all-start = ((bf16[8,64,192]{2,1,0:T(8,128)(2,1)}), bf16[8,64,192]{2,1,0:T(8,128)(2,1)S(1)}, u32[]{:S(2)}, u32[]{:S(2)}) async-start(bf16[8,64,192]{2,1,0:T(8,128)(2,1)} %shard_map.29), calls=%async_computation | async-start | bytes 524288 | tf_op jit(solution)/shard_map/all_to_all | solution.py:418
  14.2 0.6 %cosine_multiply_fusion = (f32[256,128]{0,1:T(8,128)S(1)}, f32[256,128]{0,1:T(8,128)S(1)}) fusion(s32[128]{0:T(128)S(1)} %iota_add_fusion, f32[256]{0:T(256)S(1)} %get-tuple-element.7, f32[256]{0:T(256)S(1)} %get-tuple-element.8), kind=kLoop, calls=%fused_computation.8 | loop fusion | flops 524288 | bytes 264704 | tf_op jit(solution)/shard_map/mul | solution.py:51
  14.8 0.7 %maximum_bitcast_fusion.table_ref = f32[256,256]{1,0:T(8,128)} fusion(f32[256,128]{0,1:T(8,128)S(1)} %get-tuple-element.6, f32[256,128]{0,1:T(8,128)S(1)} %get-tuple-element.5), kind=kLoop, calls=%fused_computation | loop fusion | flops 65536 | bytes 524288 | tf_op jit(solution)/shard_map/transpose | solution.py:422
  15.6 8.8 %all-to-all-done = bf16[8,64,192]{2,1,0:T(8,128)(2,1)S(1)} async-done(((bf16[8,64,192]{2,1,0:T(8,128)(2,1)}), bf16[8,64,192]{2,1,0:T(8,128)(2,1)S(1)}, u32[]{:S(2)}, u32[]{:S(2)}) %all-to-all-start) | async-done | bytes 196640 | tf_op jit(solution)/shard_map/all_to_all | solution.py:418
  24.4 0.0 copy-start
  24.4 0.7 %copy-done = bf16[8,64,192]{2,1,0:T(8,128)(2,1)} copy-done((bf16[8,64,192]{2,1,0:T(8,128)(2,1)}, bf16[8,64,192]{2,1,0:T(8,128)(2,1)S(1)}, u32[]{:S(2)}) %copy-start) | copy-done | bytes 196632
  25.1 5.1 %shard_map.30 = bf16[64,128,256]{2,1,0:T(8,128)(2,1)} custom-call(bf16[512,192]{1,0:T(8,128)(2,1)} %bitcast.5, f32[128,320]{1,0:T(8,128)} %reshape.8.matrix_ref, f32[256,256]{1,0:T(8,128)} %maximum_bitcast_fusion.table_ref), custom_call_target="tpu_custom_call" | custom-call | flops 346030080 | bytes 4816896 | tf_op jit(solution)/shard_map/pallas_call | solution.py:349
  (5 shorter events, 0.1 us)
Async XLA Ops:
  0.0 4.8 %collective-permute-start = (bf16[64,512]{1,0:T(8,128)(2,1)}, bf16[64,512]{1,0:T(8,128)(2,1)S(1)}, u32[]{:S(2)}, u32[]{:S(2)}) collective-permute-start(bf16[64,512]{1,0:T(8,128)(2,1)} %bitcast.6), channel_id=1, source_target_pairs={{1,0},{2,1},{3,2},{5,4},{6,5},{7,6},{9,8},{10,9},{11,10},{13,12},{... | collective-permute-start | bytes 196616 | tf_op jit(solution)/shard_map/ppermute | solution.py:414
  6.9 17.5 %all-to-all-start = ((bf16[8,64,192]{2,1,0:T(8,128)(2,1)}), bf16[8,64,192]{2,1,0:T(8,128)(2,1)S(1)}, u32[]{:S(2)}, u32[]{:S(2)}) async-start(bf16[8,64,192]{2,1,0:T(8,128)(2,1)} %shard_map.29), calls=%async_computation | async-start | bytes 524288 | tf_op jit(solution)/shard_map/all_to_all | solution.py:418
  24.4 0.7 %copy-start = (bf16[8,64,192]{2,1,0:T(8,128)(2,1)}, bf16[8,64,192]{2,1,0:T(8,128)(2,1)S(1)}, u32[]{:S(2)}) copy-start(bf16[8,64,192]{2,1,0:T(8,128)(2,1)S(1)} %all-to-all-done) | copy-start | bytes 589828

commit v10 on v9

--- a/solution.py
+++ b/solution.py
@@ -50,6 +50,16 @@
     return jnp.concatenate(
         [window_taper * jnp.cos(angles), -window_taper * jnp.sin(angles)], axis=1
     )
+
+
+def fourier_table_t():
+    moment = lax.broadcasted_iota(jnp.int32, (NFFT, NFFT), 1)
+    frequency = lax.broadcasted_iota(jnp.int32, (NFFT, NFFT), 0) % NF + 1
+    phase_index = moment * frequency % NFFT
+    angles = phase_index.astype(jnp.float32) * (2.0 * jnp.pi / NFFT)
+    window_taper = 0.5 - 0.5 * jnp.cos(moment.astype(jnp.float32) * (2.0 * jnp.pi / NFFT))
+    real_rows = lax.broadcasted_iota(jnp.int32, (NFFT, NFFT), 0) < NF
+    return jnp.where(real_rows, window_taper * jnp.cos(angles), -window_taper * jnp.sin(angles))
 
 
 def whiten_t(filtered):
@@ -270,12 +280,21 @@
     )(*pieces)
 
 
-def fused_kernel(rows, chunk, samples_ref, matrix_ref, table_ref, out_hbm, own_f32, shifted,
+def fused_kernel(rows, chunk, taps_ref, samples_ref, table_ref, out_hbm, own_f32, shifted,
                  buffers, sems):
-    tap_count = matrix_ref.shape[1] - matrix_ref.shape[0] * 2
-    outputs = matrix_ref.shape[0]
+    tap_count = taps_ref.shape[0]
+    outputs = NFFT // 2
     length, channels = samples_ref.shape
     blocks = length // (2 * outputs)
+    lanes = 3 * NF
+    lane = lax.broadcasted_iota(jnp.int32, (1, lanes), 1)
+    row = jnp.zeros((1, lanes), jnp.float32)
+    for k in range(tap_count):
+        row = jnp.where(lane == tap_count - 1 - k, taps_ref[k], row)
+    rolled = pltpu.roll(
+        jnp.broadcast_to(row, (outputs, lanes)), 0, 1, stride=2, stride_axis=0
+    )
+    matrix = rolled[:, : 2 * outputs + tap_count]
     x = samples_ref[...].astype(jnp.float32)
     joined = jnp.concatenate(
         [
@@ -285,7 +304,6 @@
         ],
         axis=0,
     )
-    matrix = matrix_ref[...]
     filtered = jnp.concatenate(
         [
             jnp.dot(
@@ -342,14 +360,14 @@
             copy.wait()
 
 
-def fused_spectra(samples, matrix, table_t, rows):
+def fused_spectra(samples, filter_taps, table_t, rows):
     length, channels = samples.shape
     chunk = 8
     span = channels - chunk
     return pl.pallas_call(
         functools.partial(fused_kernel, rows, chunk),
         out_shape=jax.ShapeDtypeStruct((rows, LAGS, NFFT), jnp.bfloat16),
-        in_specs=[pl.BlockSpec(memory_space=pltpu.VMEM)] * 3,
+        in_specs=[pl.BlockSpec(memory_space=pltpu.SMEM)] + [pl.BlockSpec(memory_space=pltpu.VMEM)] * 2,
         out_specs=pl.BlockSpec(memory_space=pl.ANY),
         scratch_shapes=[
             pltpu.VMEM((rows, NFFT), jnp.float32),
@@ -358,11 +376,11 @@
             pltpu.SemaphoreType.DMA((4, 4)),
         ],
         cost_estimate=pl.CostEstimate(
-            flops=6 * rows * LAGS * NF + 12 * channels * (matrix.size * length // 256 + NFFT * NFFT),
+            flops=6 * rows * LAGS * NF + 12 * channels * (NF * 320 * length // 256 + NFFT * NFFT),
             transcendentals=2 * NF * channels,
-            bytes_accessed=rows * LAGS * NFFT * 2 + 2 * samples.size + 4 * (matrix.size + table_t.size),
+            bytes_accessed=rows * LAGS * NFFT * 2 + 2 * samples.size + 4 * table_t.size,
         ),
-    )(samples, matrix, table_t)
+    )(filter_taps, samples, table_t)
 
 
 def cross_spectra(own, extended):
@@ -418,8 +436,7 @@
     gathered = lax.all_to_all(windows, "ta", split_axis=0, concat_axis=0, tiled=True)
     samples = gathered.reshape(extent * slab, width)
     if extent * slab == 2 * NFFT:
-        matrix = tap_rows(filter_taps, NFFT // 2)
-        return fused_spectra(samples, matrix, fourier_table().T, block_rows)[None]
+        return fused_spectra(samples, filter_taps, fourier_table_t(), block_rows)[None]
     filtered = decimate_t(samples.astype(jnp.float32), filter_taps)
     whitened_t = whiten_t(filtered)
     segments, columns, _ = whitened_t.shape

time: 30.6 us -> 28.6 us (0.935)
  the two profiles are of different devices: /device:TPU:0 before, /device:TPU:1 now
where the time goes in v10:
time: 28.6 us; the launch traced here: 28.3 us
  waiting for transfers between devices  9.02 us (32%)
  Pallas kernels  8.29 us (29%)
  starting transfers between devices  7.52 us (26%)
  other arithmetic  2.13 us (7%)
  local copies, waits for them, and re-layouts  1.31 us (5%)
    all_to_all x1, waiting for transfers between devices, body(): lax.all_to_all(windows, 'ta', split_axis=0, concat_axis=0, tiled=True)  6.03 us
    all_to_all x1, starting transfers between devices, body(): lax.all_to_all(windows, 'ta', split_axis=0, concat_axis=0, tiled=True)  5.57 us
    pallas_call x1, Pallas kernels, fused_spectra(): pl.pallas_call(functools.partial(fused_kernel, rows, chunk), out_shape=ja...  5.08 us
    ppermute x1, waiting for transfers between devices, body(): following = lax.ppermute(turned, 'col', route)  3 us
    select_n x1, other arithmetic, fourier_table_t(): jnp.where(real_rows, window_taper * jnp.cos(angles), -window_taper * jnp....  2.08 us
    ppermute x1, starting transfers between devices, body(): following = lax.ppermute(turned, 'col', route)  1.96 us
    pallas_call x1, Pallas kernels, channel_windows(): pl.pallas_call(functools.partial(windows_kernel, width, tail_rows), out_s...  1.65 us
    pallas_call x1, Pallas kernels, channel_windows(): pl.pallas_call(functools.partial(tail_windows_kernel, width, count), out_...  1.56 us
  transfers between devices with their start and end apart: 2, of which 2 were waited for; matrix products, arithmetic and copies ran while one was open for 8% of the time, Pallas kernels for 6%

profile of v10, /device:TPU:1, one launch (start us, length us, event | category | flops | bytes accessed | tf_op | source)
XLA Modules:
  0.0 28.3 jit_solution(2889619834000914464)
XLA Ops:
  0.0 2.0 %collective-permute-start = (bf16[64,512]{1,0:T(8,128)(2,1)}, bf16[64,512]{1,0:T(8,128)(2,1)S(1)}, u32[]{:S(2)}, u32[]{:S(2)}) collective-permute-start(bf16[64,512]{1,0:T(8,128)(2,1)} %bitcast.4), channel_id=1, source_target_pairs={{1,0},{2,1},{3,2},{5,4},{6,5},{7,6},{9,8},{10,9},{11,10},{13,12},{... | collective-permute-start | bytes 196616 | tf_op jit(solution)/shard_map/ppermute | solution.py:432
  2.0 1.6 %shard_map.28.windows_hbm = bf16[8,64,192]{2,1,0:T(8,128)(2,1)} custom-call(bf16[64,512]{1,0:T(8,128)(2,1)} %bitcast.5), custom_call_target="tpu_custom_call" | custom-call | bytes 262144 | tf_op jit(solution)/shard_map/pallas_call | solution.py:111
  3.7 3.0 %collective-permute-done = bf16[64,512]{1,0:T(8,128)(2,1)S(1)} collective-permute-done((bf16[64,512]{1,0:T(8,128)(2,1)}, bf16[64,512]{1,0:T(8,128)(2,1)S(1)}, u32[]{:S(2)}, u32[]{:S(2)}) %collective-permute-start) | collective-permute-done | bytes 65568 | tf_op jit(solution)/shard_map/ppermute | solution.py:432
  6.7 0.6 %slice.4.tail_ref = bf16[64,128]{1,0:T(8,128)(2,1)} slice(bf16[64,512]{1,0:T(8,128)(2,1)S(1)} %collective-permute-done), slice={[0:64], [0:128]} | slice | bytes 32768 | tf_op jit(solution)/shard_map/slice | solution.py:433
  7.3 1.6 %shard_map.29 = bf16[8,64,192]{2,1,0:T(8,128)(2,1)} custom-call(bf16[64,512]{1,0:T(8,128)(2,1)} %bitcast.6, bf16[64,128]{1,0:T(8,128)(2,1)} %slice.4.tail_ref, bf16[8,64,192]{2,1,0:T(8,128)(2,1)} %shard_map.28.windows_hbm), custom_call_target="tpu_custom_call", output_to_operand_aliasing={{}: (2, {})} | custom-call | bytes 163840 | tf_op jit(solution)/shard_map/pallas_call | solution.py:119
  8.8 5.6 %all-to-all-start = ((bf16[8,64,192]{2,1,0:T(8,128)(2,1)}), bf16[8,64,192]{2,1,0:T(8,128)(2,1)S(1)}, u32[]{:S(2)}, u32[]{:S(2)}) async-start(bf16[8,64,192]{2,1,0:T(8,128)(2,1)} %shard_map.29), calls=%async_computation | async-start | bytes 524288 | tf_op jit(solution)/shard_map/all_to_all | solution.py:436
  14.4 2.1 %multiply_select_fusion.table_ref = f32[256,256]{1,0:T(8,128)} fusion(f32[256]{0:T(256)S(1)} %get-tuple-element.10, s32[256]{0:T(256)S(1)} %get-tuple-element.7, s32[256]{0:T(256)S(1)} %get-tuple-element.8, f32[256]{0:T(256)S(1)} %get-tuple-element.9, pred[256]{0:T(512)(128)(4,1)S(1)} %get-tuple-element.5, pred[256]{0:T(512)(128)(4,1)S(1)} %get-tuple-element.6), kind=kLoop, calls=%fused_computation.6 | loop fusion | flops 1245184 | bytes 266752 | tf_op jit(solution)/shard_map/jit(_where)/select_n | solution.py:62
  16.5 6.0 %all-to-all-done = bf16[8,64,192]{2,1,0:T(8,128)(2,1)S(1)} async-done(((bf16[8,64,192]{2,1,0:T(8,128)(2,1)}), bf16[8,64,192]{2,1,0:T(8,128)(2,1)S(1)}, u32[]{:S(2)}, u32[]{:S(2)}) %all-to-all-start) | async-done | bytes 196640 | tf_op jit(solution)/shard_map/all_to_all | solution.py:436
  22.5 0.0 copy-start
  22.5 0.7 %copy-done = bf16[8,64,192]{2,1,0:T(8,128)(2,1)} copy-done((bf16[8,64,192]{2,1,0:T(8,128)(2,1)}, bf16[8,64,192]{2,1,0:T(8,128)(2,1)S(1)}, u32[]{:S(2)}) %copy-start) | copy-done | bytes 196632
  23.2 5.1 %shard_map.30 = bf16[64,128,256]{2,1,0:T(8,128)(2,1)} custom-call(f32[64]{0:T(128)} %taps_ref.1, bf16[512,192]{1,0:T(8,128)(2,1)} %bitcast.3, f32[256,256]{1,0:T(8,128)} %multiply_select_fusion.table_ref), custom_call_target="tpu_custom_call" | custom-call | flops 346030080 | bytes 4653056 | tf_op jit(solution)/shard_map/pallas_call | solution.py:367
  (3 shorter events, 0.1 us)
Async XLA Ops:
  0.0 6.7 %collective-permute-start = (bf16[64,512]{1,0:T(8,128)(2,1)}, bf16[64,512]{1,0:T(8,128)(2,1)S(1)}, u32[]{:S(2)}, u32[]{:S(2)}) collective-permute-start(bf16[64,512]{1,0:T(8,128)(2,1)} %bitcast.4), channel_id=1, source_target_pairs={{1,0},{2,1},{3,2},{5,4},{6,5},{7,6},{9,8},{10,9},{11,10},{13,12},{... | collective-permute-start | bytes 196616 | tf_op jit(solution)/shard_map/ppermute | solution.py:432
  8.8 13.7 %all-to-all-start = ((bf16[8,64,192]{2,1,0:T(8,128)(2,1)}), bf16[8,64,192]{2,1,0:T(8,128)(2,1)S(1)}, u32[]{:S(2)}, u32[]{:S(2)}) async-start(bf16[8,64,192]{2,1,0:T(8,128)(2,1)} %shard_map.29), calls=%async_computation | async-start | bytes 524288 | tf_op jit(solution)/shard_map/all_to_all | solution.py:436
  22.5 0.7 %copy-start = (bf16[8,64,192]{2,1,0:T(8,128)(2,1)}, bf16[8,64,192]{2,1,0:T(8,128)(2,1)S(1)}, u32[]{:S(2)}) copy-start(bf16[8,64,192]{2,1,0:T(8,128)(2,1)S(1)} %all-to-all-done) | copy-start | bytes 589828

commit v11 on v10

--- a/solution.py
+++ b/solution.py
@@ -280,6 +280,22 @@
     )(*pieces)
 
 
+def split_three(values):
+    high = values.astype(jnp.bfloat16)
+    rest = values - high.astype(jnp.float32)
+    middle = rest.astype(jnp.bfloat16)
+    low = (rest - middle.astype(jnp.float32)).astype(jnp.bfloat16)
+    return [high, middle, low]
+
+
+def exact_dot(parts, operand):
+    total = None
+    for part in parts:
+        term = jnp.dot(part, operand, preferred_element_type=jnp.float32)
+        total = term if total is None else total + term
+    return total
+
+
 def fused_kernel(rows, chunk, taps_ref, samples_ref, table_ref, out_hbm, own_f32, shifted,
                  buffers, sems):
     tap_count = taps_ref.shape[0]
@@ -291,35 +307,30 @@
     row = jnp.zeros((1, lanes), jnp.float32)
     for k in range(tap_count):
         row = jnp.where(lane == tap_count - 1 - k, taps_ref[k], row)
-    rolled = pltpu.roll(
-        jnp.broadcast_to(row, (outputs, lanes)), 0, 1, stride=2, stride_axis=0
-    )
-    matrix = rolled[:, : 2 * outputs + tap_count]
-    x = samples_ref[...].astype(jnp.float32)
+    matrices = []
+    for part in split_three(row):
+        rolled = pltpu.roll(
+            jnp.broadcast_to(part.astype(jnp.float32), (outputs, lanes)), 0, 1, stride=2, stride_axis=0
+        )
+        matrices.append(rolled[:, : 2 * outputs + tap_count].astype(jnp.bfloat16))
+    x = samples_ref[...]
     joined = jnp.concatenate(
         [
-            jnp.zeros((tap_count, channels), jnp.float32),
+            jnp.zeros((tap_count, channels), x.dtype),
             x,
-            jnp.zeros((2 * outputs - tap_count, channels), jnp.float32),
+            jnp.zeros((2 * outputs - tap_count, channels), x.dtype),
         ],
         axis=0,
     )
     filtered = jnp.concatenate(
         [
-            jnp.dot(
-                matrix,
-                joined[b * 2 * outputs : b * 2 * outputs + 2 * outputs + tap_count],
-                precision=lax.Precision.HIGHEST,
-                preferred_element_type=jnp.float32,
-            )
+            exact_dot(matrices, joined[b * 2 * outputs : b * 2 * outputs + 2 * outputs + tap_count])
             for b in range(blocks)
         ],
         axis=0,
     )
-    filtered = filtered.astype(jnp.bfloat16).astype(jnp.float32)
-    spectrum = jnp.dot(
-        table_ref[...], filtered, precision=lax.Precision.HIGHEST, preferred_element_type=jnp.float32
-    )
+    filtered = filtered.astype(jnp.bfloat16)
+    spectrum = exact_dot([table_ref[p] for p in range(table_ref.shape[0])], filtered)
     real_part = spectrum[:NF]
     imag_part = spectrum[NF:]
     powers = real_part * real_part + imag_part * imag_part
@@ -378,7 +389,7 @@
         cost_estimate=pl.CostEstimate(
             flops=6 * rows * LAGS * NF + 12 * channels * (NF * 320 * length // 256 + NFFT * NFFT),
             transcendentals=2 * NF * channels,
-            bytes_accessed=rows * LAGS * NFFT * 2 + 2 * samples.size + 4 * table_t.size,
+            bytes_accessed=rows * LAGS * NFFT * 2 + 2 * samples.size + 2 * table_t.size,
         ),
     )(filter_taps, samples, table_t)
 
@@ -436,7 +447,8 @@
     gathered = lax.all_to_all(windows, "ta", split_axis=0, concat_axis=0, tiled=True)
     samples = gathered.reshape(extent * slab, width)
     if extent * slab == 2 * NFFT:
-        return fused_spectra(samples, filter_taps, fourier_table_t(), block_rows)[None]
+        table_parts = jnp.stack(split_three(fourier_table_t()))
+        return fused_spectra(samples, filter_taps, table_parts, block_rows)[None]
     filtered = decimate_t(samples.astype(jnp.float32), filter_taps)
     whitened_t = whiten_t(filtered)
     segments, columns, _ = whitened_t.shape

time: 28.6 us -> 28.4 us (level)
    select_n x1 -> x0, other arithmetic: 2.08 us -> none  [fourier_table_t(): jnp.where(real_rows, window_taper * jnp.cos(angles), -window_taper * jnp....]
    convert_element_type x0 -> x1, other arithmetic: none -> 1.44 us  [split_three(): high = values.astype(jnp.bfloat16)]
    another operation x0 -> x1, other arithmetic: none -> 0.79 us  [body(): table_parts = jnp.stack(split_three(fourier_table_t()))]
where the time goes in v11:
time: 28.4 us; the launch traced here: 28.1 us
  waiting for transfers between devices  8.86 us (31%)
  Pallas kernels  8.09 us (28%)
  starting transfers between devices  7.52 us (26%)
  other arithmetic  2.29 us (8%)
  local copies, waits for them, and re-layouts  1.3 us (5%)
    all_to_all x1, waiting for transfers between devices, body(): lax.all_to_all(windows, 'ta', split_axis=0, concat_axis=0, tiled=True)  5.88 us
    all_to_all x1, starting transfers between devices, body(): lax.all_to_all(windows, 'ta', split_axis=0, concat_axis=0, tiled=True)  5.57 us
    pallas_call x1, Pallas kernels, fused_spectra(): pl.pallas_call(functools.partial(fused_kernel, rows, chunk), out_shape=ja...  4.88 us
    ppermute x1, waiting for transfers between devices, body(): following = lax.ppermute(turned, 'col', route)  2.98 us
    ppermute x1, starting transfers between devices, body(): following = lax.ppermute(turned, 'col', route)  1.96 us
    pallas_call x1, Pallas kernels, channel_windows(): pl.pallas_call(functools.partial(windows_kernel, width, tail_rows), out_s...  1.65 us
    pallas_call x1, Pallas kernels, channel_windows(): pl.pallas_call(functools.partial(tail_windows_kernel, width, count), out_...  1.56 us
    convert_element_type x1, other arithmetic, split_three(): high = values.astype(jnp.bfloat16)  1.44 us
  transfers between devices with their start and end apart: 2, of which 2 were waited for; matrix products, arithmetic and copies ran while one was open for 8% of the time, Pallas kernels for 6%

profile of v11, /device:TPU:1, one launch (start us, length us, event | category | flops | bytes accessed | tf_op | source)
XLA Modules:
  0.0 28.1 jit_solution(15178256860051504496)
XLA Ops:
  0.0 2.0 %collective-permute-start = (bf16[64,512]{1,0:T(8,128)(2,1)}, bf16[64,512]{1,0:T(8,128)(2,1)S(1)}, u32[]{:S(2)}, u32[]{:S(2)}) collective-permute-start(bf16[64,512]{1,0:T(8,128)(2,1)} %bitcast.4), channel_id=1, source_target_pairs={{1,0},{2,1},{3,2},{5,4},{6,5},{7,6},{9,8},{10,9},{11,10},{13,12},{... | collective-permute-start | bytes 196616 | tf_op jit(solution)/shard_map/ppermute | solution.py:443
  2.0 1.6 %shard_map.28.windows_hbm = bf16[8,64,192]{2,1,0:T(8,128)(2,1)} custom-call(bf16[64,512]{1,0:T(8,128)(2,1)} %bitcast.5), custom_call_target="tpu_custom_call" | custom-call | bytes 262144 | tf_op jit(solution)/shard_map/pallas_call | solution.py:111
  3.7 3.0 %collective-permute-done = bf16[64,512]{1,0:T(8,128)(2,1)S(1)} collective-permute-done((bf16[64,512]{1,0:T(8,128)(2,1)}, bf16[64,512]{1,0:T(8,128)(2,1)S(1)}, u32[]{:S(2)}, u32[]{:S(2)}) %collective-permute-start) | collective-permute-done | bytes 65568 | tf_op jit(solution)/shard_map/ppermute | solution.py:443
  6.7 0.6 %slice.4.tail_ref = bf16[64,128]{1,0:T(8,128)(2,1)} slice(bf16[64,512]{1,0:T(8,128)(2,1)S(1)} %collective-permute-done), slice={[0:64], [0:128]} | slice | bytes 32768 | tf_op jit(solution)/shard_map/slice | solution.py:444
  7.3 1.6 %shard_map.29 = bf16[8,64,192]{2,1,0:T(8,128)(2,1)} custom-call(bf16[64,512]{1,0:T(8,128)(2,1)} %bitcast.6, bf16[64,128]{1,0:T(8,128)(2,1)} %slice.4.tail_ref, bf16[8,64,192]{2,1,0:T(8,128)(2,1)} %shard_map.28.windows_hbm), custom_call_target="tpu_custom_call", output_to_operand_aliasing={{}: (2, {})} | custom-call | bytes 163840 | tf_op jit(solution)/shard_map/pallas_call | solution.py:119
  8.8 5.6 %all-to-all-start = ((bf16[8,64,192]{2,1,0:T(8,128)(2,1)}), bf16[8,64,192]{2,1,0:T(8,128)(2,1)S(1)}, u32[]{:S(2)}, u32[]{:S(2)}) async-start(bf16[8,64,192]{2,1,0:T(8,128)(2,1)} %shard_map.29), calls=%async_computation | async-start | bytes 524288 | tf_op jit(solution)/shard_map/all_to_all | solution.py:447
  14.4 1.4 %fusion.4 = (bf16[1,256,256]{2,1,0:T(8,128)(2,1)S(1)}, bf16[1,256,256]{2,1,0:T(8,128)(2,1)S(1)}, bf16[1,256,256]{2,1,0:T(8,128)(2,1)S(1)}) fusion(f32[256]{0:T(256)S(1)} %get-tuple-element.13, s32[256]{0:T(256)S(1)} %get-tuple-element.10, s32[256]{0:T(256)S(1)} %get-tuple-element.11, pred[256]{0:T(512)(128)(4,1)S(1)} %get-tuple-element.8, ...), kind=kLoop, calls=%fused_computation.11 | loop fusion | flops 1703936 | bytes 397824 | tf_op jit(solution)/shard_map/convert_element_type | solution.py:284
  15.8 0.8 %pad_maximum_fusion.table_ref = bf16[3,256,256]{2,1,0:T(8,128)(2,1)} fusion(bf16[1,256,256]{2,1,0:T(8,128)(2,1)S(1)} %get-tuple-element.7, bf16[1,256,256]{2,1,0:T(8,128)(2,1)S(1)} %get-tuple-element.6, bf16[1,256,256]{2,1,0:T(8,128)(2,1)S(1)} %get-tuple-element.5), kind=kLoop, calls=%fused_computation | loop fusion | flops 393216 | bytes 786432 | tf_op jit(solution)/shard_map/stack | solution.py:450
  16.6 5.9 %all-to-all-done = bf16[8,64,192]{2,1,0:T(8,128)(2,1)S(1)} async-done(((bf16[8,64,192]{2,1,0:T(8,128)(2,1)}), bf16[8,64,192]{2,1,0:T(8,128)(2,1)S(1)}, u32[]{:S(2)}, u32[]{:S(2)}) %all-to-all-start) | async-done | bytes 196640 | tf_op jit(solution)/shard_map/all_to_all | solution.py:447
  22.5 0.0 copy-start
  22.5 0.7 %copy-done = bf16[8,64,192]{2,1,0:T(8,128)(2,1)} copy-done((bf16[8,64,192]{2,1,0:T(8,128)(2,1)}, bf16[8,64,192]{2,1,0:T(8,128)(2,1)S(1)}, u32[]{:S(2)}) %copy-start) | copy-done | bytes 196632
  23.2 4.9 %shard_map.30 = bf16[64,128,256]{2,1,0:T(8,128)(2,1)} custom-call(f32[64]{0:T(128)} %taps_ref.1, bf16[512,192]{1,0:T(8,128)(2,1)} %bitcast.3, bf16[3,256,256]{2,1,0:T(8,128)(2,1)} %pad_maximum_fusion.table_ref), custom_call_target="tpu_custom_call" | custom-call | flops 346030080 | bytes 4784128 | tf_op jit(solution)/shard_map/pallas_call | solution.py:378
  (3 shorter events, 0.1 us)
Async XLA Ops:
  0.0 6.7 %collective-permute-start = (bf16[64,512]{1,0:T(8,128)(2,1)}, bf16[64,512]{1,0:T(8,128)(2,1)S(1)}, u32[]{:S(2)}, u32[]{:S(2)}) collective-permute-start(bf16[64,512]{1,0:T(8,128)(2,1)} %bitcast.4), channel_id=1, source_target_pairs={{1,0},{2,1},{3,2},{5,4},{6,5},{7,6},{9,8},{10,9},{11,10},{13,12},{... | collective-permute-start | bytes 196616 | tf_op jit(solution)/shard_map/ppermute | solution.py:443
  8.8 13.7 %all-to-all-start = ((bf16[8,64,192]{2,1,0:T(8,128)(2,1)}), bf16[8,64,192]{2,1,0:T(8,128)(2,1)S(1)}, u32[]{:S(2)}, u32[]{:S(2)}) async-start(bf16[8,64,192]{2,1,0:T(8,128)(2,1)} %shard_map.29), calls=%async_computation | async-start | bytes 524288 | tf_op jit(solution)/shard_map/all_to_all | solution.py:447
  22.5 0.7 %copy-start = (bf16[8,64,192]{2,1,0:T(8,128)(2,1)}, bf16[8,64,192]{2,1,0:T(8,128)(2,1)S(1)}, u32[]{:S(2)}) copy-start(bf16[8,64,192]{2,1,0:T(8,128)(2,1)S(1)} %all-to-all-done) | copy-start | bytes 589828

commit v12 on v11

--- a/solution.py
+++ b/solution.py
@@ -286,6 +286,14 @@
     middle = rest.astype(jnp.bfloat16)
     low = (rest - middle.astype(jnp.float32)).astype(jnp.bfloat16)
     return [high, middle, low]
+
+
+def split_three_kept(values):
+    high = lax.reduce_precision(values, exponent_bits=8, mantissa_bits=7)
+    rest = values - high
+    middle = lax.reduce_precision(rest, exponent_bits=8, mantissa_bits=7)
+    low = rest - middle
+    return [part.astype(jnp.bfloat16) for part in (high, middle, low)]
 
 
 def exact_dot(parts, operand):
@@ -447,7 +455,7 @@
     gathered = lax.all_to_all(windows, "ta", split_axis=0, concat_axis=0, tiled=True)
     samples = gathered.reshape(extent * slab, width)
     if extent * slab == 2 * NFFT:
-        table_parts = jnp.stack(split_three(fourier_table_t()))
+        table_parts = jnp.stack(split_three_kept(fourier_table_t()))
         return fused_spectra(samples, filter_taps, table_parts, block_rows)[None]
     filtered = decimate_t(samples.astype(jnp.float32), filter_taps)
     whitened_t = whiten_t(filtered)

time: 28.4 us -> 28.4 us (level)
  no operation moved by 1% of the time
where the time goes in v12:
time: 28.4 us; the launch traced here: 28.1 us
  waiting for transfers between devices  8.84 us (31%)
  Pallas kernels  8.09 us (28%)
  starting transfers between devices  7.52 us (26%)
  other arithmetic  2.31 us (8%)
  local copies, waits for them, and re-layouts  1.3 us (5%)
    all_to_all x1, waiting for transfers between devices, body(): lax.all_to_all(windows, 'ta', split_axis=0, concat_axis=0, tiled=True)  5.86 us
    all_to_all x1, starting transfers between devices, body(): lax.all_to_all(windows, 'ta', split_axis=0, concat_axis=0, tiled=True)  5.57 us
    pallas_call x1, Pallas kernels, fused_spectra(): pl.pallas_call(functools.partial(fused_kernel, rows, chunk), out_shape=ja...  4.88 us
    ppermute x1, waiting for transfers between devices, body(): following = lax.ppermute(turned, 'col', route)  2.98 us
    ppermute x1, starting transfers between devices, body(): following = lax.ppermute(turned, 'col', route)  1.96 us
    pallas_call x1, Pallas kernels, channel_windows(): pl.pallas_call(functools.partial(windows_kernel, width, tail_rows), out_s...  1.65 us
    pallas_call x1, Pallas kernels, channel_windows(): pl.pallas_call(functools.partial(tail_windows_kernel, width, count), out_...  1.56 us
    convert_element_type x1, other arithmetic, split_three_kept(): return [part.astype(jnp.bfloat16) for part in (high, middle, low)]  1.47 us
  transfers between devices with their start and end apart: 2, of which 2 were waited for; matrix products, arithmetic and copies ran while one was open for 8% of the time, Pallas kernels for 6%

profile of v12, /device:TPU:1, one launch (start us, length us, event | category | flops | bytes accessed | tf_op | source)
XLA Modules:
  0.0 28.1 jit_solution(4108595280441415560)
XLA Ops:
  0.0 2.0 %collective-permute-start = (bf16[64,512]{1,0:T(8,128)(2,1)}, bf16[64,512]{1,0:T(8,128)(2,1)S(1)}, u32[]{:S(2)}, u32[]{:S(2)}) collective-permute-start(bf16[64,512]{1,0:T(8,128)(2,1)} %bitcast.4), channel_id=1, source_target_pairs={{1,0},{2,1},{3,2},{5,4},{6,5},{7,6},{9,8},{10,9},{11,10},{13,12},{... | collective-permute-start | bytes 196616 | tf_op jit(solution)/shard_map/ppermute | solution.py:451
  2.0 1.6 %shard_map.28.windows_hbm = bf16[8,64,192]{2,1,0:T(8,128)(2,1)} custom-call(bf16[64,512]{1,0:T(8,128)(2,1)} %bitcast.5), custom_call_target="tpu_custom_call" | custom-call | bytes 262144 | tf_op jit(solution)/shard_map/pallas_call | solution.py:111
  3.7 3.0 %collective-permute-done = bf16[64,512]{1,0:T(8,128)(2,1)S(1)} collective-permute-done((bf16[64,512]{1,0:T(8,128)(2,1)}, bf16[64,512]{1,0:T(8,128)(2,1)S(1)}, u32[]{:S(2)}, u32[]{:S(2)}) %collective-permute-start) | collective-permute-done | bytes 65568 | tf_op jit(solution)/shard_map/ppermute | solution.py:451
  6.7 0.6 %slice.4.tail_ref = bf16[64,128]{1,0:T(8,128)(2,1)} slice(bf16[64,512]{1,0:T(8,128)(2,1)S(1)} %collective-permute-done), slice={[0:64], [0:128]} | slice | bytes 32768 | tf_op jit(solution)/shard_map/slice | solution.py:452
  7.3 1.6 %shard_map.29 = bf16[8,64,192]{2,1,0:T(8,128)(2,1)} custom-call(bf16[64,512]{1,0:T(8,128)(2,1)} %bitcast.6, bf16[64,128]{1,0:T(8,128)(2,1)} %slice.4.tail_ref, bf16[8,64,192]{2,1,0:T(8,128)(2,1)} %shard_map.28.windows_hbm), custom_call_target="tpu_custom_call", output_to_operand_aliasing={{}: (2, {})} | custom-call | bytes 163840 | tf_op jit(solution)/shard_map/pallas_call | solution.py:119
  8.8 5.6 %all-to-all-start = ((bf16[8,64,192]{2,1,0:T(8,128)(2,1)}), bf16[8,64,192]{2,1,0:T(8,128)(2,1)S(1)}, u32[]{:S(2)}, u32[]{:S(2)}) async-start(bf16[8,64,192]{2,1,0:T(8,128)(2,1)} %shard_map.29), calls=%async_computation | async-start | bytes 524288 | tf_op jit(solution)/shard_map/all_to_all | solution.py:455
  14.4 1.5 %reduce-precision_convert_fusion.1 = (bf16[1,256,256]{2,1,0:T(8,128)(2,1)S(1)}, bf16[1,256,256]{2,1,0:T(8,128)(2,1)S(1)}, bf16[1,256,256]{2,1,0:T(8,128)(2,1)S(1)}) fusion(f32[256]{0:T(256)S(1)} %get-tuple-element.13, s32[256]{0:T(256)S(1)} %get-tuple-element.10, s32[256]{0:T(256)S(1)} %get-tuple-element.11, pred[256]{0:T(512)(128)(4,1)S(1)} %get-tuple-element.8, ...), kind=kLoop, calls=%fused_computation.7 | loop fusion | flops 1703936 | bytes 397824 | tf_op jit(solution)/shard_map/convert_element_type | solution.py:296
  15.9 0.8 %pad_maximum_fusion.table_ref = bf16[3,256,256]{2,1,0:T(8,128)(2,1)} fusion(bf16[1,256,256]{2,1,0:T(8,128)(2,1)S(1)} %get-tuple-element.7, bf16[1,256,256]{2,1,0:T(8,128)(2,1)S(1)} %get-tuple-element.6, bf16[1,256,256]{2,1,0:T(8,128)(2,1)S(1)} %get-tuple-element.5), kind=kLoop, calls=%fused_computation | loop fusion | flops 393216 | bytes 786432 | tf_op jit(solution)/shard_map/stack | solution.py:458
  16.6 5.9 %all-to-all-done = bf16[8,64,192]{2,1,0:T(8,128)(2,1)S(1)} async-done(((bf16[8,64,192]{2,1,0:T(8,128)(2,1)}), bf16[8,64,192]{2,1,0:T(8,128)(2,1)S(1)}, u32[]{:S(2)}, u32[]{:S(2)}) %all-to-all-start) | async-done | bytes 196640 | tf_op jit(solution)/shard_map/all_to_all | solution.py:455
  22.5 0.0 copy-start
  22.5 0.7 %copy-done = bf16[8,64,192]{2,1,0:T(8,128)(2,1)} copy-done((bf16[8,64,192]{2,1,0:T(8,128)(2,1)}, bf16[8,64,192]{2,1,0:T(8,128)(2,1)S(1)}, u32[]{:S(2)}) %copy-start) | copy-done | bytes 196632
  23.2 4.9 %shard_map.30 = bf16[64,128,256]{2,1,0:T(8,128)(2,1)} custom-call(f32[64]{0:T(128)} %taps_ref.1, bf16[512,192]{1,0:T(8,128)(2,1)} %bitcast.3, bf16[3,256,256]{2,1,0:T(8,128)(2,1)} %pad_maximum_fusion.table_ref), custom_call_target="tpu_custom_call" | custom-call | flops 346030080 | bytes 4784128 | tf_op jit(solution)/shard_map/pallas_call | solution.py:386
  (3 shorter events, 0.1 us)
Async XLA Ops:
  0.0 6.7 %collective-permute-start = (bf16[64,512]{1,0:T(8,128)(2,1)}, bf16[64,512]{1,0:T(8,128)(2,1)S(1)}, u32[]{:S(2)}, u32[]{:S(2)}) collective-permute-start(bf16[64,512]{1,0:T(8,128)(2,1)} %bitcast.4), channel_id=1, source_target_pairs={{1,0},{2,1},{3,2},{5,4},{6,5},{7,6},{9,8},{10,9},{11,10},{13,12},{... | collective-permute-start | bytes 196616 | tf_op jit(solution)/shard_map/ppermute | solution.py:451
  8.8 13.7 %all-to-all-start = ((bf16[8,64,192]{2,1,0:T(8,128)(2,1)}), bf16[8,64,192]{2,1,0:T(8,128)(2,1)S(1)}, u32[]{:S(2)}, u32[]{:S(2)}) async-start(bf16[8,64,192]{2,1,0:T(8,128)(2,1)} %shard_map.29), calls=%async_computation | async-start | bytes 524288 | tf_op jit(solution)/shard_map/all_to_all | solution.py:455
  22.5 0.7 %copy-start = (bf16[8,64,192]{2,1,0:T(8,128)(2,1)}, bf16[8,64,192]{2,1,0:T(8,128)(2,1)S(1)}, u32[]{:S(2)}) copy-start(bf16[8,64,192]{2,1,0:T(8,128)(2,1)S(1)} %all-to-all-done) | copy-start | bytes 589828

commit v13 on v12

--- a/solution.py
+++ b/solution.py
@@ -392,7 +392,7 @@
             pltpu.VMEM((rows, NFFT), jnp.float32),
             pltpu.VMEM((chunk, span, NFFT), jnp.float32),
             pltpu.VMEM((4, chunk, LAGS, NFFT), jnp.bfloat16),
-            pltpu.SemaphoreType.DMA((4, 4)),
+            pltpu.SemaphoreType.DMA((4, 8)),
         ],
         cost_estimate=pl.CostEstimate(
             flops=6 * rows * LAGS * NF + 12 * channels * (NF * 320 * length // 256 + NFFT * NFFT),

time: 28.4 us -> 28.6 us (level)
  no operation moved by 1% of the time
where the time goes in v13:
time: 28.6 us; the launch traced here: 28.2 us
  waiting for transfers between devices  8.84 us (31%)
  Pallas kernels  8.21 us (29%)
  starting transfers between devices  7.52 us (26%)
  other arithmetic  2.31 us (8%)
  local copies, waits for them, and re-layouts  1.3 us (5%)
    all_to_all x1, waiting for transfers between devices, body(): lax.all_to_all(windows, 'ta', split_axis=0, concat_axis=0, tiled=True)  5.86 us
    all_to_all x1, starting transfers between devices, body(): lax.all_to_all(windows, 'ta', split_axis=0, concat_axis=0, tiled=True)  5.57 us
    pallas_call x1, Pallas kernels, fused_spectra(): pl.pallas_call(functools.partial(fused_kernel, rows, chunk), out_shape=ja...  5.01 us
    ppermute x1, waiting for transfers between devices, body(): following = lax.ppermute(turned, 'col', route)  2.98 us
    ppermute x1, starting transfers between devices, body(): following = lax.ppermute(turned, 'col', route)  1.96 us
    pallas_call x1, Pallas kernels, channel_windows(): pl.pallas_call(functools.partial(windows_kernel, width, tail_rows), out_s...  1.65 us
    pallas_call x1, Pallas kernels, channel_windows(): pl.pallas_call(functools.partial(tail_windows_kernel, width, count), out_...  1.56 us
    convert_element_type x1, other arithmetic, split_three_kept(): return [part.astype(jnp.bfloat16) for part in (high, middle, low)]  1.47 us
  transfers between devices with their start and end apart: 2, of which 2 were waited for; matrix products, arithmetic and copies ran while one was open for 8% of the time, Pallas kernels for 6%

profile of v13, /device:TPU:1, one launch (start us, length us, event | category | flops | bytes accessed | tf_op | source)
XLA Modules:
  0.0 28.2 jit_solution(17913921797393079386)
XLA Ops:
  0.0 2.0 %collective-permute-start = (bf16[64,512]{1,0:T(8,128)(2,1)}, bf16[64,512]{1,0:T(8,128)(2,1)S(1)}, u32[]{:S(2)}, u32[]{:S(2)}) collective-permute-start(bf16[64,512]{1,0:T(8,128)(2,1)} %bitcast.4), channel_id=1, source_target_pairs={{1,0},{2,1},{3,2},{5,4},{6,5},{7,6},{9,8},{10,9},{11,10},{13,12},{... | collective-permute-start | bytes 196616 | tf_op jit(solution)/shard_map/ppermute | solution.py:451
  2.0 1.6 %shard_map.28.windows_hbm = bf16[8,64,192]{2,1,0:T(8,128)(2,1)} custom-call(bf16[64,512]{1,0:T(8,128)(2,1)} %bitcast.5), custom_call_target="tpu_custom_call" | custom-call | bytes 262144 | tf_op jit(solution)/shard_map/pallas_call | solution.py:111
  3.7 3.0 %collective-permute-done = bf16[64,512]{1,0:T(8,128)(2,1)S(1)} collective-permute-done((bf16[64,512]{1,0:T(8,128)(2,1)}, bf16[64,512]{1,0:T(8,128)(2,1)S(1)}, u32[]{:S(2)}, u32[]{:S(2)}) %collective-permute-start) | collective-permute-done | bytes 65568 | tf_op jit(solution)/shard_map/ppermute | solution.py:451
  6.7 0.6 %slice.4.tail_ref = bf16[64,128]{1,0:T(8,128)(2,1)} slice(bf16[64,512]{1,0:T(8,128)(2,1)S(1)} %collective-permute-done), slice={[0:64], [0:128]} | slice | bytes 32768 | tf_op jit(solution)/shard_map/slice | solution.py:452
  7.3 1.6 %shard_map.29 = bf16[8,64,192]{2,1,0:T(8,128)(2,1)} custom-call(bf16[64,512]{1,0:T(8,128)(2,1)} %bitcast.6, bf16[64,128]{1,0:T(8,128)(2,1)} %slice.4.tail_ref, bf16[8,64,192]{2,1,0:T(8,128)(2,1)} %shard_map.28.windows_hbm), custom_call_target="tpu_custom_call", output_to_operand_aliasing={{}: (2, {})} | custom-call | bytes 163840 | tf_op jit(solution)/shard_map/pallas_call | solution.py:119
  8.8 5.6 %all-to-all-start = ((bf16[8,64,192]{2,1,0:T(8,128)(2,1)}), bf16[8,64,192]{2,1,0:T(8,128)(2,1)S(1)}, u32[]{:S(2)}, u32[]{:S(2)}) async-start(bf16[8,64,192]{2,1,0:T(8,128)(2,1)} %shard_map.29), calls=%async_computation | async-start | bytes 524288 | tf_op jit(solution)/shard_map/all_to_all | solution.py:455
  14.4 1.5 %reduce-precision_convert_fusion.1 = (bf16[1,256,256]{2,1,0:T(8,128)(2,1)S(1)}, bf16[1,256,256]{2,1,0:T(8,128)(2,1)S(1)}, bf16[1,256,256]{2,1,0:T(8,128)(2,1)S(1)}) fusion(f32[256]{0:T(256)S(1)} %get-tuple-element.13, s32[256]{0:T(256)S(1)} %get-tuple-element.10, s32[256]{0:T(256)S(1)} %get-tuple-element.11, pred[256]{0:T(512)(128)(4,1)S(1)} %get-tuple-element.8, ...), kind=kLoop, calls=%fused_computation.7 | loop fusion | flops 1703936 | bytes 397824 | tf_op jit(solution)/shard_map/convert_element_type | solution.py:296
  15.9 0.8 %pad_maximum_fusion.table_ref = bf16[3,256,256]{2,1,0:T(8,128)(2,1)} fusion(bf16[1,256,256]{2,1,0:T(8,128)(2,1)S(1)} %get-tuple-element.7, bf16[1,256,256]{2,1,0:T(8,128)(2,1)S(1)} %get-tuple-element.6, bf16[1,256,256]{2,1,0:T(8,128)(2,1)S(1)} %get-tuple-element.5), kind=kLoop, calls=%fused_computation | loop fusion | flops 393216 | bytes 786432 | tf_op jit(solution)/shard_map/stack | solution.py:458
  16.6 5.9 %all-to-all-done = bf16[8,64,192]{2,1,0:T(8,128)(2,1)S(1)} async-done(((bf16[8,64,192]{2,1,0:T(8,128)(2,1)}), bf16[8,64,192]{2,1,0:T(8,128)(2,1)S(1)}, u32[]{:S(2)}, u32[]{:S(2)}) %all-to-all-start) | async-done | bytes 196640 | tf_op jit(solution)/shard_map/all_to_all | solution.py:455
  22.5 0.0 copy-start
  22.5 0.7 %copy-done = bf16[8,64,192]{2,1,0:T(8,128)(2,1)} copy-done((bf16[8,64,192]{2,1,0:T(8,128)(2,1)}, bf16[8,64,192]{2,1,0:T(8,128)(2,1)S(1)}, u32[]{:S(2)}) %copy-start) | copy-done | bytes 196632
  23.2 5.0 %shard_map.30 = bf16[64,128,256]{2,1,0:T(8,128)(2,1)} custom-call(f32[64]{0:T(128)} %taps_ref.1, bf16[512,192]{1,0:T(8,128)(2,1)} %bitcast.3, bf16[3,256,256]{2,1,0:T(8,128)(2,1)} %pad_maximum_fusion.table_ref), custom_call_target="tpu_custom_call" | custom-call | flops 346030080 | bytes 4784128 | tf_op jit(solution)/shard_map/pallas_call | solution.py:386
  (3 shorter events, 0.1 us)
Async XLA Ops:
  0.0 6.7 %collective-permute-start = (bf16[64,512]{1,0:T(8,128)(2,1)}, bf16[64,512]{1,0:T(8,128)(2,1)S(1)}, u32[]{:S(2)}, u32[]{:S(2)}) collective-permute-start(bf16[64,512]{1,0:T(8,128)(2,1)} %bitcast.4), channel_id=1, source_target_pairs={{1,0},{2,1},{3,2},{5,4},{6,5},{7,6},{9,8},{10,9},{11,10},{13,12},{... | collective-permute-start | bytes 196616 | tf_op jit(solution)/shard_map/ppermute | solution.py:451
  8.8 13.7 %all-to-all-start = ((bf16[8,64,192]{2,1,0:T(8,128)(2,1)}), bf16[8,64,192]{2,1,0:T(8,128)(2,1)S(1)}, u32[]{:S(2)}, u32[]{:S(2)}) async-start(bf16[8,64,192]{2,1,0:T(8,128)(2,1)} %shard_map.29), calls=%async_computation | async-start | bytes 524288 | tf_op jit(solution)/shard_map/all_to_all | solution.py:455
  22.5 0.7 %copy-start = (bf16[8,64,192]{2,1,0:T(8,128)(2,1)}, bf16[8,64,192]{2,1,0:T(8,128)(2,1)S(1)}, u32[]{:S(2)}) copy-start(bf16[8,64,192]{2,1,0:T(8,128)(2,1)S(1)} %all-to-all-done) | copy-start | bytes 589828

commit v14 on v12

--- a/solution.py
+++ b/solution.py
@@ -90,22 +90,6 @@
         out_ref[j] = padded[:, j * step : j * step + width].astype(out_ref.dtype)
 
 
-def tail_windows_kernel(width, count, x_ref, tail_ref, windows_hbm, out_hbm, fresh, sem):
-    del windows_hbm
-    x = x_ref[...].astype(jnp.float32)
-    tail = tail_ref[...].astype(jnp.float32)
-    extent = out_hbm.shape[0]
-    rows = x.shape[1]
-    step = (rows + tail.shape[1] - width) // (extent - 1)
-    first = extent - count
-    padded = jnp.concatenate([x[:, first * step :], tail], axis=1)
-    for j in range(count):
-        fresh[j] = padded[:, j * step : j * step + width].astype(fresh.dtype)
-    copy = pltpu.make_async_copy(fresh, out_hbm.at[pl.ds(first, count)], sem)
-    copy.start()
-    copy.wait()
-
-
 def channel_windows(turned, tail, extent, width, tail_rows):
     slab, rows = turned.shape
     windows = pl.pallas_call(
@@ -115,25 +99,12 @@
             flops=0, transcendentals=0, bytes_accessed=2 * (slab * rows + extent * slab * width)
         ),
     )(turned)
-    count = -(-tail_rows // ((rows + tail_rows - width) // (extent - 1)))
-    return pl.pallas_call(
-        functools.partial(tail_windows_kernel, width, count),
-        out_shape=jax.ShapeDtypeStruct((extent, slab, width), turned.dtype),
-        in_specs=[
-            pl.BlockSpec(memory_space=pltpu.VMEM),
-            pl.BlockSpec(memory_space=pltpu.VMEM),
-            pl.BlockSpec(memory_space=pl.ANY),
-        ],
-        out_specs=pl.BlockSpec(memory_space=pl.ANY),
-        scratch_shapes=[
-            pltpu.VMEM((count, slab, width), turned.dtype),
-            pltpu.SemaphoreType.DMA(()),
-        ],
-        input_output_aliases={2: 0},
-        cost_estimate=pl.CostEstimate(
-            flops=0, transcendentals=0, bytes_accessed=2 * (slab * rows + 2 * count * slab * width)
-        ),
-    )(turned, tail, windows)
+    step = (rows + tail_rows - width) // (extent - 1)
+    count = -(-tail_rows // step)
+    first = extent - count
+    padded = jnp.concatenate([turned[:, first * step :], tail], axis=1)
+    patch = jnp.stack([padded[:, j * step : j * step + width] for j in range(count)])
+    return lax.dynamic_update_slice(windows, patch, (first, 0, 0))
 
 
 def cross_kernel(segments, rows_per_step, own_ref, ext_ref, out_ref):

time: 28.4 us -> 27.4 us (0.965)
  Pallas kernels: 8.09 us -> 6.53 us
  other arithmetic: 2.31 us -> 3.04 us
  waiting for transfers between devices: 8.84 us -> 8.5 us
    pallas_call x1 -> x0, Pallas kernels: 1.56 us -> none  [channel_windows(): pl.pallas_call(functools.partial(tail_windows_kernel, width, count), out_...]
    slice x0 -> x1, local copies, waits for them, and re-layouts: none -> 0.72 us  [channel_windows(): padded = jnp.concatenate([turned[:, first * step:], tail], axis=1)]
    ppermute x1, waiting for transfers between devices: 2.98 us -> 2.26 us  [body(): following = lax.ppermute(turned, 'col', route)]
    dynamic_update_slice x0 -> x1, other arithmetic: none -> 0.65 us  [channel_windows(): return lax.dynamic_update_slice(windows, patch, (first, 0, 0))]
    slice x1, local copies, waits for them, and re-layouts: 0.6 us -> 0.01 us  [body(): tail = following[:, :reach * block_rows]]
    all_to_all x1, waiting for transfers between devices: 5.86 us -> 6.24 us  [body(): lax.all_to_all(windows, 'ta', split_axis=0, concat_axis=0, tiled=True)]
  transfers between devices with their start and end apart: 2 -> 2, of which waited for: 2 -> 2; matrix products, arithmetic and copies ran while one was open for 8% -> 11% of each run, Pallas kernels for 6% -> 6%
where the time goes in v14:
time: 27.4 us; the launch traced here: 27 us
  waiting for transfers between devices  8.5 us (31%)
  starting transfers between devices  7.51 us (27%)
  Pallas kernels  6.53 us (24%)
  other arithmetic  3.04 us (11%)
  local copies, waits for them, and re-layouts  1.42 us (5%)
    all_to_all x1, waiting for transfers between devices, body(): lax.all_to_all(windows, 'ta', split_axis=0, concat_axis=0, tiled=True)  6.24 us
    all_to_all x1, starting transfers between devices, body(): lax.all_to_all(windows, 'ta', split_axis=0, concat_axis=0, tiled=True)  5.55 us
    pallas_call x1, Pallas kernels, fused_spectra(): pl.pallas_call(functools.partial(fused_kernel, rows, chunk), out_shape=ja...  4.88 us
    ppermute x1, waiting for transfers between devices, body(): following = lax.ppermute(turned, 'col', route)  2.26 us
    ppermute x1, starting transfers between devices, body(): following = lax.ppermute(turned, 'col', route)  1.96 us
    pallas_call x1, Pallas kernels, channel_windows(): pl.pallas_call(functools.partial(windows_kernel, width, tail_rows), out_s...  1.64 us
    convert_element_type x1, other arithmetic, split_three_kept(): return [part.astype(jnp.bfloat16) for part in (high, middle, low)]  1.47 us
    another operation x1, other arithmetic, body(): table_parts = jnp.stack(split_three_kept(fourier_table_t()))  0.79 us
  transfers between devices with their start and end apart: 2, of which 2 were waited for; matrix products, arithmetic and copies ran while one was open for 11% of the time, Pallas kernels for 6%

profile of v14, /device:TPU:1, one launch (start us, length us, event | category | flops | bytes accessed | tf_op | source)
XLA Modules:
  0.0 27.0 jit_solution(8893221150884047927)
XLA Ops:
  0.0 2.0 %collective-permute-start = (bf16[64,512]{1,0:T(8,128)(2,1)}, bf16[64,512]{1,0:T(8,128)(2,1)S(1)}, u32[]{:S(2)}, u32[]{:S(2)}) collective-permute-start(bf16[64,512]{1,0:T(8,128)(2,1)} %bitcast.8), channel_id=1, source_target_pairs={{1,0},{2,1},{3,2},{5,4},{6,5},{7,6},{9,8},{10,9},{11,10},{13,12},{... | collective-permute-start | bytes 196616 | tf_op jit(solution)/shard_map/ppermute | solution.py:422
  2.0 0.7 %slice.16 = bf16[64,128]{1,0:T(8,128)(2,1)S(1)} slice(bf16[64,512]{1,0:T(8,128)(2,1)} %bitcast.9), slice={[0:64], [384:512]} | slice | bytes 32768 | tf_op jit(solution)/shard_map/slice | solution.py:105
  2.7 1.6 %shard_map.28 = bf16[8,64,192]{2,1,0:T(8,128)(2,1)} custom-call(bf16[64,512]{1,0:T(8,128)(2,1)} %bitcast.10), custom_call_target="tpu_custom_call" | custom-call | bytes 262144 | tf_op jit(solution)/shard_map/pallas_call | solution.py:95
  4.4 2.3 %collective-permute-done = bf16[64,512]{1,0:T(8,128)(2,1)S(1)} collective-permute-done((bf16[64,512]{1,0:T(8,128)(2,1)}, bf16[64,512]{1,0:T(8,128)(2,1)S(1)}, u32[]{:S(2)}, u32[]{:S(2)}) %collective-permute-start) | collective-permute-done | bytes 65568 | tf_op jit(solution)/shard_map/ppermute | solution.py:422
  6.7 0.1 maximum_bitcast_fusion
  6.7 0.6 %maximum_dynamic-update-slice_fusion = bf16[8,64,192]{2,1,0:T(8,128)(2,1)} fusion(bf16[8,64,192]{2,1,0:T(8,128)(2,1)} %shard_map.28, bf16[1,64,192]{2,1,0:T(8,128)(2,1)S(1)} %get-tuple-element.6, bf16[1,64,192]{2,1,0:T(8,128)(2,1)S(1)} %get-tuple-element.5), kind=kLoop, calls=%fused_computation.13 | loop fusion | flops 98304 | bytes 114688 | tf_op jit(solution)/shard_map/dynamic_update_slice | solution.py:107
  7.4 5.6 %all-to-all-start = ((bf16[8,64,192]{2,1,0:T(8,128)(2,1)}), bf16[8,64,192]{2,1,0:T(8,128)(2,1)S(1)}, u32[]{:S(2)}, u32[]{:S(2)}) async-start(bf16[8,64,192]{2,1,0:T(8,128)(2,1)} %maximum_dynamic-update-slice_fusion), calls=%async_computation | async-start | bytes 524288 | tf_op jit(solution)/shard_map/all_to_all | solution.py:426
  12.9 1.5 %reduce-precision_convert_fusion.1 = (bf16[1,256,256]{2,1,0:T(8,128)(2,1)S(1)}, bf16[1,256,256]{2,1,0:T(8,128)(2,1)S(1)}, bf16[1,256,256]{2,1,0:T(8,128)(2,1)S(1)}) fusion(f32[256]{0:T(256)S(1)} %get-tuple-element.15, s32[256]{0:T(256)S(1)} %get-tuple-element.12, s32[256]{0:T(256)S(1)} %get-tuple-element.13, pred[256]{0:T(512)(128)(4,1)S(1)} %get-tuple-element.10, ...), kind=kLoop, calls=%fused_computation.7 | loop fusion | flops 1703936 | bytes 397824 | tf_op jit(solution)/shard_map/convert_element_type | solution.py:267
  14.4 0.8 %pad_maximum_fusion.table_ref = bf16[3,256,256]{2,1,0:T(8,128)(2,1)} fusion(bf16[1,256,256]{2,1,0:T(8,128)(2,1)S(1)} %get-tuple-element.9, bf16[1,256,256]{2,1,0:T(8,128)(2,1)S(1)} %get-tuple-element.8, bf16[1,256,256]{2,1,0:T(8,128)(2,1)S(1)} %get-tuple-element.7), kind=kLoop, calls=%fused_computation | loop fusion | flops 393216 | bytes 786432 | tf_op jit(solution)/shard_map/stack | solution.py:429
  15.2 6.2 %all-to-all-done = bf16[8,64,192]{2,1,0:T(8,128)(2,1)S(1)} async-done(((bf16[8,64,192]{2,1,0:T(8,128)(2,1)}), bf16[8,64,192]{2,1,0:T(8,128)(2,1)S(1)}, u32[]{:S(2)}, u32[]{:S(2)}) %all-to-all-start) | async-done | bytes 196640 | tf_op jit(solution)/shard_map/all_to_all | solution.py:426
  21.5 0.0 copy-start
  21.5 0.7 %copy-done = bf16[8,64,192]{2,1,0:T(8,128)(2,1)} copy-done((bf16[8,64,192]{2,1,0:T(8,128)(2,1)}, bf16[8,64,192]{2,1,0:T(8,128)(2,1)S(1)}, u32[]{:S(2)}) %copy-start) | copy-done | bytes 196632
  22.1 4.9 %shard_map.29 = bf16[64,128,256]{2,1,0:T(8,128)(2,1)} custom-call(f32[64]{0:T(128)} %taps_ref.1, bf16[512,192]{1,0:T(8,128)(2,1)} %bitcast.7, bf16[3,256,256]{2,1,0:T(8,128)(2,1)} %pad_maximum_fusion.table_ref), custom_call_target="tpu_custom_call" | custom-call | flops 346030080 | bytes 4784128 | tf_op jit(solution)/shard_map/pallas_call | solution.py:357
  (4 shorter events, 0.1 us)
Async XLA Ops:
  0.0 6.7 %collective-permute-start = (bf16[64,512]{1,0:T(8,128)(2,1)}, bf16[64,512]{1,0:T(8,128)(2,1)S(1)}, u32[]{:S(2)}, u32[]{:S(2)}) collective-permute-start(bf16[64,512]{1,0:T(8,128)(2,1)} %bitcast.8), channel_id=1, source_target_pairs={{1,0},{2,1},{3,2},{5,4},{6,5},{7,6},{9,8},{10,9},{11,10},{13,12},{... | collective-permute-start | bytes 196616 | tf_op jit(solution)/shard_map/ppermute | solution.py:422
  7.4 14.1 %all-to-all-start = ((bf16[8,64,192]{2,1,0:T(8,128)(2,1)}), bf16[8,64,192]{2,1,0:T(8,128)(2,1)S(1)}, u32[]{:S(2)}, u32[]{:S(2)}) async-start(bf16[8,64,192]{2,1,0:T(8,128)(2,1)} %maximum_dynamic-update-slice_fusion), calls=%async_computation | async-start | bytes 524288 | tf_op jit(solution)/shard_map/all_to_all | solution.py:426
  21.5 0.7 %copy-start = (bf16[8,64,192]{2,1,0:T(8,128)(2,1)}, bf16[8,64,192]{2,1,0:T(8,128)(2,1)S(1)}, u32[]{:S(2)}) copy-start(bf16[8,64,192]{2,1,0:T(8,128)(2,1)S(1)} %all-to-all-done) | copy-start | bytes 589828

commit v15 on v14

--- a/solution.py
+++ b/solution.py
@@ -102,9 +102,10 @@
     step = (rows + tail_rows - width) // (extent - 1)
     count = -(-tail_rows // step)
     first = extent - count
-    padded = jnp.concatenate([turned[:, first * step :], tail], axis=1)
-    patch = jnp.stack([padded[:, j * step : j * step + width] for j in range(count)])
-    return lax.dynamic_update_slice(windows, patch, (first, 0, 0))
+    for j in range(first, extent):
+        offset = rows - j * step
+        windows = lax.dynamic_update_slice(windows, tail[None, :, : width - offset], (j, 0, offset))
+    return windows
 
 
 def cross_kernel(segments, rows_per_step, own_ref, ext_ref, out_ref):

time: 27.4 us -> 28.4 us (1.036)
  local copies, waits for them, and re-layouts: 1.42 us -> 2.86 us
  other arithmetic: 3.04 us -> 2.31 us
  waiting for transfers between devices: 8.5 us -> 8.84 us
    dynamic_update_slice x0 -> x2, local copies, waits for them, and re-layouts: none -> 2.16 us  [channel_windows(): lax.dynamic_update_slice(windows, tail[None, :, :width - offset], (j, 0,...]
    slice x2 -> x0, local copies, waits for them, and re-layouts: 0.73 us -> none  [the longest x1 0.72 us: channel_windows(): padded = jnp.concatenate([turned[:, first * step:], tail], axis=1)]
    ppermute x1, waiting for transfers between devices: 2.26 us -> 2.98 us  [body(): following = lax.ppermute(turned, 'col', route)]
    dynamic_update_slice x1 -> x0, other arithmetic: 0.65 us -> none  [channel_windows(): return lax.dynamic_update_slice(windows, patch, (first, 0, 0))]
    all_to_all x1, waiting for transfers between devices: 6.24 us -> 5.86 us  [body(): lax.all_to_all(windows, 'ta', split_axis=0, concat_axis=0, tiled=True)]
  transfers between devices with their start and end apart: 2 -> 2, of which waited for: 2 -> 2; matrix products, arithmetic and copies ran while one was open for 11% -> 8% of each run, Pallas kernels for 6% -> 6%
where the time goes in v15:
time: 28.4 us; the launch traced here: 28.1 us
  waiting for transfers between devices  8.84 us (31%)
  starting transfers between devices  7.51 us (26%)
  Pallas kernels  6.53 us (23%)
  local copies, waits for them, and re-layouts  2.86 us (10%)
  other arithmetic  2.31 us (8%)
    all_to_all x1, waiting for transfers between devices, body(): lax.all_to_all(windows, 'ta', split_axis=0, concat_axis=0, tiled=True)  5.86 us
    all_to_all x1, starting transfers between devices, body(): lax.all_to_all(windows, 'ta', split_axis=0, concat_axis=0, tiled=True)  5.55 us
    pallas_call x1, Pallas kernels, fused_spectra(): pl.pallas_call(functools.partial(fused_kernel, rows, chunk), out_shape=ja...  4.88 us
    ppermute x1, waiting for transfers between devices, body(): following = lax.ppermute(turned, 'col', route)  2.98 us
    dynamic_update_slice x2, local copies, waits for them, and re-layouts, channel_windows(): lax.dynamic_update_slice(windows, tail[None, :, :width - offset], (j, 0,...  2.16 us
    ppermute x1, starting transfers between devices, body(): following = lax.ppermute(turned, 'col', route)  1.96 us
    pallas_call x1, Pallas kernels, channel_windows(): pl.pallas_call(functools.partial(windows_kernel, width, tail_rows), out_s...  1.65 us
    convert_element_type x1, other arithmetic, split_three_kept(): return [part.astype(jnp.bfloat16) for part in (high, middle, low)]  1.47 us
  transfers between devices with their start and end apart: 2, of which 2 were waited for; matrix products, arithmetic and copies ran while one was open for 8% of the time, Pallas kernels for 6%

profile of v15, /device:TPU:1, one launch (start us, length us, event | category | flops | bytes accessed | tf_op | source)
XLA Modules:
  0.0 28.1 jit_solution(14950160324790607747)
XLA Ops:
  0.0 2.0 %collective-permute-start = (bf16[64,512]{1,0:T(8,128)(2,1)}, bf16[64,512]{1,0:T(8,128)(2,1)S(1)}, u32[]{:S(2)}, u32[]{:S(2)}) collective-permute-start(bf16[64,512]{1,0:T(8,128)(2,1)} %bitcast.10), channel_id=1, source_target_pairs={{1,0},{2,1},{3,2},{5,4},{6,5},{7,6},{9,8},{10,9},{11,10},{13,12},{... | collective-permute-start | bytes 196616 | tf_op jit(solution)/shard_map/ppermute | solution.py:423
  2.0 1.6 %shard_map.28 = bf16[8,64,192]{2,1,0:T(8,128)(2,1)} custom-call(bf16[64,512]{1,0:T(8,128)(2,1)} %bitcast.11), custom_call_target="tpu_custom_call" | custom-call | bytes 262144 | tf_op jit(solution)/shard_map/pallas_call | solution.py:95
  3.7 3.0 %collective-permute-done = bf16[64,512]{1,0:T(8,128)(2,1)S(1)} collective-permute-done((bf16[64,512]{1,0:T(8,128)(2,1)}, bf16[64,512]{1,0:T(8,128)(2,1)S(1)}, u32[]{:S(2)}, u32[]{:S(2)}) %collective-permute-start) | collective-permute-done | bytes 65568 | tf_op jit(solution)/shard_map/ppermute | solution.py:423
  6.7 0.6 %fusion.4 = bf16[8,64,192]{2,1,0:T(8,128)(2,1)} fusion(bf16[8,64,192]{2,1,0:T(8,128)(2,1)} %shard_map.28, bf16[64,512]{1,0:T(8,128)(2,1)S(1)} %collective-permute-done), kind=kLoop, calls=%fused_computation.15 | loop fusion | bytes 24576 | tf_op jit(solution)/shard_map/dynamic_update_slice | solution.py:107
  7.3 1.6 %dynamic_update_slice.7 = bf16[8,64,192]{2,1,0:T(8,128)(2,1)} dynamic-update-slice(bf16[8,64,192]{2,1,0:T(8,128)(2,1)} %fusion.4, bf16[1,64,128]{2,1,0:T(8,128)(2,1)S(1)} %slice_bitcast_fusion, s32[]{:T(128)} %constant.33.clone.1, s32[]{:T(128)} %constant.31.clone.1, s32[]{:T(128)} %constant.34.clone.1) | dynamic-update-slice | bytes 32772 | tf_op jit(solution)/shard_map/dynamic_update_slice | solution.py:107
  8.8 5.6 %all-to-all-start = ((bf16[8,64,192]{2,1,0:T(8,128)(2,1)}), bf16[8,64,192]{2,1,0:T(8,128)(2,1)S(1)}, u32[]{:S(2)}, u32[]{:S(2)}) async-start(bf16[8,64,192]{2,1,0:T(8,128)(2,1)} %dynamic_update_slice.7), calls=%async_computation | async-start | bytes 524288 | tf_op jit(solution)/shard_map/all_to_all | solution.py:427
  14.4 1.5 %reduce-precision_convert_fusion.1 = (bf16[1,256,256]{2,1,0:T(8,128)(2,1)S(1)}, bf16[1,256,256]{2,1,0:T(8,128)(2,1)S(1)}, bf16[1,256,256]{2,1,0:T(8,128)(2,1)S(1)}) fusion(f32[256]{0:T(256)S(1)} %get-tuple-element.13, s32[256]{0:T(256)S(1)} %get-tuple-element.10, s32[256]{0:T(256)S(1)} %get-tuple-element.11, pred[256]{0:T(512)(128)(4,1)S(1)} %get-tuple-element.8, ...), kind=kLoop, calls=%fused_computation.7 | loop fusion | flops 1703936 | bytes 397824 | tf_op jit(solution)/shard_map/convert_element_type | solution.py:268
  15.8 0.8 %pad_maximum_fusion.table_ref = bf16[3,256,256]{2,1,0:T(8,128)(2,1)} fusion(bf16[1,256,256]{2,1,0:T(8,128)(2,1)S(1)} %get-tuple-element.7, bf16[1,256,256]{2,1,0:T(8,128)(2,1)S(1)} %get-tuple-element.6, bf16[1,256,256]{2,1,0:T(8,128)(2,1)S(1)} %get-tuple-element.5), kind=kLoop, calls=%fused_computation | loop fusion | flops 393216 | bytes 786432 | tf_op jit(solution)/shard_map/stack | solution.py:430
  16.6 5.9 %all-to-all-done = bf16[8,64,192]{2,1,0:T(8,128)(2,1)S(1)} async-done(((bf16[8,64,192]{2,1,0:T(8,128)(2,1)}), bf16[8,64,192]{2,1,0:T(8,128)(2,1)S(1)}, u32[]{:S(2)}, u32[]{:S(2)}) %all-to-all-start) | async-done | bytes 196640 | tf_op jit(solution)/shard_map/all_to_all | solution.py:427
  22.5 0.0 copy-start
  22.5 0.7 %copy-done = bf16[8,64,192]{2,1,0:T(8,128)(2,1)} copy-done((bf16[8,64,192]{2,1,0:T(8,128)(2,1)}, bf16[8,64,192]{2,1,0:T(8,128)(2,1)S(1)}, u32[]{:S(2)}) %copy-start) | copy-done | bytes 196632
  23.2 4.9 %shard_map.29 = bf16[64,128,256]{2,1,0:T(8,128)(2,1)} custom-call(f32[64]{0:T(128)} %taps_ref.1, bf16[512,192]{1,0:T(8,128)(2,1)} %bitcast.9, bf16[3,256,256]{2,1,0:T(8,128)(2,1)} %pad_maximum_fusion.table_ref), custom_call_target="tpu_custom_call" | custom-call | flops 346030080 | bytes 4784128 | tf_op jit(solution)/shard_map/pallas_call | solution.py:358
  (4 shorter events, 0.1 us)
Async XLA Ops:
  0.0 6.7 %collective-permute-start = (bf16[64,512]{1,0:T(8,128)(2,1)}, bf16[64,512]{1,0:T(8,128)(2,1)S(1)}, u32[]{:S(2)}, u32[]{:S(2)}) collective-permute-start(bf16[64,512]{1,0:T(8,128)(2,1)} %bitcast.10), channel_id=1, source_target_pairs={{1,0},{2,1},{3,2},{5,4},{6,5},{7,6},{9,8},{10,9},{11,10},{13,12},{... | collective-permute-start | bytes 196616 | tf_op jit(solution)/shard_map/ppermute | solution.py:423
  8.8 13.7 %all-to-all-start = ((bf16[8,64,192]{2,1,0:T(8,128)(2,1)}), bf16[8,64,192]{2,1,0:T(8,128)(2,1)S(1)}, u32[]{:S(2)}, u32[]{:S(2)}) async-start(bf16[8,64,192]{2,1,0:T(8,128)(2,1)} %dynamic_update_slice.7), calls=%async_computation | async-start | bytes 524288 | tf_op jit(solution)/shard_map/all_to_all | solution.py:427
  22.5 0.7 %copy-start = (bf16[8,64,192]{2,1,0:T(8,128)(2,1)}, bf16[8,64,192]{2,1,0:T(8,128)(2,1)S(1)}, u32[]{:S(2)}) copy-start(bf16[8,64,192]{2,1,0:T(8,128)(2,1)S(1)} %all-to-all-done) | copy-start | bytes 589828

commit v16 on v14

--- a/solution.py
+++ b/solution.py
@@ -82,27 +82,31 @@
     )
 
 
-def windows_kernel(width, tail_rows, x_ref, out_ref):
+def windows_kernel(width, tail_rows, x_ref, out_ref, last_ref):
     x = x_ref[...].astype(jnp.float32)
     padded = jnp.concatenate([x, jnp.zeros((x.shape[0], tail_rows), jnp.float32)], axis=1)
     step = (padded.shape[1] - width) // (out_ref.shape[0] - 1)
     for j in range(out_ref.shape[0]):
         out_ref[j] = padded[:, j * step : j * step + width].astype(out_ref.dtype)
+    last_ref[...] = x[:, x.shape[1] - last_ref.shape[1] :].astype(last_ref.dtype)
 
 
 def channel_windows(turned, tail, extent, width, tail_rows):
     slab, rows = turned.shape
-    windows = pl.pallas_call(
+    step = (rows + tail_rows - width) // (extent - 1)
+    count = -(-tail_rows // step)
+    first = extent - count
+    windows, last = pl.pallas_call(
         functools.partial(windows_kernel, width, tail_rows),
-        out_shape=jax.ShapeDtypeStruct((extent, slab, width), turned.dtype),
+        out_shape=(
+            jax.ShapeDtypeStruct((extent, slab, width), turned.dtype),
+            jax.ShapeDtypeStruct((slab, rows - first * step), turned.dtype),
+        ),
         cost_estimate=pl.CostEstimate(
             flops=0, transcendentals=0, bytes_accessed=2 * (slab * rows + extent * slab * width)
         ),
     )(turned)
-    step = (rows + tail_rows - width) // (extent - 1)
-    count = -(-tail_rows // step)
-    first = extent - count
-    padded = jnp.concatenate([turned[:, first * step :], tail], axis=1)
+    padded = jnp.concatenate([last, tail], axis=1)
     patch = jnp.stack([padded[:, j * step : j * step + width] for j in range(count)])
     return lax.dynamic_update_slice(windows, patch, (first, 0, 0))
 

time: 27.4 us -> 27.8 us (1.015)
  other arithmetic: 3.04 us -> 3.82 us
  local copies, waits for them, and re-layouts: 1.42 us -> 0.69 us
  waiting for transfers between devices: 8.5 us -> 8.85 us
    another operation x1, other arithmetic: 0.09 us -> 0.88 us  [channel_windows(): jnp.stack([padded[:, j * step:j * step + width] for j in range(count)])]
    slice x1 -> x0, local copies, waits for them, and re-layouts: 0.72 us -> none  [channel_windows(): padded = jnp.concatenate([turned[:, first * step:], tail], axis=1)]
    ppermute x1, waiting for transfers between devices: 2.26 us -> 2.98 us  [body(): following = lax.ppermute(turned, 'col', route)]
    all_to_all x1, waiting for transfers between devices: 6.24 us -> 5.87 us  [body(): lax.all_to_all(windows, 'ta', split_axis=0, concat_axis=0, tiled=True)]
  transfers between devices with their start and end apart: 2 -> 2, of which waited for: 2 -> 2; matrix products, arithmetic and copies ran while one was open for 11% -> 8% of each run, Pallas kernels for 6% -> 6%
where the time goes in v16:
time: 27.8 us; the launch traced here: 27.4 us
  waiting for transfers between devices  8.85 us (32%)
  starting transfers between devices  7.51 us (27%)
  Pallas kernels  6.53 us (23%)
  other arithmetic  3.82 us (14%)
  local copies, waits for them, and re-layouts  0.69 us (2%)
    all_to_all x1, waiting for transfers between devices, body(): lax.all_to_all(windows, 'ta', split_axis=0, concat_axis=0, tiled=True)  5.87 us
    all_to_all x1, starting transfers between devices, body(): lax.all_to_all(windows, 'ta', split_axis=0, concat_axis=0, tiled=True)  5.55 us
    pallas_call x1, Pallas kernels, fused_spectra(): pl.pallas_call(functools.partial(fused_kernel, rows, chunk), out_shape=ja...  4.88 us
    ppermute x1, waiting for transfers between devices, body(): following = lax.ppermute(turned, 'col', route)  2.98 us
    ppermute x1, starting transfers between devices, body(): following = lax.ppermute(turned, 'col', route)  1.96 us
    pallas_call x1, Pallas kernels, channel_windows(): pl.pallas_call(functools.partial(windows_kernel, width, tail_rows), out_s...  1.65 us
    convert_element_type x1, other arithmetic, split_three_kept(): return [part.astype(jnp.bfloat16) for part in (high, middle, low)]  1.47 us
    another operation x1, other arithmetic, channel_windows(): jnp.stack([padded[:, j * step:j * step + width] for j in range(count)])  0.88 us
  transfers between devices with their start and end apart: 2, of which 2 were waited for; matrix products, arithmetic and copies ran while one was open for 8% of the time, Pallas kernels for 6%

profile of v16, /device:TPU:1, one launch (start us, length us, event | category | flops | bytes accessed | tf_op | source)
XLA Modules:
  0.0 27.4 jit_solution(2378250923356284132)
XLA Ops:
  0.0 2.0 %collective-permute-start = (bf16[64,512]{1,0:T(8,128)(2,1)}, bf16[64,512]{1,0:T(8,128)(2,1)S(1)}, u32[]{:S(2)}, u32[]{:S(2)}) collective-permute-start(bf16[64,512]{1,0:T(8,128)(2,1)} %bitcast.8), channel_id=1, source_target_pairs={{1,0},{2,1},{3,2},{5,4},{6,5},{7,6},{9,8},{10,9},{11,10},{13,12},{... | collective-permute-start | bytes 196616 | tf_op jit(solution)/shard_map/ppermute | solution.py:426
  2.0 1.6 %shard_map.28 = (bf16[8,64,192]{2,1,0:T(8,128)(2,1)}, bf16[64,128]{1,0:T(8,128)(2,1)}) custom-call(bf16[64,512]{1,0:T(8,128)(2,1)} %bitcast.9), custom_call_target="tpu_custom_call" | custom-call | bytes 262144 | tf_op jit(solution)/shard_map/pallas_call | solution.py:99
  3.7 3.0 %collective-permute-done = bf16[64,512]{1,0:T(8,128)(2,1)S(1)} collective-permute-done((bf16[64,512]{1,0:T(8,128)(2,1)}, bf16[64,512]{1,0:T(8,128)(2,1)S(1)}, u32[]{:S(2)}, u32[]{:S(2)}) %collective-permute-start) | collective-permute-done | bytes 65568 | tf_op jit(solution)/shard_map/ppermute | solution.py:426
  6.7 0.9 %maximum_bitcast_fusion = (bf16[1,64,192]{2,1,0:T(8,128)(2,1)S(1)}, bf16[1,64,192]{2,1,0:T(8,128)(2,1)S(1)}) fusion(bf16[64,128]{1,0:T(8,128)(2,1)S(1)} %slice.12, bf16[64,128]{1,0:T(8,128)(2,1)} %get-tuple-element.8), kind=kLoop, calls=%fused_computation.16 | loop fusion | flops 98304 | bytes 81920 | tf_op jit(solution)/shard_map/stack | solution.py:110
  7.5 0.6 %maximum_dynamic-update-slice_fusion = bf16[8,64,192]{2,1,0:T(8,128)(2,1)} fusion(bf16[8,64,192]{2,1,0:T(8,128)(2,1)} %get-tuple-element.7, bf16[1,64,192]{2,1,0:T(8,128)(2,1)S(1)} %get-tuple-element.10, bf16[1,64,192]{2,1,0:T(8,128)(2,1)S(1)} %get-tuple-element.9), kind=kLoop, calls=%fused_computation.13 | loop fusion | flops 98304 | bytes 114688 | tf_op jit(solution)/shard_map/dynamic_update_slice | solution.py:111
  8.2 5.6 %all-to-all-start = ((bf16[8,64,192]{2,1,0:T(8,128)(2,1)}), bf16[8,64,192]{2,1,0:T(8,128)(2,1)S(1)}, u32[]{:S(2)}, u32[]{:S(2)}) async-start(bf16[8,64,192]{2,1,0:T(8,128)(2,1)} %maximum_dynamic-update-slice_fusion), calls=%async_computation | async-start | bytes 524288 | tf_op jit(solution)/shard_map/all_to_all | solution.py:430
  13.7 1.5 %reduce-precision_convert_fusion.1 = (bf16[1,256,256]{2,1,0:T(8,128)(2,1)S(1)}, bf16[1,256,256]{2,1,0:T(8,128)(2,1)S(1)}, bf16[1,256,256]{2,1,0:T(8,128)(2,1)S(1)}) fusion(f32[256]{0:T(256)S(1)} %get-tuple-element.19, s32[256]{0:T(256)S(1)} %get-tuple-element.16, s32[256]{0:T(256)S(1)} %get-tuple-element.17, pred[256]{0:T(512)(128)(4,1)S(1)} %get-tuple-element.14, ...), kind=kLoop, calls=%fused_computation.7 | loop fusion | flops 1703936 | bytes 397824 | tf_op jit(solution)/shard_map/convert_element_type | solution.py:271
  15.2 0.8 %pad_maximum_fusion.table_ref = bf16[3,256,256]{2,1,0:T(8,128)(2,1)} fusion(bf16[1,256,256]{2,1,0:T(8,128)(2,1)S(1)} %get-tuple-element.13, bf16[1,256,256]{2,1,0:T(8,128)(2,1)S(1)} %get-tuple-element.12, bf16[1,256,256]{2,1,0:T(8,128)(2,1)S(1)} %get-tuple-element.11), kind=kLoop, calls=%fused_computation | loop fusion | flops 393216 | bytes 786432 | tf_op jit(solution)/shard_map/stack | solution.py:433
  16.0 5.9 %all-to-all-done = bf16[8,64,192]{2,1,0:T(8,128)(2,1)S(1)} async-done(((bf16[8,64,192]{2,1,0:T(8,128)(2,1)}), bf16[8,64,192]{2,1,0:T(8,128)(2,1)S(1)}, u32[]{:S(2)}, u32[]{:S(2)}) %all-to-all-start) | async-done | bytes 196640 | tf_op jit(solution)/shard_map/all_to_all | solution.py:430
  21.9 0.0 copy-start
  21.9 0.7 %copy-done = bf16[8,64,192]{2,1,0:T(8,128)(2,1)} copy-done((bf16[8,64,192]{2,1,0:T(8,128)(2,1)}, bf16[8,64,192]{2,1,0:T(8,128)(2,1)S(1)}, u32[]{:S(2)}) %copy-start) | copy-done | bytes 196632
  22.6 4.9 %shard_map.29 = bf16[64,128,256]{2,1,0:T(8,128)(2,1)} custom-call(f32[64]{0:T(128)} %taps_ref.1, bf16[512,192]{1,0:T(8,128)(2,1)} %bitcast.7, bf16[3,256,256]{2,1,0:T(8,128)(2,1)} %pad_maximum_fusion.table_ref), custom_call_target="tpu_custom_call" | custom-call | flops 346030080 | bytes 4784128 | tf_op jit(solution)/shard_map/pallas_call | solution.py:361
  (4 shorter events, 0.1 us)
Async XLA Ops:
  0.0 6.7 %collective-permute-start = (bf16[64,512]{1,0:T(8,128)(2,1)}, bf16[64,512]{1,0:T(8,128)(2,1)S(1)}, u32[]{:S(2)}, u32[]{:S(2)}) collective-permute-start(bf16[64,512]{1,0:T(8,128)(2,1)} %bitcast.8), channel_id=1, source_target_pairs={{1,0},{2,1},{3,2},{5,4},{6,5},{7,6},{9,8},{10,9},{11,10},{13,12},{... | collective-permute-start | bytes 196616 | tf_op jit(solution)/shard_map/ppermute | solution.py:426
  8.2 13.7 %all-to-all-start = ((bf16[8,64,192]{2,1,0:T(8,128)(2,1)}), bf16[8,64,192]{2,1,0:T(8,128)(2,1)S(1)}, u32[]{:S(2)}, u32[]{:S(2)}) async-start(bf16[8,64,192]{2,1,0:T(8,128)(2,1)} %maximum_dynamic-update-slice_fusion), calls=%async_computation | async-start | bytes 524288 | tf_op jit(solution)/shard_map/all_to_all | solution.py:430
  21.9 0.7 %copy-start = (bf16[8,64,192]{2,1,0:T(8,128)(2,1)}, bf16[8,64,192]{2,1,0:T(8,128)(2,1)S(1)}, u32[]{:S(2)}) copy-start(bf16[8,64,192]{2,1,0:T(8,128)(2,1)S(1)} %all-to-all-done) | copy-start | bytes 589828

commit v17 on v14

--- a/solution.py
+++ b/solution.py
@@ -275,8 +275,12 @@
     return total
 
 
-def fused_kernel(rows, chunk, taps_ref, samples_ref, table_ref, out_hbm, own_f32, shifted,
-                 buffers, sems):
+def fused_kernel(rows, chunk, taps_ref, samples_hbm, table_hbm, out_hbm, own_f32, shifted,
+                 buffers, sems, samples_ref, table_ref, in_sems):
+    fetch_samples = pltpu.make_async_copy(samples_hbm, samples_ref, in_sems.at[0])
+    fetch_table = pltpu.make_async_copy(table_hbm, table_ref, in_sems.at[1])
+    fetch_samples.start()
+    fetch_table.start()
     tap_count = taps_ref.shape[0]
     outputs = NFFT // 2
     length, channels = samples_ref.shape
@@ -292,6 +296,7 @@
             jnp.broadcast_to(part.astype(jnp.float32), (outputs, lanes)), 0, 1, stride=2, stride_axis=0
         )
         matrices.append(rolled[:, : 2 * outputs + tap_count].astype(jnp.bfloat16))
+    fetch_samples.wait()
     x = samples_ref[...]
     joined = jnp.concatenate(
         [
@@ -309,6 +314,7 @@
         axis=0,
     )
     filtered = filtered.astype(jnp.bfloat16)
+    fetch_table.wait()
     spectrum = exact_dot([table_ref[p] for p in range(table_ref.shape[0])], filtered)
     real_part = spectrum[:NF]
     imag_part = spectrum[NF:]
@@ -357,13 +363,16 @@
     return pl.pallas_call(
         functools.partial(fused_kernel, rows, chunk),
         out_shape=jax.ShapeDtypeStruct((rows, LAGS, NFFT), jnp.bfloat16),
-        in_specs=[pl.BlockSpec(memory_space=pltpu.SMEM)] + [pl.BlockSpec(memory_space=pltpu.VMEM)] * 2,
+        in_specs=[pl.BlockSpec(memory_space=pltpu.SMEM)] + [pl.BlockSpec(memory_space=pl.ANY)] * 2,
         out_specs=pl.BlockSpec(memory_space=pl.ANY),
         scratch_shapes=[
             pltpu.VMEM((rows, NFFT), jnp.float32),
             pltpu.VMEM((chunk, span, NFFT), jnp.float32),
             pltpu.VMEM((4, chunk, LAGS, NFFT), jnp.bfloat16),
             pltpu.SemaphoreType.DMA((4, 4)),
+            pltpu.VMEM(samples.shape, samples.dtype),
+            pltpu.VMEM(table_t.shape, table_t.dtype),
+            pltpu.SemaphoreType.DMA((2,)),
         ],
         cost_estimate=pl.CostEstimate(
             flops=6 * rows * LAGS * NF + 12 * channels * (NF * 320 * length // 256 + NFFT * NFFT),

time: 27.4 us -> 27.9 us (1.018)
  Pallas kernels: 6.53 us -> 7.06 us
    pallas_call x1, Pallas kernels: 4.88 us -> 5.42 us  [fused_spectra(): pl.pallas_call(functools.partial(fused_kernel, rows, chunk), out_shape=ja...]
where the time goes in v17:
time: 27.9 us; the launch traced here: 27.6 us
  waiting for transfers between devices  8.5 us (30%)
  starting transfers between devices  7.51 us (27%)
  Pallas kernels  7.06 us (25%)
  other arithmetic  3.04 us (11%)
  local copies, waits for them, and re-layouts  1.42 us (5%)
    all_to_all x1, waiting for transfers between devices, body(): lax.all_to_all(windows, 'ta', split_axis=0, concat_axis=0, tiled=True)  6.24 us
    all_to_all x1, starting transfers between devices, body(): lax.all_to_all(windows, 'ta', split_axis=0, concat_axis=0, tiled=True)  5.55 us
    pallas_call x1, Pallas kernels, fused_spectra(): pl.pallas_call(functools.partial(fused_kernel, rows, chunk), out_shape=ja...  5.42 us
    ppermute x1, waiting for transfers between devices, body(): following = lax.ppermute(turned, 'col', route)  2.26 us
    ppermute x1, starting transfers between devices, body(): following = lax.ppermute(turned, 'col', route)  1.96 us
    pallas_call x1, Pallas kernels, channel_windows(): pl.pallas_call(functools.partial(windows_kernel, width, tail_rows), out_s...  1.64 us
    convert_element_type x1, other arithmetic, split_three_kept(): return [part.astype(jnp.bfloat16) for part in (high, middle, low)]  1.47 us
    another operation x1, other arithmetic, body(): table_parts = jnp.stack(split_three_kept(fourier_table_t()))  0.79 us
  transfers between devices with their start and end apart: 2, of which 2 were waited for; matrix products, arithmetic and copies ran while one was open for 11% of the time, Pallas kernels for 6%

profile of v17, /device:TPU:1, one launch (start us, length us, event | category | flops | bytes accessed | tf_op | source)
XLA Modules:
  0.0 27.6 jit_solution(13102581136657114569)
XLA Ops:
  0.0 2.0 %collective-permute-start = (bf16[64,512]{1,0:T(8,128)(2,1)}, bf16[64,512]{1,0:T(8,128)(2,1)S(1)}, u32[]{:S(2)}, u32[]{:S(2)}) collective-permute-start(bf16[64,512]{1,0:T(8,128)(2,1)} %bitcast.8), channel_id=1, source_target_pairs={{1,0},{2,1},{3,2},{5,4},{6,5},{7,6},{9,8},{10,9},{11,10},{13,12},{... | collective-permute-start | bytes 196616 | tf_op jit(solution)/shard_map/ppermute | solution.py:431
  2.0 0.7 %slice.16 = bf16[64,128]{1,0:T(8,128)(2,1)S(1)} slice(bf16[64,512]{1,0:T(8,128)(2,1)} %bitcast.9), slice={[0:64], [384:512]} | slice | bytes 32768 | tf_op jit(solution)/shard_map/slice | solution.py:105
  2.7 1.6 %shard_map.28 = bf16[8,64,192]{2,1,0:T(8,128)(2,1)} custom-call(bf16[64,512]{1,0:T(8,128)(2,1)} %bitcast.10), custom_call_target="tpu_custom_call" | custom-call | bytes 262144 | tf_op jit(solution)/shard_map/pallas_call | solution.py:95
  4.4 2.3 %collective-permute-done = bf16[64,512]{1,0:T(8,128)(2,1)S(1)} collective-permute-done((bf16[64,512]{1,0:T(8,128)(2,1)}, bf16[64,512]{1,0:T(8,128)(2,1)S(1)}, u32[]{:S(2)}, u32[]{:S(2)}) %collective-permute-start) | collective-permute-done | bytes 65568 | tf_op jit(solution)/shard_map/ppermute | solution.py:431
  6.7 0.1 maximum_bitcast_fusion
  6.7 0.6 %maximum_dynamic-update-slice_fusion = bf16[8,64,192]{2,1,0:T(8,128)(2,1)} fusion(bf16[8,64,192]{2,1,0:T(8,128)(2,1)} %shard_map.28, bf16[1,64,192]{2,1,0:T(8,128)(2,1)S(1)} %get-tuple-element.6, bf16[1,64,192]{2,1,0:T(8,128)(2,1)S(1)} %get-tuple-element.5), kind=kLoop, calls=%fused_computation.13 | loop fusion | flops 98304 | bytes 114688 | tf_op jit(solution)/shard_map/dynamic_update_slice | solution.py:107
  7.4 5.6 %all-to-all-start = ((bf16[8,64,192]{2,1,0:T(8,128)(2,1)}), bf16[8,64,192]{2,1,0:T(8,128)(2,1)S(1)}, u32[]{:S(2)}, u32[]{:S(2)}) async-start(bf16[8,64,192]{2,1,0:T(8,128)(2,1)} %maximum_dynamic-update-slice_fusion), calls=%async_computation | async-start | bytes 524288 | tf_op jit(solution)/shard_map/all_to_all | solution.py:435
  12.9 1.5 %reduce-precision_convert_fusion.1 = (bf16[1,256,256]{2,1,0:T(8,128)(2,1)S(1)}, bf16[1,256,256]{2,1,0:T(8,128)(2,1)S(1)}, bf16[1,256,256]{2,1,0:T(8,128)(2,1)S(1)}) fusion(f32[256]{0:T(256)S(1)} %get-tuple-element.15, s32[256]{0:T(256)S(1)} %get-tuple-element.12, s32[256]{0:T(256)S(1)} %get-tuple-element.13, pred[256]{0:T(512)(128)(4,1)S(1)} %get-tuple-element.10, ...), kind=kLoop, calls=%fused_computation.7 | loop fusion | flops 1703936 | bytes 397824 | tf_op jit(solution)/shard_map/convert_element_type | solution.py:267
  14.4 0.8 %pad_maximum_fusion.table_hbm = bf16[3,256,256]{2,1,0:T(8,128)(2,1)} fusion(bf16[1,256,256]{2,1,0:T(8,128)(2,1)S(1)} %get-tuple-element.9, bf16[1,256,256]{2,1,0:T(8,128)(2,1)S(1)} %get-tuple-element.8, bf16[1,256,256]{2,1,0:T(8,128)(2,1)S(1)} %get-tuple-element.7), kind=kLoop, calls=%fused_computation | loop fusion | flops 393216 | bytes 786432 | tf_op jit(solution)/shard_map/stack | solution.py:438
  15.2 6.2 %all-to-all-done = bf16[8,64,192]{2,1,0:T(8,128)(2,1)S(1)} async-done(((bf16[8,64,192]{2,1,0:T(8,128)(2,1)}), bf16[8,64,192]{2,1,0:T(8,128)(2,1)S(1)}, u32[]{:S(2)}, u32[]{:S(2)}) %all-to-all-start) | async-done | bytes 196640 | tf_op jit(solution)/shard_map/all_to_all | solution.py:435
  21.5 0.0 copy-start
  21.5 0.7 %copy-done = bf16[8,64,192]{2,1,0:T(8,128)(2,1)} copy-done((bf16[8,64,192]{2,1,0:T(8,128)(2,1)}, bf16[8,64,192]{2,1,0:T(8,128)(2,1)S(1)}, u32[]{:S(2)}) %copy-start) | copy-done | bytes 196632
  22.1 5.4 %shard_map.29 = bf16[64,128,256]{2,1,0:T(8,128)(2,1)} custom-call(f32[64]{0:T(128)} %taps_ref.1, bf16[512,192]{1,0:T(8,128)(2,1)} %bitcast.7, bf16[3,256,256]{2,1,0:T(8,128)(2,1)} %pad_maximum_fusion.table_hbm), custom_call_target="tpu_custom_call" | custom-call | flops 346030080 | bytes 4784128 | tf_op jit(solution)/shard_map/pallas_call | solution.py:363
  (4 shorter events, 0.1 us)
Async XLA Ops:
  0.0 6.7 %collective-permute-start = (bf16[64,512]{1,0:T(8,128)(2,1)}, bf16[64,512]{1,0:T(8,128)(2,1)S(1)}, u32[]{:S(2)}, u32[]{:S(2)}) collective-permute-start(bf16[64,512]{1,0:T(8,128)(2,1)} %bitcast.8), channel_id=1, source_target_pairs={{1,0},{2,1},{3,2},{5,4},{6,5},{7,6},{9,8},{10,9},{11,10},{13,12},{... | collective-permute-start | bytes 196616 | tf_op jit(solution)/shard_map/ppermute | solution.py:431
  7.4 14.1 %all-to-all-start = ((bf16[8,64,192]{2,1,0:T(8,128)(2,1)}), bf16[8,64,192]{2,1,0:T(8,128)(2,1)S(1)}, u32[]{:S(2)}, u32[]{:S(2)}) async-start(bf16[8,64,192]{2,1,0:T(8,128)(2,1)} %maximum_dynamic-update-slice_fusion), calls=%async_computation | async-start | bytes 524288 | tf_op jit(solution)/shard_map/all_to_all | solution.py:435
  21.5 0.7 %copy-start = (bf16[8,64,192]{2,1,0:T(8,128)(2,1)}, bf16[8,64,192]{2,1,0:T(8,128)(2,1)S(1)}, u32[]{:S(2)}) copy-start(bf16[8,64,192]{2,1,0:T(8,128)(2,1)S(1)} %all-to-all-done) | copy-start | bytes 589828

commit v18 on v14

--- a/solution.py
+++ b/solution.py
@@ -319,8 +319,13 @@
     extended = whitened.astype(jnp.bfloat16).astype(jnp.float32).T
     span = shifted.shape[1]
     own_f32[...] = extended[:rows]
+    narrow = extended.astype(jnp.bfloat16)
+    offset = lax.broadcasted_iota(jnp.int32, (span, channels), 1) - lax.broadcasted_iota(
+        jnp.int32, (span, channels), 0
+    )
     for i in range(chunk):
-        shifted[i] = extended[i : i + span]
+        pick = (offset == i).astype(jnp.bfloat16)
+        shifted[i] = jnp.dot(pick, narrow, preferred_element_type=jnp.float32)
     slots, parts = buffers.shape[0], sems.shape[1]
     part = chunk // parts
     copies = []

time: 27.4 us -> 27.6 us (level)
  no operation moved by 1% of the time
where the time goes in v18:
time: 27.6 us; the launch traced here: 27.2 us
  waiting for transfers between devices  8.5 us (31%)
  starting transfers between devices  7.51 us (27%)
  Pallas kernels  6.73 us (24%)
  other arithmetic  3.04 us (11%)
  local copies, waits for them, and re-layouts  1.42 us (5%)
    all_to_all x1, waiting for transfers between devices, body(): lax.all_to_all(windows, 'ta', split_axis=0, concat_axis=0, tiled=True)  6.24 us
    all_to_all x1, starting transfers between devices, body(): lax.all_to_all(windows, 'ta', split_axis=0, concat_axis=0, tiled=True)  5.55 us
    pallas_call x1, Pallas kernels, fused_spectra(): pl.pallas_call(functools.partial(fused_kernel, rows, chunk), out_shape=ja...  5.09 us
    ppermute x1, waiting for transfers between devices, body(): following = lax.ppermute(turned, 'col', route)  2.26 us
    ppermute x1, starting transfers between devices, body(): following = lax.ppermute(turned, 'col', route)  1.96 us
    pallas_call x1, Pallas kernels, channel_windows(): pl.pallas_call(functools.partial(windows_kernel, width, tail_rows), out_s...  1.64 us
    convert_element_type x1, other arithmetic, split_three_kept(): return [part.astype(jnp.bfloat16) for part in (high, middle, low)]  1.47 us
    another operation x1, other arithmetic, body(): table_parts = jnp.stack(split_three_kept(fourier_table_t()))  0.79 us
  transfers between devices with their start and end apart: 2, of which 2 were waited for; matrix products, arithmetic and copies ran while one was open for 11% of the time, Pallas kernels for 6%

profile of v18, /device:TPU:1, one launch (start us, length us, event | category | flops | bytes accessed | tf_op | source)
XLA Modules:
  0.0 27.2 jit_solution(2587352704988237459)
XLA Ops:
  0.0 2.0 %collective-permute-start = (bf16[64,512]{1,0:T(8,128)(2,1)}, bf16[64,512]{1,0:T(8,128)(2,1)S(1)}, u32[]{:S(2)}, u32[]{:S(2)}) collective-permute-start(bf16[64,512]{1,0:T(8,128)(2,1)} %bitcast.8), channel_id=1, source_target_pairs={{1,0},{2,1},{3,2},{5,4},{6,5},{7,6},{9,8},{10,9},{11,10},{13,12},{... | collective-permute-start | bytes 196616 | tf_op jit(solution)/shard_map/ppermute | solution.py:427
  2.0 0.7 %slice.16 = bf16[64,128]{1,0:T(8,128)(2,1)S(1)} slice(bf16[64,512]{1,0:T(8,128)(2,1)} %bitcast.9), slice={[0:64], [384:512]} | slice | bytes 32768 | tf_op jit(solution)/shard_map/slice | solution.py:105
  2.7 1.6 %shard_map.28 = bf16[8,64,192]{2,1,0:T(8,128)(2,1)} custom-call(bf16[64,512]{1,0:T(8,128)(2,1)} %bitcast.10), custom_call_target="tpu_custom_call" | custom-call | bytes 262144 | tf_op jit(solution)/shard_map/pallas_call | solution.py:95
  4.4 2.3 %collective-permute-done = bf16[64,512]{1,0:T(8,128)(2,1)S(1)} collective-permute-done((bf16[64,512]{1,0:T(8,128)(2,1)}, bf16[64,512]{1,0:T(8,128)(2,1)S(1)}, u32[]{:S(2)}, u32[]{:S(2)}) %collective-permute-start) | collective-permute-done | bytes 65568 | tf_op jit(solution)/shard_map/ppermute | solution.py:427
  6.7 0.1 maximum_bitcast_fusion
  6.7 0.6 %maximum_dynamic-update-slice_fusion = bf16[8,64,192]{2,1,0:T(8,128)(2,1)} fusion(bf16[8,64,192]{2,1,0:T(8,128)(2,1)} %shard_map.28, bf16[1,64,192]{2,1,0:T(8,128)(2,1)S(1)} %get-tuple-element.6, bf16[1,64,192]{2,1,0:T(8,128)(2,1)S(1)} %get-tuple-element.5), kind=kLoop, calls=%fused_computation.13 | loop fusion | flops 98304 | bytes 114688 | tf_op jit(solution)/shard_map/dynamic_update_slice | solution.py:107
  7.4 5.6 %all-to-all-start = ((bf16[8,64,192]{2,1,0:T(8,128)(2,1)}), bf16[8,64,192]{2,1,0:T(8,128)(2,1)S(1)}, u32[]{:S(2)}, u32[]{:S(2)}) async-start(bf16[8,64,192]{2,1,0:T(8,128)(2,1)} %maximum_dynamic-update-slice_fusion), calls=%async_computation | async-start | bytes 524288 | tf_op jit(solution)/shard_map/all_to_all | solution.py:431
  12.9 1.5 %reduce-precision_convert_fusion.1 = (bf16[1,256,256]{2,1,0:T(8,128)(2,1)S(1)}, bf16[1,256,256]{2,1,0:T(8,128)(2,1)S(1)}, bf16[1,256,256]{2,1,0:T(8,128)(2,1)S(1)}) fusion(f32[256]{0:T(256)S(1)} %get-tuple-element.15, s32[256]{0:T(256)S(1)} %get-tuple-element.12, s32[256]{0:T(256)S(1)} %get-tuple-element.13, pred[256]{0:T(512)(128)(4,1)S(1)} %get-tuple-element.10, ...), kind=kLoop, calls=%fused_computation.7 | loop fusion | flops 1703936 | bytes 397824 | tf_op jit(solution)/shard_map/convert_element_type | solution.py:267
  14.4 0.8 %pad_maximum_fusion.table_ref = bf16[3,256,256]{2,1,0:T(8,128)(2,1)} fusion(bf16[1,256,256]{2,1,0:T(8,128)(2,1)S(1)} %get-tuple-element.9, bf16[1,256,256]{2,1,0:T(8,128)(2,1)S(1)} %get-tuple-element.8, bf16[1,256,256]{2,1,0:T(8,128)(2,1)S(1)} %get-tuple-element.7), kind=kLoop, calls=%fused_computation | loop fusion | flops 393216 | bytes 786432 | tf_op jit(solution)/shard_map/stack | solution.py:434
  15.2 6.2 %all-to-all-done = bf16[8,64,192]{2,1,0:T(8,128)(2,1)S(1)} async-done(((bf16[8,64,192]{2,1,0:T(8,128)(2,1)}), bf16[8,64,192]{2,1,0:T(8,128)(2,1)S(1)}, u32[]{:S(2)}, u32[]{:S(2)}) %all-to-all-start) | async-done | bytes 196640 | tf_op jit(solution)/shard_map/all_to_all | solution.py:431
  21.5 0.0 copy-start
  21.5 0.7 %copy-done = bf16[8,64,192]{2,1,0:T(8,128)(2,1)} copy-done((bf16[8,64,192]{2,1,0:T(8,128)(2,1)}, bf16[8,64,192]{2,1,0:T(8,128)(2,1)S(1)}, u32[]{:S(2)}) %copy-start) | copy-done | bytes 196632
  22.1 5.1 %shard_map.29 = bf16[64,128,256]{2,1,0:T(8,128)(2,1)} custom-call(f32[64]{0:T(128)} %taps_ref.1, bf16[512,192]{1,0:T(8,128)(2,1)} %bitcast.7, bf16[3,256,256]{2,1,0:T(8,128)(2,1)} %pad_maximum_fusion.table_ref), custom_call_target="tpu_custom_call" | custom-call | flops 346030080 | bytes 4784128 | tf_op jit(solution)/shard_map/pallas_call | solution.py:362
  (4 shorter events, 0.1 us)
Async XLA Ops:
  0.0 6.7 %collective-permute-start = (bf16[64,512]{1,0:T(8,128)(2,1)}, bf16[64,512]{1,0:T(8,128)(2,1)S(1)}, u32[]{:S(2)}, u32[]{:S(2)}) collective-permute-start(bf16[64,512]{1,0:T(8,128)(2,1)} %bitcast.8), channel_id=1, source_target_pairs={{1,0},{2,1},{3,2},{5,4},{6,5},{7,6},{9,8},{10,9},{11,10},{13,12},{... | collective-permute-start | bytes 196616 | tf_op jit(solution)/shard_map/ppermute | solution.py:427
  7.4 14.1 %all-to-all-start = ((bf16[8,64,192]{2,1,0:T(8,128)(2,1)}), bf16[8,64,192]{2,1,0:T(8,128)(2,1)S(1)}, u32[]{:S(2)}, u32[]{:S(2)}) async-start(bf16[8,64,192]{2,1,0:T(8,128)(2,1)} %maximum_dynamic-update-slice_fusion), calls=%async_computation | async-start | bytes 524288 | tf_op jit(solution)/shard_map/all_to_all | solution.py:431
  21.5 0.7 %copy-start = (bf16[8,64,192]{2,1,0:T(8,128)(2,1)}, bf16[8,64,192]{2,1,0:T(8,128)(2,1)S(1)}, u32[]{:S(2)}) copy-start(bf16[8,64,192]{2,1,0:T(8,128)(2,1)S(1)} %all-to-all-done) | copy-start | bytes 589828

commit v19 on v14

--- a/solution.py
+++ b/solution.py
@@ -314,7 +314,7 @@
     imag_part = spectrum[NF:]
     powers = real_part * real_part + imag_part * imag_part
     mean_power = jnp.mean(powers, axis=0, keepdims=True)
-    whitening = 1.0 / jnp.sqrt(powers + mean_power + 1e-06)
+    whitening = lax.rsqrt(powers + mean_power + 1e-06)
     whitened = jnp.concatenate([real_part * whitening, imag_part * whitening], axis=0)
     extended = whitened.astype(jnp.bfloat16).astype(jnp.float32).T
     span = shifted.shape[1]

time: 27.4 us -> 27.4 us (level)
  no operation moved by 1% of the time
where the time goes in v19:
time: 27.4 us; the launch traced here: 27 us
  waiting for transfers between devices  8.5 us (31%)
  starting transfers between devices  7.51 us (27%)
  Pallas kernels  6.5 us (24%)
  other arithmetic  3.04 us (11%)
  local copies, waits for them, and re-layouts  1.42 us (5%)
    all_to_all x1, waiting for transfers between devices, body(): lax.all_to_all(windows, 'ta', split_axis=0, concat_axis=0, tiled=True)  6.24 us
    all_to_all x1, starting transfers between devices, body(): lax.all_to_all(windows, 'ta', split_axis=0, concat_axis=0, tiled=True)  5.55 us
    pallas_call x1, Pallas kernels, fused_spectra(): pl.pallas_call(functools.partial(fused_kernel, rows, chunk), out_shape=ja...  4.86 us
    ppermute x1, waiting for transfers between devices, body(): following = lax.ppermute(turned, 'col', route)  2.26 us
    ppermute x1, starting transfers between devices, body(): following = lax.ppermute(turned, 'col', route)  1.96 us
    pallas_call x1, Pallas kernels, channel_windows(): pl.pallas_call(functools.partial(windows_kernel, width, tail_rows), out_s...  1.64 us
    convert_element_type x1, other arithmetic, split_three_kept(): return [part.astype(jnp.bfloat16) for part in (high, middle, low)]  1.47 us
    another operation x1, other arithmetic, body(): table_parts = jnp.stack(split_three_kept(fourier_table_t()))  0.79 us
  transfers between devices with their start and end apart: 2, of which 2 were waited for; matrix products, arithmetic and copies ran while one was open for 11% of the time, Pallas kernels for 6%

profile of v19, /device:TPU:1, one launch (start us, length us, event | category | flops | bytes accessed | tf_op | source)
XLA Modules:
  0.0 27.0 jit_solution(845368373101119334)
XLA Ops:
  0.0 2.0 %collective-permute-start = (bf16[64,512]{1,0:T(8,128)(2,1)}, bf16[64,512]{1,0:T(8,128)(2,1)S(1)}, u32[]{:S(2)}, u32[]{:S(2)}) collective-permute-start(bf16[64,512]{1,0:T(8,128)(2,1)} %bitcast.8), channel_id=1, source_target_pairs={{1,0},{2,1},{3,2},{5,4},{6,5},{7,6},{9,8},{10,9},{11,10},{13,12},{... | collective-permute-start | bytes 196616 | tf_op jit(solution)/shard_map/ppermute | solution.py:422
  2.0 0.7 %slice.16 = bf16[64,128]{1,0:T(8,128)(2,1)S(1)} slice(bf16[64,512]{1,0:T(8,128)(2,1)} %bitcast.9), slice={[0:64], [384:512]} | slice | bytes 32768 | tf_op jit(solution)/shard_map/slice | solution.py:105
  2.7 1.6 %shard_map.28 = bf16[8,64,192]{2,1,0:T(8,128)(2,1)} custom-call(bf16[64,512]{1,0:T(8,128)(2,1)} %bitcast.10), custom_call_target="tpu_custom_call" | custom-call | bytes 262144 | tf_op jit(solution)/shard_map/pallas_call | solution.py:95
  4.4 2.3 %collective-permute-done = bf16[64,512]{1,0:T(8,128)(2,1)S(1)} collective-permute-done((bf16[64,512]{1,0:T(8,128)(2,1)}, bf16[64,512]{1,0:T(8,128)(2,1)S(1)}, u32[]{:S(2)}, u32[]{:S(2)}) %collective-permute-start) | collective-permute-done | bytes 65568 | tf_op jit(solution)/shard_map/ppermute | solution.py:422
  6.7 0.1 maximum_bitcast_fusion
  6.7 0.6 %maximum_dynamic-update-slice_fusion = bf16[8,64,192]{2,1,0:T(8,128)(2,1)} fusion(bf16[8,64,192]{2,1,0:T(8,128)(2,1)} %shard_map.28, bf16[1,64,192]{2,1,0:T(8,128)(2,1)S(1)} %get-tuple-element.6, bf16[1,64,192]{2,1,0:T(8,128)(2,1)S(1)} %get-tuple-element.5), kind=kLoop, calls=%fused_computation.13 | loop fusion | flops 98304 | bytes 114688 | tf_op jit(solution)/shard_map/dynamic_update_slice | solution.py:107
  7.4 5.6 %all-to-all-start = ((bf16[8,64,192]{2,1,0:T(8,128)(2,1)}), bf16[8,64,192]{2,1,0:T(8,128)(2,1)S(1)}, u32[]{:S(2)}, u32[]{:S(2)}) async-start(bf16[8,64,192]{2,1,0:T(8,128)(2,1)} %maximum_dynamic-update-slice_fusion), calls=%async_computation | async-start | bytes 524288 | tf_op jit(solution)/shard_map/all_to_all | solution.py:426
  12.9 1.5 %reduce-precision_convert_fusion.1 = (bf16[1,256,256]{2,1,0:T(8,128)(2,1)S(1)}, bf16[1,256,256]{2,1,0:T(8,128)(2,1)S(1)}, bf16[1,256,256]{2,1,0:T(8,128)(2,1)S(1)}) fusion(f32[256]{0:T(256)S(1)} %get-tuple-element.15, s32[256]{0:T(256)S(1)} %get-tuple-element.12, s32[256]{0:T(256)S(1)} %get-tuple-element.13, pred[256]{0:T(512)(128)(4,1)S(1)} %get-tuple-element.10, ...), kind=kLoop, calls=%fused_computation.7 | loop fusion | flops 1703936 | bytes 397824 | tf_op jit(solution)/shard_map/convert_element_type | solution.py:267
  14.4 0.8 %pad_maximum_fusion.table_ref = bf16[3,256,256]{2,1,0:T(8,128)(2,1)} fusion(bf16[1,256,256]{2,1,0:T(8,128)(2,1)S(1)} %get-tuple-element.9, bf16[1,256,256]{2,1,0:T(8,128)(2,1)S(1)} %get-tuple-element.8, bf16[1,256,256]{2,1,0:T(8,128)(2,1)S(1)} %get-tuple-element.7), kind=kLoop, calls=%fused_computation | loop fusion | flops 393216 | bytes 786432 | tf_op jit(solution)/shard_map/stack | solution.py:429
  15.2 6.2 %all-to-all-done = bf16[8,64,192]{2,1,0:T(8,128)(2,1)S(1)} async-done(((bf16[8,64,192]{2,1,0:T(8,128)(2,1)}), bf16[8,64,192]{2,1,0:T(8,128)(2,1)S(1)}, u32[]{:S(2)}, u32[]{:S(2)}) %all-to-all-start) | async-done | bytes 196640 | tf_op jit(solution)/shard_map/all_to_all | solution.py:426
  21.5 0.0 copy-start
  21.5 0.7 %copy-done = bf16[8,64,192]{2,1,0:T(8,128)(2,1)} copy-done((bf16[8,64,192]{2,1,0:T(8,128)(2,1)}, bf16[8,64,192]{2,1,0:T(8,128)(2,1)S(1)}, u32[]{:S(2)}) %copy-start) | copy-done | bytes 196632
  22.1 4.9 %shard_map.29 = bf16[64,128,256]{2,1,0:T(8,128)(2,1)} custom-call(f32[64]{0:T(128)} %taps_ref.1, bf16[512,192]{1,0:T(8,128)(2,1)} %bitcast.7, bf16[3,256,256]{2,1,0:T(8,128)(2,1)} %pad_maximum_fusion.table_ref), custom_call_target="tpu_custom_call" | custom-call | flops 346030080 | bytes 4784128 | tf_op jit(solution)/shard_map/pallas_call | solution.py:357
  (4 shorter events, 0.1 us)
Async XLA Ops:
  0.0 6.7 %collective-permute-start = (bf16[64,512]{1,0:T(8,128)(2,1)}, bf16[64,512]{1,0:T(8,128)(2,1)S(1)}, u32[]{:S(2)}, u32[]{:S(2)}) collective-permute-start(bf16[64,512]{1,0:T(8,128)(2,1)} %bitcast.8), channel_id=1, source_target_pairs={{1,0},{2,1},{3,2},{5,4},{6,5},{7,6},{9,8},{10,9},{11,10},{13,12},{... | collective-permute-start | bytes 196616 | tf_op jit(solution)/shard_map/ppermute | solution.py:422
  7.4 14.1 %all-to-all-start = ((bf16[8,64,192]{2,1,0:T(8,128)(2,1)}), bf16[8,64,192]{2,1,0:T(8,128)(2,1)S(1)}, u32[]{:S(2)}, u32[]{:S(2)}) async-start(bf16[8,64,192]{2,1,0:T(8,128)(2,1)} %maximum_dynamic-update-slice_fusion), calls=%async_computation | async-start | bytes 524288 | tf_op jit(solution)/shard_map/all_to_all | solution.py:426
  21.5 0.7 %copy-start = (bf16[8,64,192]{2,1,0:T(8,128)(2,1)}, bf16[8,64,192]{2,1,0:T(8,128)(2,1)S(1)}, u32[]{:S(2)}) copy-start(bf16[8,64,192]{2,1,0:T(8,128)(2,1)S(1)} %all-to-all-done) | copy-start | bytes 589828

commit v20 on v19

--- a/solution.py
+++ b/solution.py
@@ -102,8 +102,14 @@
     step = (rows + tail_rows - width) // (extent - 1)
     count = -(-tail_rows // step)
     first = extent - count
-    padded = jnp.concatenate([turned[:, first * step :], tail], axis=1)
-    patch = jnp.stack([padded[:, j * step : j * step + width] for j in range(count)])
+    patch = jnp.stack(
+        [
+            jnp.concatenate(
+                [windows[j, :, : rows - j * step], tail[:, : width - (rows - j * step)]], axis=1
+            )
+            for j in range(first, extent)
+        ]
+    )
     return lax.dynamic_update_slice(windows, patch, (first, 0, 0))
 
 

time: 27.4 us -> 28.7 us (1.047)
  the two profiles are of different devices: /device:TPU:1 before, /device:TPU:0 now
where the time goes in v20:
time: 28.7 us; the launch traced here: 28.3 us
  starting transfers between devices  8.56 us (30%)
  waiting for transfers between devices  7.98 us (28%)
  Pallas kernels  6.5 us (23%)
  other arithmetic  3.03 us (11%)
  local copies, waits for them, and re-layouts  2.14 us (7%)
    all_to_all x1, waiting for transfers between devices, body(): lax.all_to_all(windows, 'ta', split_axis=0, concat_axis=0, tiled=True)  7.97 us
    all_to_all x1, starting transfers between devices, body(): lax.all_to_all(windows, 'ta', split_axis=0, concat_axis=0, tiled=True)  7.28 us
    pallas_call x1, Pallas kernels, fused_spectra(): pl.pallas_call(functools.partial(fused_kernel, rows, chunk), out_shape=ja...  4.86 us
    pallas_call x1, Pallas kernels, channel_windows(): pl.pallas_call(functools.partial(windows_kernel, width, tail_rows), out_s...  1.65 us
    convert_element_type x1, other arithmetic, split_three_kept(): return [part.astype(jnp.bfloat16) for part in (high, middle, low)]  1.47 us
    squeeze x2, local copies, waits for them, and re-layouts, channel_windows(): windows[j, :, :rows - j * step]  1.44 us
    ppermute x1, starting transfers between devices, body(): following = lax.ppermute(turned, 'col', route)  1.28 us
    another operation x1, other arithmetic, body(): table_parts = jnp.stack(split_three_kept(fourier_table_t()))  0.79 us
  transfers between devices with their start and end apart: 2, of which 1 were waited for; matrix products, arithmetic and copies ran while one was open for 13% of the time, Pallas kernels for 6%

profile of v20, /device:TPU:0, one launch (start us, length us, event | category | flops | bytes accessed | tf_op | source)
XLA Modules:
  0.0 28.3 jit_solution(13112707729562297193)
XLA Ops:
  0.0 1.3 %collective-permute-start = (bf16[64,512]{1,0:T(8,128)(2,1)}, bf16[64,512]{1,0:T(8,128)(2,1)S(1)}, u32[]{:S(2)}, u32[]{:S(2)}) collective-permute-start(bf16[64,512]{1,0:T(8,128)(2,1)} %bitcast.12), channel_id=1, source_target_pairs={{1,0},{2,1},{3,2},{5,4},{6,5},{7,6},{9,8},{10,9},{11,10},{13,12},{... | collective-permute-start | bytes 196616 | tf_op jit(solution)/shard_map/ppermute | solution.py:428
  1.3 1.6 %shard_map.28 = bf16[8,64,192]{2,1,0:T(8,128)(2,1)} custom-call(bf16[64,512]{1,0:T(8,128)(2,1)} %bitcast.13), custom_call_target="tpu_custom_call" | custom-call | bytes 262144 | tf_op jit(solution)/shard_map/pallas_call | solution.py:95
  3.0 0.7 %slice_bitcast_fusion = bf16[64,64]{1,0:T(8,128)(2,1)S(1)} fusion(bf16[8,64,192]{2,1,0:T(8,128)(2,1)} %shard_map.28), kind=kLoop, calls=%fused_computation.16 | loop fusion | bytes 16384 | tf_op jit(solution)/shard_map/squeeze | solution.py:108
  3.7 0.7 %slice_bitcast_fusion.1 = bf16[64,128]{1,0:T(8,128)(2,1)S(1)} fusion(bf16[8,64,192]{2,1,0:T(8,128)(2,1)} %shard_map.28), kind=kLoop, calls=%fused_computation.17 | loop fusion | bytes 32768 | tf_op jit(solution)/shard_map/squeeze | solution.py:108
  4.4 0.0 collective-permute-done
  4.5 0.1 maximum_bitcast_fusion
  4.5 0.6 %maximum_dynamic-update-slice_fusion = bf16[8,64,192]{2,1,0:T(8,128)(2,1)} fusion(bf16[8,64,192]{2,1,0:T(8,128)(2,1)} %shard_map.28, bf16[1,64,192]{2,1,0:T(8,128)(2,1)S(1)} %get-tuple-element.9, bf16[1,64,192]{2,1,0:T(8,128)(2,1)S(1)} %get-tuple-element.8), kind=kLoop, calls=%fused_computation.13 | loop fusion | flops 98304 | bytes 114688 | tf_op jit(solution)/shard_map/dynamic_update_slice | solution.py:113
  5.2 7.3 %all-to-all-start = ((bf16[8,64,192]{2,1,0:T(8,128)(2,1)}), bf16[8,64,192]{2,1,0:T(8,128)(2,1)S(1)}, u32[]{:S(2)}, u32[]{:S(2)}) async-start(bf16[8,64,192]{2,1,0:T(8,128)(2,1)} %maximum_dynamic-update-slice_fusion), calls=%async_computation | async-start | bytes 524288 | tf_op jit(solution)/shard_map/all_to_all | solution.py:432
  12.5 1.5 %reduce-precision_convert_fusion.1 = (bf16[1,256,256]{2,1,0:T(8,128)(2,1)S(1)}, bf16[1,256,256]{2,1,0:T(8,128)(2,1)S(1)}, bf16[1,256,256]{2,1,0:T(8,128)(2,1)S(1)}) fusion(f32[256]{0:T(256)S(1)} %get-tuple-element.15, s32[256]{0:T(256)S(1)} %get-tuple-element.12, s32[256]{0:T(256)S(1)} %get-tuple-element.13, pred[256]{0:T(512)(128)(4,1)S(1)} %get-tuple-element.10, ...), kind=kLoop, calls=%fused_computation.7 | loop fusion | flops 1703936 | bytes 397824 | tf_op jit(solution)/shard_map/convert_element_type | solution.py:273
  13.9 0.8 %pad_maximum_fusion.table_ref = bf16[3,256,256]{2,1,0:T(8,128)(2,1)} fusion(bf16[1,256,256]{2,1,0:T(8,128)(2,1)S(1)} %get-tuple-element.7, bf16[1,256,256]{2,1,0:T(8,128)(2,1)S(1)} %get-tuple-element.6, bf16[1,256,256]{2,1,0:T(8,128)(2,1)S(1)} %get-tuple-element.5), kind=kLoop, calls=%fused_computation | loop fusion | flops 393216 | bytes 786432 | tf_op jit(solution)/shard_map/stack | solution.py:435
  14.7 8.0 %all-to-all-done = bf16[8,64,192]{2,1,0:T(8,128)(2,1)S(1)} async-done(((bf16[8,64,192]{2,1,0:T(8,128)(2,1)}), bf16[8,64,192]{2,1,0:T(8,128)(2,1)S(1)}, u32[]{:S(2)}, u32[]{:S(2)}) %all-to-all-start) | async-done | bytes 196640 | tf_op jit(solution)/shard_map/all_to_all | solution.py:432
  22.7 0.0 copy-start
  22.7 0.7 %copy-done = bf16[8,64,192]{2,1,0:T(8,128)(2,1)} copy-done((bf16[8,64,192]{2,1,0:T(8,128)(2,1)}, bf16[8,64,192]{2,1,0:T(8,128)(2,1)S(1)}, u32[]{:S(2)}) %copy-start) | copy-done | bytes 196632
  23.4 4.9 %shard_map.29 = bf16[64,128,256]{2,1,0:T(8,128)(2,1)} custom-call(f32[64]{0:T(128)} %taps_ref.1, bf16[512,192]{1,0:T(8,128)(2,1)} %bitcast.11, bf16[3,256,256]{2,1,0:T(8,128)(2,1)} %pad_maximum_fusion.table_ref), custom_call_target="tpu_custom_call" | custom-call | flops 346030080 | bytes 4784128 | tf_op jit(solution)/shard_map/pallas_call | solution.py:363
  (5 shorter events, 0.1 us)
Async XLA Ops:
  0.0 4.4 %collective-permute-start = (bf16[64,512]{1,0:T(8,128)(2,1)}, bf16[64,512]{1,0:T(8,128)(2,1)S(1)}, u32[]{:S(2)}, u32[]{:S(2)}) collective-permute-start(bf16[64,512]{1,0:T(8,128)(2,1)} %bitcast.12), channel_id=1, source_target_pairs={{1,0},{2,1},{3,2},{5,4},{6,5},{7,6},{9,8},{10,9},{11,10},{13,12},{... | collective-permute-start | bytes 196616 | tf_op jit(solution)/shard_map/ppermute | solution.py:428
  5.2 17.5 %all-to-all-start = ((bf16[8,64,192]{2,1,0:T(8,128)(2,1)}), bf16[8,64,192]{2,1,0:T(8,128)(2,1)S(1)}, u32[]{:S(2)}, u32[]{:S(2)}) async-start(bf16[8,64,192]{2,1,0:T(8,128)(2,1)} %maximum_dynamic-update-slice_fusion), calls=%async_computation | async-start | bytes 524288 | tf_op jit(solution)/shard_map/all_to_all | solution.py:432
  22.7 0.7 %copy-start = (bf16[8,64,192]{2,1,0:T(8,128)(2,1)}, bf16[8,64,192]{2,1,0:T(8,128)(2,1)S(1)}, u32[]{:S(2)}) copy-start(bf16[8,64,192]{2,1,0:T(8,128)(2,1)S(1)} %all-to-all-done) | copy-start | bytes 589828

commit v21 on v19

--- a/solution.py
+++ b/solution.py
@@ -362,8 +362,8 @@
         scratch_shapes=[
             pltpu.VMEM((rows, NFFT), jnp.float32),
             pltpu.VMEM((chunk, span, NFFT), jnp.float32),
-            pltpu.VMEM((4, chunk, LAGS, NFFT), jnp.bfloat16),
-            pltpu.SemaphoreType.DMA((4, 4)),
+            pltpu.VMEM((rows // chunk, chunk, LAGS, NFFT), jnp.bfloat16),
+            pltpu.SemaphoreType.DMA((rows // chunk, 4)),
         ],
         cost_estimate=pl.CostEstimate(
             flops=6 * rows * LAGS * NF + 12 * channels * (NF * 320 * length // 256 + NFFT * NFFT),

time: 27.4 us -> 27.6 us (level)
  Pallas kernels: 6.5 us -> 6.79 us
    pallas_call x1, Pallas kernels: 4.86 us -> 5.15 us  [fused_spectra(): pl.pallas_call(functools.partial(fused_kernel, rows, chunk), out_shape=ja...]
where the time goes in v21:
time: 27.6 us; the launch traced here: 27.3 us
  waiting for transfers between devices  8.5 us (31%)
  starting transfers between devices  7.51 us (27%)
  Pallas kernels  6.79 us (25%)
  other arithmetic  3.04 us (11%)
  local copies, waits for them, and re-layouts  1.42 us (5%)
    all_to_all x1, waiting for transfers between devices, body(): lax.all_to_all(windows, 'ta', split_axis=0, concat_axis=0, tiled=True)  6.24 us
    all_to_all x1, starting transfers between devices, body(): lax.all_to_all(windows, 'ta', split_axis=0, concat_axis=0, tiled=True)  5.55 us
    pallas_call x1, Pallas kernels, fused_spectra(): pl.pallas_call(functools.partial(fused_kernel, rows, chunk), out_shape=ja...  5.15 us
    ppermute x1, waiting for transfers between devices, body(): following = lax.ppermute(turned, 'col', route)  2.26 us
    ppermute x1, starting transfers between devices, body(): following = lax.ppermute(turned, 'col', route)  1.96 us
    pallas_call x1, Pallas kernels, channel_windows(): pl.pallas_call(functools.partial(windows_kernel, width, tail_rows), out_s...  1.64 us
    convert_element_type x1, other arithmetic, split_three_kept(): return [part.astype(jnp.bfloat16) for part in (high, middle, low)]  1.47 us
    another operation x1, other arithmetic, body(): table_parts = jnp.stack(split_three_kept(fourier_table_t()))  0.79 us
  transfers between devices with their start and end apart: 2, of which 2 were waited for; matrix products, arithmetic and copies ran while one was open for 11% of the time, Pallas kernels for 6%

profile of v21, /device:TPU:1, one launch (start us, length us, event | category | flops | bytes accessed | tf_op | source)
XLA Modules:
  0.0 27.3 jit_solution(8071909268128816956)
XLA Ops:
  0.0 2.0 %collective-permute-start = (bf16[64,512]{1,0:T(8,128)(2,1)}, bf16[64,512]{1,0:T(8,128)(2,1)S(1)}, u32[]{:S(2)}, u32[]{:S(2)}) collective-permute-start(bf16[64,512]{1,0:T(8,128)(2,1)} %bitcast.8), channel_id=1, source_target_pairs={{1,0},{2,1},{3,2},{5,4},{6,5},{7,6},{9,8},{10,9},{11,10},{13,12},{... | collective-permute-start | bytes 196616 | tf_op jit(solution)/shard_map/ppermute | solution.py:422
  2.0 0.7 %slice.16 = bf16[64,128]{1,0:T(8,128)(2,1)S(1)} slice(bf16[64,512]{1,0:T(8,128)(2,1)} %bitcast.9), slice={[0:64], [384:512]} | slice | bytes 32768 | tf_op jit(solution)/shard_map/slice | solution.py:105
  2.7 1.6 %shard_map.28 = bf16[8,64,192]{2,1,0:T(8,128)(2,1)} custom-call(bf16[64,512]{1,0:T(8,128)(2,1)} %bitcast.10), custom_call_target="tpu_custom_call" | custom-call | bytes 262144 | tf_op jit(solution)/shard_map/pallas_call | solution.py:95
  4.4 2.3 %collective-permute-done = bf16[64,512]{1,0:T(8,128)(2,1)S(1)} collective-permute-done((bf16[64,512]{1,0:T(8,128)(2,1)}, bf16[64,512]{1,0:T(8,128)(2,1)S(1)}, u32[]{:S(2)}, u32[]{:S(2)}) %collective-permute-start) | collective-permute-done | bytes 65568 | tf_op jit(solution)/shard_map/ppermute | solution.py:422
  6.7 0.1 maximum_bitcast_fusion
  6.7 0.6 %maximum_dynamic-update-slice_fusion = bf16[8,64,192]{2,1,0:T(8,128)(2,1)} fusion(bf16[8,64,192]{2,1,0:T(8,128)(2,1)} %shard_map.28, bf16[1,64,192]{2,1,0:T(8,128)(2,1)S(1)} %get-tuple-element.6, bf16[1,64,192]{2,1,0:T(8,128)(2,1)S(1)} %get-tuple-element.5), kind=kLoop, calls=%fused_computation.13 | loop fusion | flops 98304 | bytes 114688 | tf_op jit(solution)/shard_map/dynamic_update_slice | solution.py:107
  7.4 5.6 %all-to-all-start = ((bf16[8,64,192]{2,1,0:T(8,128)(2,1)}), bf16[8,64,192]{2,1,0:T(8,128)(2,1)S(1)}, u32[]{:S(2)}, u32[]{:S(2)}) async-start(bf16[8,64,192]{2,1,0:T(8,128)(2,1)} %maximum_dynamic-update-slice_fusion), calls=%async_computation | async-start | bytes 524288 | tf_op jit(solution)/shard_map/all_to_all | solution.py:426
  12.9 1.5 %reduce-precision_convert_fusion.1 = (bf16[1,256,256]{2,1,0:T(8,128)(2,1)S(1)}, bf16[1,256,256]{2,1,0:T(8,128)(2,1)S(1)}, bf16[1,256,256]{2,1,0:T(8,128)(2,1)S(1)}) fusion(f32[256]{0:T(256)S(1)} %get-tuple-element.15, s32[256]{0:T(256)S(1)} %get-tuple-element.12, s32[256]{0:T(256)S(1)} %get-tuple-element.13, pred[256]{0:T(512)(128)(4,1)S(1)} %get-tuple-element.10, ...), kind=kLoop, calls=%fused_computation.7 | loop fusion | flops 1703936 | bytes 397824 | tf_op jit(solution)/shard_map/convert_element_type | solution.py:267
  14.4 0.8 %pad_maximum_fusion.table_ref = bf16[3,256,256]{2,1,0:T(8,128)(2,1)} fusion(bf16[1,256,256]{2,1,0:T(8,128)(2,1)S(1)} %get-tuple-element.9, bf16[1,256,256]{2,1,0:T(8,128)(2,1)S(1)} %get-tuple-element.8, bf16[1,256,256]{2,1,0:T(8,128)(2,1)S(1)} %get-tuple-element.7), kind=kLoop, calls=%fused_computation | loop fusion | flops 393216 | bytes 786432 | tf_op jit(solution)/shard_map/stack | solution.py:429
  15.2 6.2 %all-to-all-done = bf16[8,64,192]{2,1,0:T(8,128)(2,1)S(1)} async-done(((bf16[8,64,192]{2,1,0:T(8,128)(2,1)}), bf16[8,64,192]{2,1,0:T(8,128)(2,1)S(1)}, u32[]{:S(2)}, u32[]{:S(2)}) %all-to-all-start) | async-done | bytes 196640 | tf_op jit(solution)/shard_map/all_to_all | solution.py:426
  21.5 0.0 copy-start
  21.5 0.7 %copy-done = bf16[8,64,192]{2,1,0:T(8,128)(2,1)} copy-done((bf16[8,64,192]{2,1,0:T(8,128)(2,1)}, bf16[8,64,192]{2,1,0:T(8,128)(2,1)S(1)}, u32[]{:S(2)}) %copy-start) | copy-done | bytes 196632
  22.1 5.2 %shard_map.29 = bf16[64,128,256]{2,1,0:T(8,128)(2,1)} custom-call(f32[64]{0:T(128)} %taps_ref.1, bf16[512,192]{1,0:T(8,128)(2,1)} %bitcast.7, bf16[3,256,256]{2,1,0:T(8,128)(2,1)} %pad_maximum_fusion.table_ref), custom_call_target="tpu_custom_call" | custom-call | flops 346030080 | bytes 4784128 | tf_op jit(solution)/shard_map/pallas_call | solution.py:357
  (4 shorter events, 0.1 us)
Async XLA Ops:
  0.0 6.7 %collective-permute-start = (bf16[64,512]{1,0:T(8,128)(2,1)}, bf16[64,512]{1,0:T(8,128)(2,1)S(1)}, u32[]{:S(2)}, u32[]{:S(2)}) collective-permute-start(bf16[64,512]{1,0:T(8,128)(2,1)} %bitcast.8), channel_id=1, source_target_pairs={{1,0},{2,1},{3,2},{5,4},{6,5},{7,6},{9,8},{10,9},{11,10},{13,12},{... | collective-permute-start | bytes 196616 | tf_op jit(solution)/shard_map/ppermute | solution.py:422
  7.4 14.1 %all-to-all-start = ((bf16[8,64,192]{2,1,0:T(8,128)(2,1)}), bf16[8,64,192]{2,1,0:T(8,128)(2,1)S(1)}, u32[]{:S(2)}, u32[]{:S(2)}) async-start(bf16[8,64,192]{2,1,0:T(8,128)(2,1)} %maximum_dynamic-update-slice_fusion), calls=%async_computation | async-start | bytes 524288 | tf_op jit(solution)/shard_map/all_to_all | solution.py:426
  21.5 0.7 %copy-start = (bf16[8,64,192]{2,1,0:T(8,128)(2,1)}, bf16[8,64,192]{2,1,0:T(8,128)(2,1)S(1)}, u32[]{:S(2)}) copy-start(bf16[8,64,192]{2,1,0:T(8,128)(2,1)S(1)} %all-to-all-done) | copy-start | bytes 589828

commit v22 on v19

--- a/solution.py
+++ b/solution.py
@@ -309,7 +309,7 @@
         axis=0,
     )
     filtered = filtered.astype(jnp.bfloat16)
-    spectrum = exact_dot([table_ref[p] for p in range(table_ref.shape[0])], filtered)
+    spectrum = exact_dot(split_three(table_ref[...]), filtered)
     real_part = spectrum[:NF]
     imag_part = spectrum[NF:]
     powers = real_part * real_part + imag_part * imag_part
@@ -368,7 +368,7 @@
         cost_estimate=pl.CostEstimate(
             flops=6 * rows * LAGS * NF + 12 * channels * (NF * 320 * length // 256 + NFFT * NFFT),
             transcendentals=2 * NF * channels,
-            bytes_accessed=rows * LAGS * NFFT * 2 + 2 * samples.size + 2 * table_t.size,
+            bytes_accessed=rows * LAGS * NFFT * 2 + 2 * samples.size + 4 * table_t.size,
         ),
     )(filter_taps, samples, table_t)
 
@@ -426,8 +426,7 @@
     gathered = lax.all_to_all(windows, "ta", split_axis=0, concat_axis=0, tiled=True)
     samples = gathered.reshape(extent * slab, width)
     if extent * slab == 2 * NFFT:
-        table_parts = jnp.stack(split_three_kept(fourier_table_t()))
-        return fused_spectra(samples, filter_taps, table_parts, block_rows)[None]
+        return fused_spectra(samples, filter_taps, fourier_table_t(), block_rows)[None]
     filtered = decimate_t(samples.astype(jnp.float32), filter_taps)
     whitened_t = whiten_t(filtered)
     segments, columns, _ = whitened_t.shape

time: 27.4 us -> 27.3 us (level)
    select_n x0 -> x1, other arithmetic: none -> 2.08 us  [fourier_table_t(): jnp.where(real_rows, window_taper * jnp.cos(angles), -window_taper * jnp....]
    convert_element_type x1 -> x0, other arithmetic: 1.47 us -> none  [split_three_kept(): return [part.astype(jnp.bfloat16) for part in (high, middle, low)]]
    another operation x1 -> x0, other arithmetic: 0.79 us -> none  [body(): table_parts = jnp.stack(split_three_kept(fourier_table_t()))]
where the time goes in v22:
time: 27.3 us; the launch traced here: 27 us
  waiting for transfers between devices  8.67 us (32%)
  starting transfers between devices  7.51 us (28%)
  Pallas kernels  6.46 us (24%)
  other arithmetic  2.87 us (11%)
  local copies, waits for them, and re-layouts  1.42 us (5%)
    all_to_all x1, waiting for transfers between devices, body(): lax.all_to_all(windows, 'ta', split_axis=0, concat_axis=0, tiled=True)  6.39 us
    all_to_all x1, starting transfers between devices, body(): lax.all_to_all(windows, 'ta', split_axis=0, concat_axis=0, tiled=True)  5.55 us
    pallas_call x1, Pallas kernels, fused_spectra(): pl.pallas_call(functools.partial(fused_kernel, rows, chunk), out_shape=ja...  4.81 us
    ppermute x1, waiting for transfers between devices, body(): following = lax.ppermute(turned, 'col', route)  2.28 us
    select_n x1, other arithmetic, fourier_table_t(): jnp.where(real_rows, window_taper * jnp.cos(angles), -window_taper * jnp....  2.08 us
    ppermute x1, starting transfers between devices, body(): following = lax.ppermute(turned, 'col', route)  1.96 us
    pallas_call x1, Pallas kernels, channel_windows(): pl.pallas_call(functools.partial(windows_kernel, width, tail_rows), out_s...  1.64 us
    slice x1, local copies, waits for them, and re-layouts, channel_windows(): padded = jnp.concatenate([turned[:, first * step:], tail], axis=1)  0.72 us
  transfers between devices with their start and end apart: 2, of which 2 were waited for; matrix products, arithmetic and copies ran while one was open for 11% of the time, Pallas kernels for 6%

profile of v22, /device:TPU:1, one launch (start us, length us, event | category | flops | bytes accessed | tf_op | source)
XLA Modules:
  0.0 27.0 jit_solution(297186547746786000)
XLA Ops:
  0.0 2.0 %collective-permute-start = (bf16[64,512]{1,0:T(8,128)(2,1)}, bf16[64,512]{1,0:T(8,128)(2,1)S(1)}, u32[]{:S(2)}, u32[]{:S(2)}) collective-permute-start(bf16[64,512]{1,0:T(8,128)(2,1)} %bitcast.8), channel_id=1, source_target_pairs={{1,0},{2,1},{3,2},{5,4},{6,5},{7,6},{9,8},{10,9},{11,10},{13,12},{... | collective-permute-start | bytes 196616 | tf_op jit(solution)/shard_map/ppermute | solution.py:422
  2.0 0.7 %slice.16 = bf16[64,128]{1,0:T(8,128)(2,1)S(1)} slice(bf16[64,512]{1,0:T(8,128)(2,1)} %bitcast.9), slice={[0:64], [384:512]} | slice | bytes 32768 | tf_op jit(solution)/shard_map/slice | solution.py:105
  2.7 1.6 %shard_map.28 = bf16[8,64,192]{2,1,0:T(8,128)(2,1)} custom-call(bf16[64,512]{1,0:T(8,128)(2,1)} %bitcast.10), custom_call_target="tpu_custom_call" | custom-call | bytes 262144 | tf_op jit(solution)/shard_map/pallas_call | solution.py:95
  4.4 2.3 %collective-permute-done = bf16[64,512]{1,0:T(8,128)(2,1)S(1)} collective-permute-done((bf16[64,512]{1,0:T(8,128)(2,1)}, bf16[64,512]{1,0:T(8,128)(2,1)S(1)}, u32[]{:S(2)}, u32[]{:S(2)}) %collective-permute-start) | collective-permute-done | bytes 65568 | tf_op jit(solution)/shard_map/ppermute | solution.py:422
  6.7 0.1 maximum_bitcast_fusion
  6.7 0.6 %maximum_dynamic-update-slice_fusion = bf16[8,64,192]{2,1,0:T(8,128)(2,1)} fusion(bf16[8,64,192]{2,1,0:T(8,128)(2,1)} %shard_map.28, bf16[1,64,192]{2,1,0:T(8,128)(2,1)S(1)} %get-tuple-element.6, bf16[1,64,192]{2,1,0:T(8,128)(2,1)S(1)} %get-tuple-element.5), kind=kLoop, calls=%fused_computation.7 | loop fusion | flops 98304 | bytes 114688 | tf_op jit(solution)/shard_map/dynamic_update_slice | solution.py:107
  7.4 5.6 %all-to-all-start = ((bf16[8,64,192]{2,1,0:T(8,128)(2,1)}), bf16[8,64,192]{2,1,0:T(8,128)(2,1)S(1)}, u32[]{:S(2)}, u32[]{:S(2)}) async-start(bf16[8,64,192]{2,1,0:T(8,128)(2,1)} %maximum_dynamic-update-slice_fusion), calls=%async_computation | async-start | bytes 524288 | tf_op jit(solution)/shard_map/all_to_all | solution.py:426
  13.0 2.1 %multiply_select_fusion.table_ref = f32[256,256]{1,0:T(8,128)} fusion(f32[256]{0:T(256)S(1)} %get-tuple-element.12, s32[256]{0:T(256)S(1)} %get-tuple-element.9, s32[256]{0:T(256)S(1)} %get-tuple-element.10, f32[256]{0:T(256)S(1)} %get-tuple-element.11, pred[256]{0:T(512)(128)(4,1)S(1)} %get-tuple-element.7, pred[256]{0:T(512)(128)(4,1)S(1)} %get-tuple-element.8), kind=kLoop, calls=%fused_computation.6 | loop fusion | flops 1245184 | bytes 266752 | tf_op jit(solution)/shard_map/jit(_where)/select_n | solution.py:62
  15.0 6.4 %all-to-all-done = bf16[8,64,192]{2,1,0:T(8,128)(2,1)S(1)} async-done(((bf16[8,64,192]{2,1,0:T(8,128)(2,1)}), bf16[8,64,192]{2,1,0:T(8,128)(2,1)S(1)}, u32[]{:S(2)}, u32[]{:S(2)}) %all-to-all-start) | async-done | bytes 196640 | tf_op jit(solution)/shard_map/all_to_all | solution.py:426
  21.4 0.0 copy-start
  21.4 0.7 %copy-done = bf16[8,64,192]{2,1,0:T(8,128)(2,1)} copy-done((bf16[8,64,192]{2,1,0:T(8,128)(2,1)}, bf16[8,64,192]{2,1,0:T(8,128)(2,1)S(1)}, u32[]{:S(2)}) %copy-start) | copy-done | bytes 196632
  22.1 4.8 %shard_map.29 = bf16[64,128,256]{2,1,0:T(8,128)(2,1)} custom-call(f32[64]{0:T(128)} %taps_ref.1, bf16[512,192]{1,0:T(8,128)(2,1)} %bitcast.7, f32[256,256]{1,0:T(8,128)} %multiply_select_fusion.table_ref), custom_call_target="tpu_custom_call" | custom-call | flops 346030080 | bytes 4653056 | tf_op jit(solution)/shard_map/pallas_call | solution.py:357
  (4 shorter events, 0.1 us)
Async XLA Ops:
  0.0 6.7 %collective-permute-start = (bf16[64,512]{1,0:T(8,128)(2,1)}, bf16[64,512]{1,0:T(8,128)(2,1)S(1)}, u32[]{:S(2)}, u32[]{:S(2)}) collective-permute-start(bf16[64,512]{1,0:T(8,128)(2,1)} %bitcast.8), channel_id=1, source_target_pairs={{1,0},{2,1},{3,2},{5,4},{6,5},{7,6},{9,8},{10,9},{11,10},{13,12},{... | collective-permute-start | bytes 196616 | tf_op jit(solution)/shard_map/ppermute | solution.py:422
  7.4 14.0 %all-to-all-start = ((bf16[8,64,192]{2,1,0:T(8,128)(2,1)}), bf16[8,64,192]{2,1,0:T(8,128)(2,1)S(1)}, u32[]{:S(2)}, u32[]{:S(2)}) async-start(bf16[8,64,192]{2,1,0:T(8,128)(2,1)} %maximum_dynamic-update-slice_fusion), calls=%async_computation | async-start | bytes 524288 | tf_op jit(solution)/shard_map/all_to_all | solution.py:426
  21.4 0.7 %copy-start = (bf16[8,64,192]{2,1,0:T(8,128)(2,1)}, bf16[8,64,192]{2,1,0:T(8,128)(2,1)S(1)}, u32[]{:S(2)}) copy-start(bf16[8,64,192]{2,1,0:T(8,128)(2,1)S(1)} %all-to-all-done) | copy-start | bytes 589828
